TPU v7x, 1024 devices: a whole 8x8x8 slice. The times are simulated.
1024 devices in a mesh: layer: 4 (over z_hi, core), blk: 256 (over z_lo, y, x).
Axes of the slice: x: 8, y: 8, z: 8 (z_hi: 2, z_lo: 4; z = z_hi * 4 + z_lo), core: 2. Of those that a mesh axis runs over, the one named last changes fastest.
Arguments:
- density: float32 [768, 6, 256, 256], P('blk'), may hold values from -0.15625 to 0.15625
- pattern: int32 [768, 6], replicated, may hold values from 0 to 767, as said below
Outputs:
- squared: float32 [768, 6, 256, 256], P('blk', None, None, 'layer')
- purified: float32 [768, 6, 256, 256], P('blk', None, None, 'layer')
Inputs may be any that keep to these rules, and one draw needn't show every extreme that they name: pattern[i, 0] = i and pattern[i, 1 .. 5] = (i + d) mod 768 for 5 distinct nonzero offsets d in -3 .. 3.
All inputs are finite; a program needn't handle non-finite values.
Results may differ from a plain program's by a relative error of at most 0.0016.
Values may be sent and summed in bfloat16 or wider, within the bound.
No kernel may reach another device: no remote copies, remote signals or barrier semaphores. Data moves between devices by JAX's collectives and lax.ppermute only.
A program may use at most 64 MiB of HBM per device.

v0:
```python
import jax
import jax.numpy as jnp
from jax import lax
from jax.sharding import PartitionSpec as P

BAND = 3


def padded_2(value, sides, width):
    for axis, dim in sides:
        size, length = (lax.axis_size(axis), value.shape[dim])
        up = [(i, (i + 1) % size) for i in range(size)]
        down = [(j, i) for i, j in up]
        last = lax.slice_in_dim(value, length - width, length, axis=dim)
        initial = lax.slice_in_dim(value, 0, width, axis=dim)
        before = lax.ppermute(last, axis, up)
        after = lax.ppermute(initial, axis, down)
        value = jnp.concatenate([before, value, after], axis=dim)
    return value


def body(density, pattern):
    count_rows, slots, order, _ = density.shape
    width = order // lax.axis_size("layer")
    start_col = lax.axis_index("layer") * width
    total_rows = pattern.shape[0]
    first = lax.axis_index("blk") * count_rows
    own = lax.dynamic_slice_in_dim(pattern, first, count_rows, 0)
    neighbor = pattern[own]
    equal = neighbor[:, :, None, :] == own[:, None, :, None]
    slot = jnp.argmax(equal.astype(jnp.int32), axis=3)
    valid = jnp.any(equal, axis=3).astype(jnp.float32)
    row_ids = first + jnp.arange(count_rows, dtype=jnp.int32)
    offset = (own - row_ids[:, None] + BAND) % total_rows - BAND
    place = jnp.arange(count_rows, dtype=jnp.int32)[:, None] + BAND + offset
    col_part = lax.dynamic_slice_in_dim(density, start_col, width, 3)
    padded = padded_2(col_part, (("blk", 0),), BAND)
    highest = lax.Precision.HIGHEST
    picked = padded[place[:, :, None], slot] * valid[:, :, :, None, None]

    def product(left):
        return jnp.einsum("rsac,rstcb->rtab", left, picked, precision=highest)

    squared = product(density)
    rounded = squared.astype(jnp.bfloat16)
    cubed = product(lax.all_gather(rounded, "layer", axis=3, tiled=True).astype(jnp.float32))
    return (squared, 3.0 * squared - 2.0 * cubed)


def solution(mesh):
    return jax.shard_map(
        body,
        mesh=mesh,
        in_specs=(P("blk", None, None, None), P()),
        out_specs=(P("blk", None, None, "layer"), P("blk", None, None, "layer")),
        check_vma=False,
    )
```

profile of v0, /device:TPU:1, one launch (start us, length us, event | category | flops | bytes accessed | tf_op | source)
XLA Modules:
  0.0 148.4 jit_solution(4043542013749249308)
XLA Ops:
  7.2 0.0 all-gather.2.cloned.1.call-start
  7.2 2.3 %constant_dynamic-slice_fusion.1 = f32[3,6,256,64]{3,2,1,0:T(8,128)S(1)} fusion(f32[3,6,256,256]{3,2,1,0:T(8,128)} %param.2, s32[]{:T(128)S(6)} %select_n.27), kind=kLoop, calls=%fused_computation.35 | loop fusion | bytes 2359300 | tf_op jit(solution)/shard_map/dynamic_slice | solution.py:36
  9.6 0.9 copy.40
  10.5 0.0 copy-start
  10.5 17.2 %collective-permute-start.1 = (f32[3,6,256,64]{2,3,1,0:T(8,128)S(1)}, f32[3,6,256,64]{2,3,1,0:T(8,128)}, u32[]{:S(2)}, u32[]{:S(2)}) collective-permute-start(f32[3,6,256,64]{2,3,1,0:T(8,128)S(1)} %copy.40), channel_id=1, source_target_pairs={{1,0},{2,1},{3,2},{4,3},{5,4},{6,5},{7,6},{8,7},{9,8},{10,9},{11,1... | collective-permute-start | bytes 3538952 | tf_op jit(solution)/shard_map/ppermute | solution.py:17
  27.7 1.9 %collective-permute-start = (f32[3,6,256,64]{2,3,1,0:T(8,128)S(1)}, f32[3,6,256,64]{2,3,1,0:T(8,128)}, u32[]{:S(2)}, u32[]{:S(2)}) collective-permute-start(f32[3,6,256,64]{2,3,1,0:T(8,128)S(1)} %copy.40), channel_id=1, source_target_pairs={{0,1},{1,2},{2,3},{3,4},{4,5},{5,6},{6,7},{7,8},{8,9},{9,10},{10,1... | collective-permute-start | bytes 3538952 | tf_op jit(solution)/shard_map/ppermute | solution.py:16
  29.6 0.9 copy.29
  30.5 0.8 fusion.28
  31.3 0.1 copy.27
  31.4 0.1 copy.32
  31.5 0.1 copy.28
  31.6 0.1 reshape.25
  31.7 0.6 gather_fusion
  32.3 0.5 compare_reduce_fusion
  32.8 0.1 copy.33
  32.9 1.3 fusion.20
  34.2 0.1 fusion.24
  34.3 0.1 reshape.31
  34.4 17.9 %collective-permute-done.1 = f32[3,6,256,64]{2,3,1,0:T(8,128)} collective-permute-done((f32[3,6,256,64]{2,3,1,0:T(8,128)S(1)}, f32[3,6,256,64]{2,3,1,0:T(8,128)}, u32[]{:S(2)}, u32[]{:S(2)}) %collective-permute-start.1) | collective-permute-done | bytes 1179680 | tf_op jit(solution)/shard_map/ppermute | solution.py:17
  52.3 0.0 copy-done
  52.3 10.0 %collective-permute-done = f32[3,6,256,64]{2,3,1,0:T(8,128)} collective-permute-done((f32[3,6,256,64]{2,3,1,0:T(8,128)S(1)}, f32[3,6,256,64]{2,3,1,0:T(8,128)}, u32[]{:S(2)}, u32[]{:S(2)}) %collective-permute-start) | collective-permute-done | bytes 1179680 | tf_op jit(solution)/shard_map/ppermute | solution.py:16
  62.3 2.2 %pad_maximum_fusion = f32[9,6,256,64]{2,3,1,0:T(8,128)S(1)} fusion(f32[3,6,256,64]{2,3,1,0:T(8,128)} %collective-permute-done.1, f32[3,6,256,64]{2,3,1,0:T(8,128)} %copy-done, f32[3,6,256,64]{2,3,1,0:T(8,128)} %collective-permute-done), kind=kLoop, calls=%fused_computation.6 | loop fusion | flops 1769472 | bytes 7077888 | tf_op jit(solution)/shard_map/concatenate | solution.py:18
  64.5 4.5 %gather_fusion.1 = f32[108,256,64]{1,2,0:T(8,128)} fusion(f32[9,6,256,64]{2,3,1,0:T(8,128)S(1)} %pad_maximum_fusion, s32[108]{0:T(128)S(1)} %reshape.31), kind=kCustom, calls=%fused_computation.1 | custom fusion | bytes 14156640 | tf_op jit(solution)/shard_map/gather | solution.py:39
  68.9 14.9 %fusion.29 = (bf16[3,6,256,64]{2,3,1,0:T(8,128)(2,1)}, f32[3,6,256,64]{2,3,1,0:T(8,128)S(1)}) fusion(f32[3,6,256,256]{3,2,1,0:T(8,128)} %param.2, f32[3,6,6,256,64]{3,4,2,1,0:T(8,128)} %bitcast.47, f32[3,6,6]{1,2,0:T(8,128)S(1)} %copy.33), kind=kOutput, calls=%fused_computation.36 | convolution fusion | flops 5437882368 | bytes 13566384 | tf_op jit(solution)/shard_map/rsac,rstcb->rtab/dot_general | solution.py:42
  83.8 0.0 copy-start.1
  83.8 0.0 all-gather.2.cloned.1.call-update
  83.8 49.5 %all-gather.2.cloned.1.call-done = bf16[3,6,256,256]{2,3,1,0:T(8,128)(2,1)} async-done(((bf16[3,6,256,64]{2,3,1,0:T(8,128)(2,1)}), bf16[3,6,256,256]{2,3,1,0:T(8,128)(2,1)}) %all-gather.2.cloned.1.call-update) | async-done | bytes 2359312 | tf_op jit(solution)/shard_map/all_gather | solution.py:46
  133.3 8.2 %multiply_subtract_fusion = f32[3,6,256,64]{2,3,1,0:T(8,128)} fusion(f32[3,6,256,64]{2,3,1,0:T(8,128)S(1)} %get-tuple-element.7, bf16[3,6,256,256]{2,3,1,0:T(8,128)(2,1)} %all-gather.2.cloned.1.call-done, f32[3,6,6,256,64]{3,4,2,1,0:T(8,128)} %bitcast.48, f32[3,6,6]{1,2,0:T(8,128)S(1)} %copy.33), kind=kOutput, calls=%fused_computation.14 | convolution fusion | flops 5438472192 | bytes 11796912 | tf_op jit(solution)/shard_map/rsac,rstcb->rtab/dot_general | solution.py:42
  141.5 0.0 copy-done.1
  (5 shorter events, 0.0 us)
Async XLA Ops:
  7.2 126.2 %all-gather.2.cloned.1.call-start = ((), (), s32[]{:S(2)}) async-start(), calls=%async_computation | async-start | bytes 2949120 | tf_op jit(solution)/shard_map/all_gather | solution.py:46
  10.5 41.8 %copy-start = (f32[3,6,256,64]{2,3,1,0:T(8,128)}, f32[3,6,256,64]{2,3,1,0:T(8,128)S(1)}, u32[]{:S(2)}) copy-start(f32[3,6,256,64]{2,3,1,0:T(8,128)S(1)} %copy.40) | copy-start | bytes 3538948
  10.5 41.8 %collective-permute-start.1 = (f32[3,6,256,64]{2,3,1,0:T(8,128)S(1)}, f32[3,6,256,64]{2,3,1,0:T(8,128)}, u32[]{:S(2)}, u32[]{:S(2)}) collective-permute-start(f32[3,6,256,64]{2,3,1,0:T(8,128)S(1)} %copy.40), channel_id=1, source_target_pairs={{1,0},{2,1},{3,2},{4,3},{5,4},{6,5},{7,6},{8,7},{9,8},{10,9},{11,1... | collective-permute-start | bytes 3538952 | tf_op jit(solution)/shard_map/ppermute | solution.py:17
  27.7 34.6 %collective-permute-start = (f32[3,6,256,64]{2,3,1,0:T(8,128)S(1)}, f32[3,6,256,64]{2,3,1,0:T(8,128)}, u32[]{:S(2)}, u32[]{:S(2)}) collective-permute-start(f32[3,6,256,64]{2,3,1,0:T(8,128)S(1)} %copy.40), channel_id=1, source_target_pairs={{0,1},{1,2},{2,3},{3,4},{4,5},{5,6},{6,7},{7,8},{8,9},{9,10},{10,1... | collective-permute-start | bytes 3538952 | tf_op jit(solution)/shard_map/ppermute | solution.py:16
  83.8 57.7 %copy-start.1 = (f32[3,6,256,64]{2,3,1,0:T(8,128)}, f32[3,6,256,64]{2,3,1,0:T(8,128)S(1)}, u32[]{:S(2)}) copy-start(f32[3,6,256,64]{2,3,1,0:T(8,128)S(1)} %get-tuple-element.7) | copy-start | bytes 3538948
Sparse Core Ops, SparseCore 0:
  84.0 49.3 all-gather.1
where the time goes:
time: 149 us; the launch traced here: 148 us
  waiting for transfers between devices  77.4 us (52%)
  matrix products  23.1 us (16%)
  starting transfers between devices  19.1 us (13%)
  between operations  14.1 us (9%)
  local copies, waits for them, and re-layouts  9.78 us (7%)
  other arithmetic  4.9 us (3%)
    all_gather x1, waiting for transfers between devices, body(): lax.all_gather(rounded, 'layer', axis=3, tiled=True).astype(jnp.float32)  49.5 us
    dot_general x2, matrix products, product(): return jnp.einsum('rsac,rstcb->rtab', left, picked, precision=highest)  23.1 us
    ppermute x1, waiting for transfers between devices, padded_2(): after = lax.ppermute(initial, axis, down)  17.9 us
    ppermute x1, starting transfers between devices, padded_2(): after = lax.ppermute(initial, axis, down)  17.2 us
    ppermute x1, waiting for transfers between devices, padded_2(): before = lax.ppermute(last, axis, up)  9.96 us
    gather x1, local copies, waits for them, and re-layouts, body(): picked = padded[place[:, :, None], slot] * valid[:, :, :, None, None]  4.48 us
  transfers between devices with their start and end apart: 3, of which 3 were waited for; matrix products, arithmetic and copies ran while one was open for 3% of the time, Pallas kernels for 0%

commit v1 on v0

v1 whole, which is shorter than its diff:
```python
import jax
import jax.numpy as jnp
from jax import lax
from jax.sharding import PartitionSpec as P

BAND = 3


def padded_2(value, sides, width):
    for axis, dim in sides:
        size, length = (lax.axis_size(axis), value.shape[dim])
        up = [(i, (i + 1) % size) for i in range(size)]
        down = [(j, i) for i, j in up]
        last = lax.slice_in_dim(value, length - width, length, axis=dim)
        initial = lax.slice_in_dim(value, 0, width, axis=dim)
        before = lax.ppermute(last, axis, up)
        after = lax.ppermute(initial, axis, down)
        value = jnp.concatenate([before, value, after], axis=dim)
    return value


def relay_pairs(mesh):
    devices = mesh.devices
    n_layer, n_blk = devices.shape
    try:
        where = {}
        for li in range(n_layer):
            for bi in range(n_blk):
                d = devices[li, bi]
                where[(tuple(d.coords), d.core_on_chip)] = (li, bi)
        depth = 1 + max(c[2] for c, _ in where)
        pairs = []
        for (coords, core), (li, bi) in where.items():
            x, y, z = coords
            step = 2 if core == 0 else -2
            one = where[((x, y, (z + step) % depth), core)]
            two = where[((x, y, (z + 2 * step) % depth), core)]
            if two != (li ^ 2, bi):
                return None
            pairs.append((li * n_blk + bi, one[0] * n_blk + one[1]))
        return sorted(pairs)
    except (AttributeError, KeyError, TypeError, IndexError):
        return None


def make_body(relay):
    def body(density, pattern):
        count_rows, slots, order, _ = density.shape
        n_layer = lax.axis_size("layer")
        width = order // n_layer
        me = lax.axis_index("layer")
        start_col = me * width
        total_rows = pattern.shape[0]
        first = lax.axis_index("blk") * count_rows
        own = lax.dynamic_slice_in_dim(pattern, first, count_rows, 0)
        neighbor = pattern[own]
        equal = neighbor[:, :, None, :] == own[:, None, :, None]
        slot = jnp.argmax(equal.astype(jnp.int32), axis=3)
        valid = jnp.any(equal, axis=3).astype(jnp.float32)
        row_ids = first + jnp.arange(count_rows, dtype=jnp.int32)
        offset = (own - row_ids[:, None] + BAND) % total_rows - BAND
        place = jnp.arange(count_rows, dtype=jnp.int32)[:, None] + BAND + offset
        col_part = lax.dynamic_slice_in_dim(density, start_col, width, 3)
        padded = padded_2(col_part, (("blk", 0),), BAND)
        highest = lax.Precision.HIGHEST
        picked = padded[place[:, :, None], slot] * valid[:, :, :, None, None]

        def product(left):
            return jnp.einsum("rsac,rstcb->rtab", left, picked, precision=highest)

        squared = product(density)
        rounded = squared.astype(jnp.bfloat16)
        across = [(i, i ^ 1) for i in range(n_layer)]
        mate = lax.ppermute(rounded, "layer", across)
        if relay is None:
            far = lax.ppermute(rounded, "layer", [(i, i ^ 2) for i in range(n_layer)])
        else:
            halfway = lax.ppermute(rounded, ("layer", "blk"), relay)
            far = lax.ppermute(halfway, ("layer", "blk"), relay)
        far_mate = lax.ppermute(far, "layer", across)
        pieces = jnp.stack([rounded, mate, far, far_mate])
        quarters = jnp.take(pieces, jnp.bitwise_xor(jnp.arange(4, dtype=jnp.int32), me), axis=0)
        gathered = jnp.moveaxis(quarters, 0, 3).reshape(count_rows, slots, order, order)
        cubed = product(gathered.astype(jnp.float32))
        return (squared, 3.0 * squared - 2.0 * cubed)

    return body


def solution(mesh):
    relay = relay_pairs(mesh) if mesh.shape["layer"] == 4 else None
    return jax.shard_map(
        make_body(relay),
        mesh=mesh,
        in_specs=(P("blk", None, None, None), P()),
        out_specs=(P("blk", None, None, "layer"), P("blk", None, None, "layer")),
        check_vma=False,
    )
```

time: 149 us -> 135 us (0.906)
  waiting for transfers between devices: 77.4 us -> 50.1 us
  starting transfers between devices: 19.1 us -> 38.8 us
  between operations: 14.1 us -> 0.81 us
  local copies, waits for them, and re-layouts: 9.78 us -> 16.1 us
  other arithmetic: 4.9 us -> 8.79 us
  matrix products: 23.1 us -> 19.8 us
    all_gather x1 -> x0, waiting for transfers between devices: 49.5 us -> none  [body(): lax.all_gather(rounded, 'layer', axis=3, tiled=True).astype(jnp.float32)]
    ppermute x0 -> x4, waiting for transfers between devices: none -> 23.2 us  [the longest x1 13.1 us: body(): halfway = lax.ppermute(rounded, ('layer', 'blk'), relay)]
    ppermute x0 -> x4, starting transfers between devices: none -> 19.7 us  [the longest x1 6.95 us: body(): far = lax.ppermute(halfway, ('layer', 'blk'), relay)]
    gather x0 -> x1, local copies, waits for them, and re-layouts: none -> 3.91 us  [body(): jnp.take(pieces, jnp.bitwise_xor(jnp.arange(4, dtype=jnp.int32), me), axi...]
    dot_general x2, matrix products: 23.1 us -> 19.8 us  [product(): return jnp.einsum('rsac,rstcb->rtab', left, picked, precision=highest)]
    unnamed x6 -> x12, local copies, waits for them, and re-layouts: 1.83 us -> 4.01 us
    select_n x0 -> x2, other arithmetic: none -> 2.11 us  [body(): jnp.take(pieces, jnp.bitwise_xor(jnp.arange(4, dtype=jnp.int32), me), axi...]
    another operation x0 -> x1, other arithmetic: none -> 1.76 us  [body(): pieces = jnp.stack([rounded, mate, far, far_mate])]
  transfers between devices with their start and end apart: 3 -> 6, of which waited for: 3 -> 5; matrix products, arithmetic and copies ran while one was open for 3% -> 4% of each run, Pallas kernels for 0% -> 0%
where the time goes in v1:
time: 135 us; the launch traced here: 134 us
  waiting for transfers between devices  50.1 us (37%)
  starting transfers between devices  38.8 us (29%)
  matrix products  19.8 us (15%)
  local copies, waits for them, and re-layouts  16.1 us (12%)
  other arithmetic  8.79 us (7%)
    dot_general x2, matrix products, product(): return jnp.einsum('rsac,rstcb->rtab', left, picked, precision=highest)  19.8 us
    ppermute x1, waiting for transfers between devices, padded_2(): after = lax.ppermute(initial, axis, down)  17.9 us
    ppermute x1, starting transfers between devices, padded_2(): after = lax.ppermute(initial, axis, down)  17.2 us
    ppermute x1, waiting for transfers between devices, body(): halfway = lax.ppermute(rounded, ('layer', 'blk'), relay)  13.1 us
    ppermute x1, waiting for transfers between devices, padded_2(): before = lax.ppermute(last, axis, up)  8.94 us
    ppermute x1, waiting for transfers between devices, body(): far = lax.ppermute(halfway, ('layer', 'blk'), relay)  8.71 us
    ppermute x1, starting transfers between devices, body(): far = lax.ppermute(halfway, ('layer', 'blk'), relay)  6.95 us
    ppermute x1, starting transfers between devices, body(): far_mate = lax.ppermute(far, 'layer', across)  5.59 us
  transfers between devices with their start and end apart: 6, of which 5 were waited for; matrix products, arithmetic and copies ran while one was open for 4% of the time, Pallas kernels for 0%

profile of v1, /device:TPU:1, one launch (start us, length us, event | category | flops | bytes accessed | tf_op | source)
XLA Modules:
  0.0 134.4 jit_solution(12398743937815917312)
XLA Ops:
  0.6 2.3 %constant_dynamic-slice_fusion.1 = f32[3,6,256,64]{3,2,1,0:T(8,128)S(1)} fusion(f32[3,6,256,256]{3,2,1,0:T(8,128)} %param.2, s32[]{:T(128)S(6)} %select_n.51), kind=kLoop, calls=%fused_computation.42 | loop fusion | bytes 2359300 | tf_op jit(solution)/shard_map/dynamic_slice | solution.py:63
  3.0 0.9 copy.48
  3.9 17.2 %collective-permute-start.1 = (f32[3,6,256,64]{2,3,1,0:T(8,128)S(1)}, f32[3,6,256,64]{2,3,1,0:T(8,128)S(1)}, u32[]{:S(2)}, u32[]{:S(2)}) collective-permute-start(f32[3,6,256,64]{2,3,1,0:T(8,128)S(1)} %copy.48), channel_id=1, source_target_pairs={{1,0},{2,1},{3,2},{4,3},{5,4},{6,5},{7,6},{8,7},{9,8},{10,9},{11,1... | collective-permute-start | bytes 3538952 | tf_op jit(solution)/shard_map/ppermute | solution.py:17
  21.1 1.9 %collective-permute-start = (f32[3,6,256,64]{2,3,1,0:T(8,128)S(1)}, f32[3,6,256,64]{2,3,1,0:T(8,128)}, u32[]{:S(2)}, u32[]{:S(2)}) collective-permute-start(f32[3,6,256,64]{2,3,1,0:T(8,128)S(1)} %copy.48), channel_id=1, source_target_pairs={{0,1},{1,2},{2,3},{3,4},{4,5},{5,6},{6,7},{7,8},{8,9},{9,10},{10,1... | collective-permute-start | bytes 3538952 | tf_op jit(solution)/shard_map/ppermute | solution.py:16
  23.0 0.9 copy.33
  24.0 0.8 fusion.19
  24.7 0.1 copy.31
  24.9 0.1 copy.32
  25.1 0.6 gather_fusion
  25.7 0.5 compare_reduce_fusion
  26.2 0.1 copy.37
  26.3 1.3 %fusion.11 = (s32[3,6,6]{2,1,0:T(8,128)}, s32[3,6,6]{2,1,0:T(8,128)S(1)}) fusion(s32[3,6]{1,0:T(4,128)S(1)} %copy.36, s32[3,6,6]{2,1,0:T(8,128)S(1)} %reshape.81), kind=kLoop, calls=%fused_computation.19 | loop fusion | flops 5076 | bytes 1368 | tf_op jit(solution)/shard_map/make_body.<locals>.body/reduce | solution.py:58
  27.8 17.9 %collective-permute-done.1 = f32[3,6,256,64]{2,3,1,0:T(8,128)S(1)} collective-permute-done((f32[3,6,256,64]{2,3,1,0:T(8,128)S(1)}, f32[3,6,256,64]{2,3,1,0:T(8,128)S(1)}, u32[]{:S(2)}, u32[]{:S(2)}) %collective-permute-start.1) | collective-permute-done | bytes 1179680 | tf_op jit(solution)/shard_map/ppermute | solution.py:17
  45.7 1.0 copy-done.2
  46.7 8.9 %collective-permute-done = f32[3,6,256,64]{2,3,1,0:T(8,128)} collective-permute-done((f32[3,6,256,64]{2,3,1,0:T(8,128)S(1)}, f32[3,6,256,64]{2,3,1,0:T(8,128)}, u32[]{:S(2)}, u32[]{:S(2)}) %collective-permute-start) | collective-permute-done | bytes 1179680 | tf_op jit(solution)/shard_map/ppermute | solution.py:16
  55.7 2.2 %pad_maximum_fusion = f32[9,6,256,64]{2,3,1,0:T(8,128)S(1)} fusion(f32[3,6,256,64]{2,3,1,0:T(8,128)} %copy-done.2, f32[3,6,256,64]{2,3,1,0:T(8,128)} %copy-done, f32[3,6,256,64]{2,3,1,0:T(8,128)} %collective-permute-done), kind=kLoop, calls=%fused_computation.7 | loop fusion | flops 1769472 | bytes 7077888 | tf_op jit(solution)/shard_map/concatenate | solution.py:18
  57.9 4.5 %gather_fusion.1 = f32[108,256,64]{1,2,0:T(8,128)} fusion(f32[9,6,256,64]{2,3,1,0:T(8,128)S(1)} %pad_maximum_fusion, s32[108]{0:T(128)S(1)} %reshape.56), kind=kCustom, calls=%fused_computation.1 | custom fusion | bytes 14156640 | tf_op jit(solution)/shard_map/gather | solution.py:66
  62.4 14.9 %fusion.21 = (bf16[3,6,256,64]{2,3,1,0:T(8,128)(2,1)S(1)}, f32[3,6,256,64]{2,3,1,0:T(8,128)}) fusion(f32[3,6,256,256]{3,2,1,0:T(8,128)} %param.2, f32[3,6,6,256,64]{3,4,2,1,0:T(8,128)} %bitcast.48, f32[3,6,6]{1,2,0:T(8,128)S(1)} %copy.37), kind=kOutput, calls=%fused_computation.43 | convolution fusion | flops 5437882368 | bytes 13566384 | tf_op jit(solution)/shard_map/rsac,rstcb->rtab/dot_general | solution.py:69
  77.3 5.2 %collective-permute-start.3 = (bf16[3,6,256,64]{2,3,1,0:T(8,128)(2,1)S(1)}, bf16[3,6,256,64]{2,3,1,0:T(8,128)(2,1)S(1)}, u32[]{:S(2)}, u32[]{:S(2)}) collective-permute-start(bf16[3,6,256,64]{2,3,1,0:T(8,128)(2,1)S(1)} %get-tuple-element.6), channel_id=1, source_target_pairs={{0,128},{1,129},{2,130},{3,131},{4,132},{5,133},{6,134},{7,135},{8... | collective-permute-start | bytes 1769480 | tf_op jit(solution)/shard_map/ppermute | solution.py:78
  82.6 13.1 %collective-permute-done.3 = bf16[3,6,256,64]{2,3,1,0:T(8,128)(2,1)S(1)} collective-permute-done((bf16[3,6,256,64]{2,3,1,0:T(8,128)(2,1)S(1)}, bf16[3,6,256,64]{2,3,1,0:T(8,128)(2,1)S(1)}, u32[]{:S(2)}, u32[]{:S(2)}) %collective-permute-start.3) | collective-permute-done | bytes 589856 | tf_op jit(solution)/shard_map/ppermute | solution.py:78
  95.7 7.0 %collective-permute-start.4 = (bf16[3,6,256,64]{2,3,1,0:T(8,128)(2,1)S(1)}, bf16[3,6,256,64]{2,3,1,0:T(8,128)(2,1)S(1)}, u32[]{:S(2)}, u32[]{:S(2)}) collective-permute-start(bf16[3,6,256,64]{2,3,1,0:T(8,128)(2,1)S(1)} %collective-permute-done.3), channel_id=1, source_target_pairs={{0,128},{1,129},{2,130},{3,131},{4,132},{5,133},{6,134},{7,135},{8... | collective-permute-start | bytes 1769480 | tf_op jit(solution)/shard_map/ppermute | solution.py:79
  102.6 1.9 %collective-permute-start.2 = (bf16[3,6,256,64]{2,3,1,0:T(8,128)(2,1)S(1)}, bf16[3,6,256,64]{2,3,1,0:T(8,128)(2,1)S(1)}, u32[]{:S(2)}, u32[]{:S(2)}) collective-permute-start(bf16[3,6,256,64]{2,3,1,0:T(8,128)(2,1)S(1)} %get-tuple-element.6), channel_id=1, source_target_pairs={{0,256},{256,0},{512,768},{768,512},{1,257},{257,1},{513,769},{769... | collective-permute-start | bytes 1769480 | tf_op jit(solution)/shard_map/ppermute | solution.py:74
  104.6 8.7 %collective-permute-done.4 = bf16[3,6,256,64]{2,3,1,0:T(8,128)(2,1)S(1)} collective-permute-done((bf16[3,6,256,64]{2,3,1,0:T(8,128)(2,1)S(1)}, bf16[3,6,256,64]{2,3,1,0:T(8,128)(2,1)S(1)}, u32[]{:S(2)}, u32[]{:S(2)}) %collective-permute-start.4) | collective-permute-done | bytes 589856 | tf_op jit(solution)/shard_map/ppermute | solution.py:79
  113.3 5.6 %collective-permute-start.5 = (bf16[3,6,256,64]{2,3,1,0:T(8,128)(2,1)S(1)}, bf16[3,6,256,64]{2,3,1,0:T(8,128)(2,1)S(1)}, u32[]{:S(2)}, u32[]{:S(2)}) collective-permute-start(bf16[3,6,256,64]{2,3,1,0:T(8,128)(2,1)S(1)} %collective-permute-done.4), channel_id=1, source_target_pairs={{0,256},{256,0},{512,768},{768,512},{1,257},{257,1},{513,769},{769... | collective-permute-start | bytes 1769480 | tf_op jit(solution)/shard_map/ppermute | solution.py:80
  118.9 1.4 %collective-permute-done.5 = bf16[3,6,256,64]{2,3,1,0:T(8,128)(2,1)S(1)} collective-permute-done((bf16[3,6,256,64]{2,3,1,0:T(8,128)(2,1)S(1)}, bf16[3,6,256,64]{2,3,1,0:T(8,128)(2,1)S(1)}, u32[]{:S(2)}, u32[]{:S(2)}) %collective-permute-start.5) | collective-permute-done | bytes 589856 | tf_op jit(solution)/shard_map/ppermute | solution.py:80
  120.3 1.8 %pad_maximum_fusion.1 = bf16[4,3,6,256,64]{3,4,2,1,0:T(8,128)(2,1)} fusion(bf16[1,3,6,256,64]{3,4,2,1,0:T(8,128)(2,1)S(1)} %bitcast.56, bf16[1,3,6,256,64]{3,4,2,1,0:T(8,128)(2,1)S(1)} %bitcast.54, bf16[1,3,6,256,64]{3,4,2,1,0:T(8,128)(2,1)S(1)} %bitcast.55, bf16[1,3,6,256,64]{3,4,2,1,0:T(8,128)(2,1)S(1)} %bitcast.53), kind=kLoop, calls=%fused_computation.10 | loop fusion | flops 3538944 | bytes 4718592 | tf_op jit(solution)/shard_map/stack | solution.py:81
  122.1 3.9 %gather_fusion.2 = bf16[4,3,6,256,64]{3,4,2,1,0:T(8,128)(2,1)} fusion(bf16[4,3,6,256,64]{3,4,2,1,0:T(8,128)(2,1)} %pad_maximum_fusion.1, s32[1024]{0:T(1024)S(1)} %pad_clamp_fusion), kind=kCustom, calls=%fused_computation.2 | custom fusion | bytes 4718608 | tf_op jit(solution)/shard_map/jit(_take)/gather | solution.py:82
  126.0 2.1 %select_bitcast_fusion = bf16[3,6,256,4,64]{2,4,1,0,3:T(8,128)(2,1)S(1)} fusion(bf16[4,3,6,256,64]{3,4,2,1,0:T(8,128)(2,1)} %gather_fusion.2, pred[4]{0:T(512)(128)(4,1)S(1)} %compare_and_fusion), kind=kLoop, calls=%fused_computation.11 | loop fusion | flops 1179648 | bytes 4718596 | tf_op jit(solution)/shard_map/jit(_take)/select_n | solution.py:82
  128.1 0.3 copy.39
  128.4 0.5 slice-done.1
  128.9 0.7 copy-done.1
  129.6 4.8 %multiply_subtract_fusion = f32[3,6,256,64]{2,3,1,0:T(8,128)} fusion(f32[3,6,256,64]{2,3,1,0:T(8,128)S(1)} %copy-done.1, bf16[3,6,256,256,1]{2,3,1,4,0:T(8,128)(2,1)S(1)} %bitcast.52, f32[3,6,6,256,64]{3,4,2,1,0:T(8,128)S(1)} %bitcast.51, f32[3,6,6]{1,2,0:T(8,128)S(1)} %copy.37), kind=kOutput, calls=%fused_computation.16 | convolution fusion | flops 5438472192 | bytes 11796912 | tf_op jit(solution)/shard_map/rsac,rstcb->rtab/dot_general | solution.py:69
  (21 shorter events, 0.4 us)
Async XLA Ops:
  3.9 41.8 %copy-start = (f32[3,6,256,64]{2,3,1,0:T(8,128)}, f32[3,6,256,64]{2,3,1,0:T(8,128)S(1)}, u32[]{:S(2)}) copy-start(f32[3,6,256,64]{2,3,1,0:T(8,128)S(1)} %copy.48) | copy-start | bytes 3538948
  3.9 41.8 %collective-permute-start.1 = (f32[3,6,256,64]{2,3,1,0:T(8,128)S(1)}, f32[3,6,256,64]{2,3,1,0:T(8,128)S(1)}, u32[]{:S(2)}, u32[]{:S(2)}) collective-permute-start(f32[3,6,256,64]{2,3,1,0:T(8,128)S(1)} %copy.48), channel_id=1, source_target_pairs={{1,0},{2,1},{3,2},{4,3},{5,4},{6,5},{7,6},{8,7},{9,8},{10,9},{11,1... | collective-permute-start | bytes 3538952 | tf_op jit(solution)/shard_map/ppermute | solution.py:17
  21.1 34.6 %collective-permute-start = (f32[3,6,256,64]{2,3,1,0:T(8,128)S(1)}, f32[3,6,256,64]{2,3,1,0:T(8,128)}, u32[]{:S(2)}, u32[]{:S(2)}) collective-permute-start(f32[3,6,256,64]{2,3,1,0:T(8,128)S(1)} %copy.48), channel_id=1, source_target_pairs={{0,1},{1,2},{2,3},{3,4},{4,5},{5,6},{6,7},{7,8},{8,9},{9,10},{10,1... | collective-permute-start | bytes 3538952 | tf_op jit(solution)/shard_map/ppermute | solution.py:16
  45.7 1.0 copy-start.2
  77.3 18.4 %collective-permute-start.3 = (bf16[3,6,256,64]{2,3,1,0:T(8,128)(2,1)S(1)}, bf16[3,6,256,64]{2,3,1,0:T(8,128)(2,1)S(1)}, u32[]{:S(2)}, u32[]{:S(2)}) collective-permute-start(bf16[3,6,256,64]{2,3,1,0:T(8,128)(2,1)S(1)} %get-tuple-element.6), channel_id=1, source_target_pairs={{0,128},{1,129},{2,130},{3,131},{4,132},{5,133},{6,134},{7,135},{8... | collective-permute-start | bytes 1769480 | tf_op jit(solution)/shard_map/ppermute | solution.py:78
  95.7 17.6 %collective-permute-start.4 = (bf16[3,6,256,64]{2,3,1,0:T(8,128)(2,1)S(1)}, bf16[3,6,256,64]{2,3,1,0:T(8,128)(2,1)S(1)}, u32[]{:S(2)}, u32[]{:S(2)}) collective-permute-start(bf16[3,6,256,64]{2,3,1,0:T(8,128)(2,1)S(1)} %collective-permute-done.3), channel_id=1, source_target_pairs={{0,128},{1,129},{2,130},{3,131},{4,132},{5,133},{6,134},{7,135},{8... | collective-permute-start | bytes 1769480 | tf_op jit(solution)/shard_map/ppermute | solution.py:79
  102.6 16.3 %collective-permute-start.2 = (bf16[3,6,256,64]{2,3,1,0:T(8,128)(2,1)S(1)}, bf16[3,6,256,64]{2,3,1,0:T(8,128)(2,1)S(1)}, u32[]{:S(2)}, u32[]{:S(2)}) collective-permute-start(bf16[3,6,256,64]{2,3,1,0:T(8,128)(2,1)S(1)} %get-tuple-element.6), channel_id=1, source_target_pairs={{0,256},{256,0},{512,768},{768,512},{1,257},{257,1},{513,769},{769... | collective-permute-start | bytes 1769480 | tf_op jit(solution)/shard_map/ppermute | solution.py:74
  113.3 7.0 %collective-permute-start.5 = (bf16[3,6,256,64]{2,3,1,0:T(8,128)(2,1)S(1)}, bf16[3,6,256,64]{2,3,1,0:T(8,128)(2,1)S(1)}, u32[]{:S(2)}, u32[]{:S(2)}) collective-permute-start(bf16[3,6,256,64]{2,3,1,0:T(8,128)(2,1)S(1)} %collective-permute-done.4), channel_id=1, source_target_pairs={{0,256},{256,0},{512,768},{768,512},{1,257},{257,1},{513,769},{769... | collective-permute-start | bytes 1769480 | tf_op jit(solution)/shard_map/ppermute | solution.py:80
  122.1 6.3 %slice-start = ((s8[7077888]{0:T(1024)(128)(4,1)}), s8[2883584]{0:T(1024)(128)(4,1)S(1)}, s32[]{:S(2)}) async-start(s8[7077888]{0:T(1024)(128)(4,1)} %bitcast.49), calls=%async_computation | async-start | bytes 5767168
  126.0 2.9 %slice-start.1 = ((s8[7077888]{0:T(1024)(128)(4,1)}), s8[4194304]{0:T(1024)(128)(4,1)S(1)}, s32[]{:S(2)}) async-start(s8[7077888]{0:T(1024)(128)(4,1)} %bitcast.49), calls=%async_computation.1 | async-start | bytes 8388608
  128.1 1.5 %copy-start.1 = (f32[3,6,256,64]{2,3,1,0:T(8,128)S(1)}, f32[3,6,256,64]{2,3,1,0:T(8,128)}, u32[]{:S(2)}) copy-start(f32[3,6,256,64]{2,3,1,0:T(8,128)} %get-tuple-element.7) | copy-start | bytes 3538948

commit v2 on v1

--- a/solution.py
+++ b/solution.py
@@ -62,26 +62,33 @@
         place = jnp.arange(count_rows, dtype=jnp.int32)[:, None] + BAND + offset
         col_part = lax.dynamic_slice_in_dim(density, start_col, width, 3)
         padded = padded_2(col_part, (("blk", 0),), BAND)
-        highest = lax.Precision.HIGHEST
         picked = padded[place[:, :, None], slot] * valid[:, :, :, None, None]
+        squared = jnp.einsum("rsac,rstcb->rtab", density, picked, precision=lax.Precision.HIGH)
+        rounded = squared.astype(jnp.bfloat16)
+        high = picked.astype(jnp.bfloat16)
+        low = (picked - high.astype(jnp.float32)).astype(jnp.bfloat16)
 
-        def product(left):
-            return jnp.einsum("rsac,rstcb->rtab", left, picked, precision=highest)
+        def cubed_part(left, half):
+            rows = lax.dynamic_slice_in_dim(high, half * 2 * width, 2 * width, 3)
+            rest = lax.dynamic_slice_in_dim(low, half * 2 * width, 2 * width, 3)
+            one = jnp.einsum("rsac,rstcb->rtab", left, rows, preferred_element_type=jnp.float32)
+            two = jnp.einsum("rsac,rstcb->rtab", left, rest, preferred_element_type=jnp.float32)
+            return one + two
 
-        squared = product(density)
-        rounded = squared.astype(jnp.bfloat16)
         across = [(i, i ^ 1) for i in range(n_layer)]
         mate = lax.ppermute(rounded, "layer", across)
+        even = (me % 2) == 0
+        near_pair = jnp.where(even, jnp.concatenate([rounded, mate], 3), jnp.concatenate([mate, rounded], 3))
+        near_part = cubed_part(near_pair, me // 2)
         if relay is None:
             far = lax.ppermute(rounded, "layer", [(i, i ^ 2) for i in range(n_layer)])
         else:
             halfway = lax.ppermute(rounded, ("layer", "blk"), relay)
+            halfway, near_part = lax.optimization_barrier((halfway, near_part))
             far = lax.ppermute(halfway, ("layer", "blk"), relay)
         far_mate = lax.ppermute(far, "layer", across)
-        pieces = jnp.stack([rounded, mate, far, far_mate])
-        quarters = jnp.take(pieces, jnp.bitwise_xor(jnp.arange(4, dtype=jnp.int32), me), axis=0)
-        gathered = jnp.moveaxis(quarters, 0, 3).reshape(count_rows, slots, order, order)
-        cubed = product(gathered.astype(jnp.float32))
+        far_pair = jnp.where(even, jnp.concatenate([far, far_mate], 3), jnp.concatenate([far_mate, far], 3))
+        cubed = near_part + cubed_part(far_pair, 1 - me // 2)
         return (squared, 3.0 * squared - 2.0 * cubed)
 
     return body

time: 135 us -> 118 us (0.87)
  waiting for transfers between devices: 50.1 us -> 28.1 us
  starting transfers between devices: 38.8 us -> 47.6 us
  local copies, waits for them, and re-layouts: 16.1 us -> 10.8 us
  matrix products: 19.8 us -> 21.9 us
    ppermute x1, waiting for transfers between devices: 17.9 us -> 0.01 us  [padded_2(): after = lax.ppermute(initial, axis, down)]
    ppermute x1, waiting for transfers between devices: 13.1 us -> 0.01 us  [body(): halfway = lax.ppermute(rounded, ('layer', 'blk'), relay)]
    ppermute x1, starting transfers between devices: 1.92 us -> 9.23 us  [body(): mate = lax.ppermute(rounded, 'layer', across)]
    ppermute x1, waiting for transfers between devices: 8.71 us -> 13.1 us  [body(): far = lax.ppermute(halfway, ('layer', 'blk'), relay)]
    ppermute x1, waiting for transfers between devices: 8.94 us -> 13 us  [padded_2(): before = lax.ppermute(last, axis, up)]
    gather x1 -> x0, local copies, waits for them, and re-layouts: 3.91 us -> none  [body(): jnp.take(pieces, jnp.bitwise_xor(jnp.arange(4, dtype=jnp.int32), me), axi...]
    convert_element_type x0 -> x1, other arithmetic: none -> 3.59 us  [body(): high = picked.astype(jnp.bfloat16)]
    dot_general x2 -> x5, matrix products: 19.8 us -> 21.9 us  [the longest x1 8.78 us: body(): jnp.einsum('rsac,rstcb->rtab', density, picked, precision=lax.Precision.H...]
  transfers between devices with their start and end apart: 6 -> 6, of which waited for: 5 -> 3; matrix products, arithmetic and copies ran while one was open for 4% -> 13% of each run, Pallas kernels for 0% -> 0%
where the time goes in v2:
time: 118 us
  starting transfers between devices  47.6 us (40%)
  waiting for transfers between devices  28.1 us (24%)
  matrix products  21.9 us (19%)
  local copies, waits for them, and re-layouts  10.8 us (9%)
  other arithmetic  8.48 us (7%)
    ppermute x1, starting transfers between devices, padded_2(): after = lax.ppermute(initial, axis, down)  15.2 us
    ppermute x1, waiting for transfers between devices, body(): far = lax.ppermute(halfway, ('layer', 'blk'), relay)  13.1 us
    ppermute x1, waiting for transfers between devices, padded_2(): before = lax.ppermute(last, axis, up)  13 us
    ppermute x1, starting transfers between devices, body(): mate = lax.ppermute(rounded, 'layer', across)  9.23 us
    dot_general x1, matrix products, body(): jnp.einsum('rsac,rstcb->rtab', density, picked, precision=lax.Precision.H...  8.78 us
    ppermute x1, starting transfers between devices, body(): far = lax.ppermute(halfway, ('layer', 'blk'), relay)  7.75 us
    ppermute x1, starting transfers between devices, body(): halfway = lax.ppermute(rounded, ('layer', 'blk'), relay)  7.34 us
    dot_general x2, matrix products, cubed_part(): jnp.einsum('rsac,rstcb->rtab', left, rows, preferred_element_type=jnp.flo...  6.83 us
  transfers between devices with their start and end apart: 6, of which 3 were waited for; matrix products, arithmetic and copies ran while one was open for 13% of the time, Pallas kernels for 0%

profile of v2, /device:TPU:1, one launch (start us, length us, event | category | flops | bytes accessed | tf_op | source)
XLA Modules:
  0.0 117.7 jit_solution(11564059548149611812)
XLA Ops:
  0.6 2.3 %constant_dynamic-slice_fusion.1 = f32[3,6,256,64]{3,2,1,0:T(8,128)S(1)} fusion(f32[3,6,256,256]{3,2,1,0:T(8,128)} %param.2, s32[]{:T(128)S(6)} %select_n.58), kind=kLoop, calls=%fused_computation.55 | loop fusion | bytes 2359300 | tf_op jit(solution)/shard_map/dynamic_slice | solution.py:63
  3.0 0.9 copy.69
  3.9 3.9 %collective-permute-start = (f32[3,6,256,64]{2,3,1,0:T(8,128)S(1)}, f32[3,6,256,64]{2,3,1,0:T(8,128)S(1)}, u32[]{:S(2)}, u32[]{:S(2)}) collective-permute-start(f32[3,6,256,64]{2,3,1,0:T(8,128)S(1)} %copy.69), channel_id=1, source_target_pairs={{0,1},{1,2},{2,3},{3,4},{4,5},{5,6},{6,7},{7,8},{8,9},{9,10},{10,1... | collective-permute-start | bytes 3538952 | tf_op jit(solution)/shard_map/ppermute | solution.py:16
  7.8 15.2 %collective-permute-start.1 = (f32[3,6,256,64]{2,3,1,0:T(8,128)S(1)}, f32[3,6,256,64]{2,3,1,0:T(8,128)}, u32[]{:S(2)}, u32[]{:S(2)}) collective-permute-start(f32[3,6,256,64]{2,3,1,0:T(8,128)S(1)} %copy.69), channel_id=1, source_target_pairs={{1,0},{2,1},{3,2},{4,3},{5,4},{6,5},{7,6},{8,7},{9,8},{10,9},{11,1... | collective-permute-start | bytes 3538952 | tf_op jit(solution)/shard_map/ppermute | solution.py:17
  23.0 0.9 copy.40
  24.0 0.8 fusion.63
  24.8 0.1 copy.43
  24.8 0.1 copy.39
  24.9 0.1 reshape.25
  25.0 0.6 gather_fusion
  25.6 0.1 copy.38
  25.7 1.3 %fusion.55 = (s32[3,6,6]{2,1,0:T(8,128)}, s32[3,6,6]{2,1,0:T(8,128)S(1)}) fusion(s32[3,6]{1,0:T(4,128)S(1)} %copy.43, s32[3,6,6]{2,1,0:T(8,128)S(1)} %reshape.54), kind=kLoop, calls=%fused_computation.35 | loop fusion | flops 5076 | bytes 1368 | tf_op jit(solution)/shard_map/make_body.<locals>.body/reduce | solution.py:58
  27.0 0.1 fusion.59
  27.1 0.1 reshape.31
  27.2 0.5 compare_reduce_fusion
  27.7 0.1 copy.44
  27.8 13.0 %collective-permute-done = f32[3,6,256,64]{2,3,1,0:T(8,128)S(1)} collective-permute-done((f32[3,6,256,64]{2,3,1,0:T(8,128)S(1)}, f32[3,6,256,64]{2,3,1,0:T(8,128)S(1)}, u32[]{:S(2)}, u32[]{:S(2)}) %collective-permute-start) | collective-permute-done | bytes 1179680 | tf_op jit(solution)/shard_map/ppermute | solution.py:16
  40.8 1.0 copy-done.3
  41.8 2.2 %pad_maximum_fusion = f32[9,6,256,64]{2,3,1,0:T(8,128)S(1)} fusion(f32[3,6,256,64]{2,3,1,0:T(8,128)} %collective-permute-done.1, f32[3,6,256,64]{2,3,1,0:T(8,128)} %copy-done, f32[3,6,256,64]{2,3,1,0:T(8,128)} %copy-done.3), kind=kLoop, calls=%fused_computation.7 | loop fusion | flops 1769472 | bytes 7077888 | tf_op jit(solution)/shard_map/concatenate | solution.py:18
  44.0 4.5 %gather_fusion.1 = f32[108,256,64]{1,2,0:T(8,128)} fusion(f32[9,6,256,64]{2,3,1,0:T(8,128)S(1)} %pad_maximum_fusion, s32[108]{0:T(128)S(1)} %reshape.31), kind=kCustom, calls=%fused_computation.1 | custom fusion | bytes 14156640 | tf_op jit(solution)/shard_map/gather | solution.py:65
  48.5 8.8 %fusion.72 = (bf16[3,6,256,64]{2,3,1,0:T(8,128)(2,1)}, f32[3,6,256,64]{2,3,1,0:T(8,128)}) fusion(f32[3,6,256,256]{3,2,1,0:T(8,128)} %param.2, f32[3,6,6,256,64]{3,4,2,1,0:T(8,128)} %bitcast.73, f32[3,6,6]{1,2,0:T(8,128)S(1)} %copy.44), kind=kOutput, calls=%fused_computation.62 | convolution fusion | flops 2719973376 | bytes 13566384 | tf_op jit(solution)/shard_map/rsac,rstcb->rtab/dot_general | solution.py:66
  57.3 9.2 %collective-permute-start.3 = (bf16[3,6,256,64]{2,3,1,0:T(8,128)(2,1)}, bf16[3,6,256,64]{2,3,1,0:T(8,128)(2,1)}, u32[]{:S(2)}, u32[]{:S(2)}) collective-permute-start(bf16[3,6,256,64]{2,3,1,0:T(8,128)(2,1)} %get-tuple-element.12), channel_id=1, source_target_pairs={{0,256},{256,0},{512,768},{768,512},{1,257},{257,1},{513,769},{769... | collective-permute-start | bytes 1769480 | tf_op jit(solution)/shard_map/ppermute | solution.py:79
  66.6 7.3 %collective-permute-start.2 = (bf16[3,6,256,64]{2,3,1,0:T(8,128)(2,1)}, bf16[3,6,256,64]{2,3,1,0:T(8,128)(2,1)S(1)}, u32[]{:S(2)}, u32[]{:S(2)}) collective-permute-start(bf16[3,6,256,64]{2,3,1,0:T(8,128)(2,1)} %get-tuple-element.12), channel_id=1, source_target_pairs={{0,128},{1,129},{2,130},{3,131},{4,132},{5,133},{6,134},{7,135},{8... | collective-permute-start | bytes 1769480 | tf_op jit(solution)/shard_map/ppermute | solution.py:86
  73.9 3.6 %fusion = (bf16[3,6,6,256,64]{3,4,1,2,0:T(8,128)(2,1)S(1)}, bf16[3,6,6,256,64]{3,4,1,2,0:T(8,128)(2,1)S(1)}) fusion(f32[3,6,6,256,64]{3,4,2,1,0:T(8,128)} %bitcast.74, f32[3,6,6]{1,2,0:T(8,128)S(1)} %copy.44), kind=kLoop, calls=%fused_computation.4 | loop fusion | flops 8847360 | bytes 14156208 | tf_op jit(solution)/shard_map/convert_element_type | solution.py:68
  77.5 3.5 %fusion.15 = f32[3,6,64,256]{3,2,1,0:T(8,128)S(1)} fusion(bf16[3,6,6,256,64]{3,4,1,2,0:T(8,128)(2,1)S(1)} %get-tuple-element.11, s32[]{:T(128)S(6)} %select_n.65, bf16[3,6,256,64]{2,3,1,0:T(8,128)(2,1)} %collective-permute-done.3, bf16[3,6,256,64]{2,3,1,0:T(8,128)(2,1)} %get-tuple-element.12, pred[]{:T(512)S(6)} %eq.25), kind=kOutput, calls=%fused_computation.18 | convolution fusion | flops 458293248 | bytes 4128773 | tf_op jit(solution)/shard_map/rsac,rstcb->rtab/dot_general | solution.py:75
  81.1 3.4 %fusion.42 = f32[3,6,256,64]{2,3,1,0:T(8,128)} fusion(f32[3,6,64,256]{3,2,1,0:T(8,128)S(1)} %fusion.15, bf16[3,6,6,256,64]{3,4,1,2,0:T(8,128)(2,1)S(1)} %get-tuple-element.10, s32[]{:T(128)S(6)} %select_n.65, bf16[3,6,256,64]{2,3,1,0:T(8,128)(2,1)} %collective-permute-done.3, bf16[3,6,256,64]{2,3,1,0:T(8,128)(2,1)} %get-tuple-element.12, pred[]{:T(512)S(6)} %eq.25), kind=kOutput, calls=%fused_computation.27 | convolution fusion | flops 458588160 | bytes 5308421 | tf_op jit(solution)/shard_map/rsac,rstcb->rtab/dot_general | solution.py:74
  84.5 7.7 %collective-permute-start.4 = (bf16[3,6,256,64]{2,3,1,0:T(8,128)(2,1)S(1)}, bf16[3,6,256,64]{2,3,1,0:T(8,128)(2,1)}, u32[]{:S(2)}, u32[]{:S(2)}) collective-permute-start(bf16[3,6,256,64]{2,3,1,0:T(8,128)(2,1)S(1)} %collective-permute-done.2), channel_id=1, source_target_pairs={{0,128},{1,129},{2,130},{3,131},{4,132},{5,133},{6,134},{7,135},{8... | collective-permute-start | bytes 1769480 | tf_op jit(solution)/shard_map/ppermute | solution.py:88
  92.2 13.1 %collective-permute-done.4 = bf16[3,6,256,64]{2,3,1,0:T(8,128)(2,1)} collective-permute-done((bf16[3,6,256,64]{2,3,1,0:T(8,128)(2,1)S(1)}, bf16[3,6,256,64]{2,3,1,0:T(8,128)(2,1)}, u32[]{:S(2)}, u32[]{:S(2)}) %collective-permute-start.4) | collective-permute-done | bytes 589856 | tf_op jit(solution)/shard_map/ppermute | solution.py:88
  105.4 4.1 %collective-permute-start.5 = (bf16[3,6,256,64]{2,3,1,0:T(8,128)(2,1)}, bf16[3,6,256,64]{2,3,1,0:T(8,128)(2,1)}, u32[]{:S(2)}, u32[]{:S(2)}) collective-permute-start(bf16[3,6,256,64]{2,3,1,0:T(8,128)(2,1)} %collective-permute-done.4), channel_id=1, source_target_pairs={{0,256},{256,0},{512,768},{768,512},{1,257},{257,1},{513,769},{769... | collective-permute-start | bytes 1769480 | tf_op jit(solution)/shard_map/ppermute | solution.py:89
  109.6 1.9 %collective-permute-done.5 = bf16[3,6,256,64]{2,3,1,0:T(8,128)(2,1)} collective-permute-done((bf16[3,6,256,64]{2,3,1,0:T(8,128)(2,1)}, bf16[3,6,256,64]{2,3,1,0:T(8,128)(2,1)}, u32[]{:S(2)}, u32[]{:S(2)}) %collective-permute-start.5) | collective-permute-done | bytes 589856 | tf_op jit(solution)/shard_map/ppermute | solution.py:89
  111.5 2.8 %fusion.21 = f32[3,6,64,256]{3,2,1,0:T(8,128)S(1)} fusion(bf16[3,6,6,256,64]{3,4,1,2,0:T(8,128)(2,1)} %copy-done.1, s32[]{:T(128)S(6)} %select_n.69, bf16[3,6,256,64]{2,3,1,0:T(8,128)(2,1)} %collective-permute-done.5, bf16[3,6,256,64]{2,3,1,0:T(8,128)(2,1)} %collective-permute-done.4, pred[]{:T(512)S(6)} %eq.25), kind=kOutput, calls=%fused_computation.20 | convolution fusion | flops 458293248 | bytes 4128773 | tf_op jit(solution)/shard_map/rsac,rstcb->rtab/dot_general | solution.py:75
  114.3 3.4 %multiply_subtract_fusion = f32[3,6,256,64]{2,3,1,0:T(8,128)} fusion(f32[3,6,256,64]{2,3,1,0:T(8,128)S(1)} %copy-done.2, f32[3,6,256,64]{2,3,1,0:T(8,128)S(1)} %copy-done.4, f32[3,6,64,256]{3,2,1,0:T(8,128)S(1)} %fusion.21, bf16[3,6,256,64]{2,3,1,0:T(8,128)(2,1)} %collective-permute-done.5, bf16[3,6,256,64]{2,3,1,0:T(8,128)(2,1)} %collective-permute-done.4, ...), kind=kOutput, calls=%fused_computation.32 | convolution fusion | flops 459767808 | bytes 7667717 | tf_op jit(solution)/shard_map/rsac,rstcb->rtab/dot_general | solution.py:74
  (17 shorter events, 0.1 us)
Async XLA Ops:
  3.9 36.9 %copy-start = (f32[3,6,256,64]{2,3,1,0:T(8,128)}, f32[3,6,256,64]{2,3,1,0:T(8,128)S(1)}, u32[]{:S(2)}) copy-start(f32[3,6,256,64]{2,3,1,0:T(8,128)S(1)} %copy.69) | copy-start | bytes 3538948
  3.9 36.9 %collective-permute-start = (f32[3,6,256,64]{2,3,1,0:T(8,128)S(1)}, f32[3,6,256,64]{2,3,1,0:T(8,128)S(1)}, u32[]{:S(2)}, u32[]{:S(2)}) collective-permute-start(f32[3,6,256,64]{2,3,1,0:T(8,128)S(1)} %copy.69), channel_id=1, source_target_pairs={{0,1},{1,2},{2,3},{3,4},{4,5},{5,6},{6,7},{7,8},{8,9},{9,10},{10,1... | collective-permute-start | bytes 3538952 | tf_op jit(solution)/shard_map/ppermute | solution.py:16
  7.8 34.0 %collective-permute-start.1 = (f32[3,6,256,64]{2,3,1,0:T(8,128)S(1)}, f32[3,6,256,64]{2,3,1,0:T(8,128)}, u32[]{:S(2)}, u32[]{:S(2)}) collective-permute-start(f32[3,6,256,64]{2,3,1,0:T(8,128)S(1)} %copy.69), channel_id=1, source_target_pairs={{1,0},{2,1},{3,2},{4,3},{5,4},{6,5},{7,6},{8,7},{9,8},{10,9},{11,1... | collective-permute-start | bytes 3538952 | tf_op jit(solution)/shard_map/ppermute | solution.py:17
  40.8 1.0 copy-start.3
  57.3 20.2 %collective-permute-start.3 = (bf16[3,6,256,64]{2,3,1,0:T(8,128)(2,1)}, bf16[3,6,256,64]{2,3,1,0:T(8,128)(2,1)}, u32[]{:S(2)}, u32[]{:S(2)}) collective-permute-start(bf16[3,6,256,64]{2,3,1,0:T(8,128)(2,1)} %get-tuple-element.12), channel_id=1, source_target_pairs={{0,256},{256,0},{512,768},{768,512},{1,257},{257,1},{513,769},{769... | collective-permute-start | bytes 1769480 | tf_op jit(solution)/shard_map/ppermute | solution.py:79
  66.6 17.9 %collective-permute-start.2 = (bf16[3,6,256,64]{2,3,1,0:T(8,128)(2,1)}, bf16[3,6,256,64]{2,3,1,0:T(8,128)(2,1)S(1)}, u32[]{:S(2)}, u32[]{:S(2)}) collective-permute-start(bf16[3,6,256,64]{2,3,1,0:T(8,128)(2,1)} %get-tuple-element.12), channel_id=1, source_target_pairs={{0,128},{1,129},{2,130},{3,131},{4,132},{5,133},{6,134},{7,135},{8... | collective-permute-start | bytes 1769480 | tf_op jit(solution)/shard_map/ppermute | solution.py:86
  77.5 7.0 %copy-start.1 = (bf16[3,6,6,256,64]{3,4,1,2,0:T(8,128)(2,1)}, bf16[3,6,6,256,64]{3,4,1,2,0:T(8,128)(2,1)S(1)}, u32[]{:S(2)}) copy-start(bf16[3,6,6,256,64]{3,4,1,2,0:T(8,128)(2,1)S(1)} %get-tuple-element.11) | copy-start | bytes 10616836
  84.5 20.9 %collective-permute-start.4 = (bf16[3,6,256,64]{2,3,1,0:T(8,128)(2,1)S(1)}, bf16[3,6,256,64]{2,3,1,0:T(8,128)(2,1)}, u32[]{:S(2)}, u32[]{:S(2)}) collective-permute-start(bf16[3,6,256,64]{2,3,1,0:T(8,128)(2,1)S(1)} %collective-permute-done.2), channel_id=1, source_target_pairs={{0,128},{1,129},{2,130},{3,131},{4,132},{5,133},{6,134},{7,135},{8... | collective-permute-start | bytes 1769480 | tf_op jit(solution)/shard_map/ppermute | solution.py:88
  105.4 6.1 %collective-permute-start.5 = (bf16[3,6,256,64]{2,3,1,0:T(8,128)(2,1)}, bf16[3,6,256,64]{2,3,1,0:T(8,128)(2,1)}, u32[]{:S(2)}, u32[]{:S(2)}) collective-permute-start(bf16[3,6,256,64]{2,3,1,0:T(8,128)(2,1)} %collective-permute-done.4), channel_id=1, source_target_pairs={{0,256},{256,0},{512,768},{768,512},{1,257},{257,1},{513,769},{769... | collective-permute-start | bytes 1769480 | tf_op jit(solution)/shard_map/ppermute | solution.py:89
  109.5 4.7 %copy-start.2 = (f32[3,6,256,64]{2,3,1,0:T(8,128)S(1)}, f32[3,6,256,64]{2,3,1,0:T(8,128)}, u32[]{:S(2)}) copy-start(f32[3,6,256,64]{2,3,1,0:T(8,128)} %get-tuple-element.13) | copy-start | bytes 3538948
  109.5 4.7 %copy-start.4 = (f32[3,6,256,64]{2,3,1,0:T(8,128)S(1)}, f32[3,6,256,64]{2,3,1,0:T(8,128)}, u32[]{:S(2)}) copy-start(f32[3,6,256,64]{2,3,1,0:T(8,128)} %fusion.42) | copy-start | bytes 3538948

commit v3 on v2

--- a/solution.py
+++ b/solution.py
@@ -65,8 +65,9 @@
         picked = padded[place[:, :, None], slot] * valid[:, :, :, None, None]
         squared = jnp.einsum("rsac,rstcb->rtab", density, picked, precision=lax.Precision.HIGH)
         rounded = squared.astype(jnp.bfloat16)
-        high = picked.astype(jnp.bfloat16)
-        low = (picked - high.astype(jnp.float32)).astype(jnp.bfloat16)
+        top = lax.reduce_precision(picked, exponent_bits=8, mantissa_bits=7)
+        high = top.astype(jnp.bfloat16)
+        low = (picked - top).astype(jnp.bfloat16)
 
         def cubed_part(left, half):
             rows = lax.dynamic_slice_in_dim(high, half * 2 * width, 2 * width, 3)

time: 118 us -> 118 us (level)
  no operation moved by 1% of the time
where the time goes in v3:
time: 118 us
  starting transfers between devices  47.5 us (40%)
  waiting for transfers between devices  28.1 us (24%)
  matrix products  21.9 us (19%)
  local copies, waits for them, and re-layouts  10.8 us (9%)
  other arithmetic  8.59 us (7%)
    ppermute x1, starting transfers between devices, padded_2(): after = lax.ppermute(initial, axis, down)  15.2 us
    ppermute x1, waiting for transfers between devices, body(): far = lax.ppermute(halfway, ('layer', 'blk'), relay)  13.1 us
    ppermute x1, waiting for transfers between devices, padded_2(): before = lax.ppermute(last, axis, up)  13 us
    ppermute x1, starting transfers between devices, body(): mate = lax.ppermute(rounded, 'layer', across)  9.23 us
    dot_general x1, matrix products, body(): jnp.einsum('rsac,rstcb->rtab', density, picked, precision=lax.Precision.H...  8.78 us
    ppermute x1, starting transfers between devices, body(): far = lax.ppermute(halfway, ('layer', 'blk'), relay)  7.64 us
    ppermute x1, starting transfers between devices, body(): halfway = lax.ppermute(rounded, ('layer', 'blk'), relay)  7.34 us
    dot_general x2, matrix products, cubed_part(): jnp.einsum('rsac,rstcb->rtab', left, rows, preferred_element_type=jnp.flo...  6.83 us
  transfers between devices with their start and end apart: 6, of which 3 were waited for; matrix products, arithmetic and copies ran while one was open for 13% of the time, Pallas kernels for 0%

profile of v3, /device:TPU:1, one launch (start us, length us, event | category | flops | bytes accessed | tf_op | source)
XLA Modules:
  0.0 117.7 jit_solution(13112823739526226483)
XLA Ops:
  0.6 2.3 %constant_dynamic-slice_fusion.1 = f32[3,6,256,64]{3,2,1,0:T(8,128)S(1)} fusion(f32[3,6,256,256]{3,2,1,0:T(8,128)} %param.2, s32[]{:T(128)S(6)} %select_n.58), kind=kLoop, calls=%fused_computation.56 | loop fusion | bytes 2359300 | tf_op jit(solution)/shard_map/dynamic_slice | solution.py:63
  3.0 0.9 copy.69
  3.9 3.9 %collective-permute-start = (f32[3,6,256,64]{2,3,1,0:T(8,128)S(1)}, f32[3,6,256,64]{2,3,1,0:T(8,128)S(1)}, u32[]{:S(2)}, u32[]{:S(2)}) collective-permute-start(f32[3,6,256,64]{2,3,1,0:T(8,128)S(1)} %copy.69), channel_id=1, source_target_pairs={{0,1},{1,2},{2,3},{3,4},{4,5},{5,6},{6,7},{7,8},{8,9},{9,10},{10,1... | collective-permute-start | bytes 3538952 | tf_op jit(solution)/shard_map/ppermute | solution.py:16
  7.8 15.2 %collective-permute-start.1 = (f32[3,6,256,64]{2,3,1,0:T(8,128)S(1)}, f32[3,6,256,64]{2,3,1,0:T(8,128)}, u32[]{:S(2)}, u32[]{:S(2)}) collective-permute-start(f32[3,6,256,64]{2,3,1,0:T(8,128)S(1)} %copy.69), channel_id=1, source_target_pairs={{1,0},{2,1},{3,2},{4,3},{5,4},{6,5},{7,6},{8,7},{9,8},{10,9},{11,1... | collective-permute-start | bytes 3538952 | tf_op jit(solution)/shard_map/ppermute | solution.py:17
  23.0 0.9 copy.40
  24.0 0.8 fusion.63
  24.8 0.1 copy.43
  24.8 0.1 copy.39
  24.9 0.1 reshape.25
  25.0 0.6 gather_fusion
  25.6 0.1 copy.38
  25.7 1.3 %fusion.55 = (s32[3,6,6]{2,1,0:T(8,128)}, s32[3,6,6]{2,1,0:T(8,128)S(1)}) fusion(s32[3,6]{1,0:T(4,128)S(1)} %copy.43, s32[3,6,6]{2,1,0:T(8,128)S(1)} %reshape.54), kind=kLoop, calls=%fused_computation.36 | loop fusion | flops 5076 | bytes 1368 | tf_op jit(solution)/shard_map/make_body.<locals>.body/reduce | solution.py:58
  27.0 0.1 fusion.59
  27.1 0.1 reshape.31
  27.2 0.5 compare_reduce_fusion
  27.7 0.1 copy.44
  27.8 13.0 %collective-permute-done = f32[3,6,256,64]{2,3,1,0:T(8,128)S(1)} collective-permute-done((f32[3,6,256,64]{2,3,1,0:T(8,128)S(1)}, f32[3,6,256,64]{2,3,1,0:T(8,128)S(1)}, u32[]{:S(2)}, u32[]{:S(2)}) %collective-permute-start) | collective-permute-done | bytes 1179680 | tf_op jit(solution)/shard_map/ppermute | solution.py:16
  40.8 1.0 copy-done.3
  41.8 2.2 %pad_maximum_fusion = f32[9,6,256,64]{2,3,1,0:T(8,128)S(1)} fusion(f32[3,6,256,64]{2,3,1,0:T(8,128)} %collective-permute-done.1, f32[3,6,256,64]{2,3,1,0:T(8,128)} %copy-done, f32[3,6,256,64]{2,3,1,0:T(8,128)} %copy-done.3), kind=kLoop, calls=%fused_computation.8 | loop fusion | flops 1769472 | bytes 7077888 | tf_op jit(solution)/shard_map/concatenate | solution.py:18
  44.0 4.5 %gather_fusion.1 = f32[108,256,64]{1,2,0:T(8,128)} fusion(f32[9,6,256,64]{2,3,1,0:T(8,128)S(1)} %pad_maximum_fusion, s32[108]{0:T(128)S(1)} %reshape.31), kind=kCustom, calls=%fused_computation.1 | custom fusion | bytes 14156640 | tf_op jit(solution)/shard_map/gather | solution.py:65
  48.5 8.8 %fusion.72 = (bf16[3,6,256,64]{2,3,1,0:T(8,128)(2,1)}, f32[3,6,256,64]{2,3,1,0:T(8,128)}) fusion(f32[3,6,256,256]{3,2,1,0:T(8,128)} %param.2, f32[3,6,6,256,64]{3,4,2,1,0:T(8,128)} %bitcast.73, f32[3,6,6]{1,2,0:T(8,128)S(1)} %copy.44), kind=kOutput, calls=%fused_computation.63 | convolution fusion | flops 2719973376 | bytes 13566384 | tf_op jit(solution)/shard_map/rsac,rstcb->rtab/dot_general | solution.py:66
  57.3 9.2 %collective-permute-start.3 = (bf16[3,6,256,64]{2,3,1,0:T(8,128)(2,1)}, bf16[3,6,256,64]{2,3,1,0:T(8,128)(2,1)}, u32[]{:S(2)}, u32[]{:S(2)}) collective-permute-start(bf16[3,6,256,64]{2,3,1,0:T(8,128)(2,1)} %get-tuple-element.12), channel_id=1, source_target_pairs={{0,256},{256,0},{512,768},{768,512},{1,257},{257,1},{513,769},{769... | collective-permute-start | bytes 1769480 | tf_op jit(solution)/shard_map/ppermute | solution.py:80
  66.6 7.3 %collective-permute-start.2 = (bf16[3,6,256,64]{2,3,1,0:T(8,128)(2,1)}, bf16[3,6,256,64]{2,3,1,0:T(8,128)(2,1)S(1)}, u32[]{:S(2)}, u32[]{:S(2)}) collective-permute-start(bf16[3,6,256,64]{2,3,1,0:T(8,128)(2,1)} %get-tuple-element.12), channel_id=1, source_target_pairs={{0,128},{1,129},{2,130},{3,131},{4,132},{5,133},{6,134},{7,135},{8... | collective-permute-start | bytes 1769480 | tf_op jit(solution)/shard_map/ppermute | solution.py:87
  73.9 3.7 %reduce-precision_convert_fusion = (bf16[3,6,6,256,64]{3,4,1,2,0:T(8,128)(2,1)S(1)}, bf16[3,6,6,256,64]{3,4,1,2,0:T(8,128)(2,1)S(1)}) fusion(f32[3,6,6,256,64]{3,4,2,1,0:T(8,128)} %bitcast.74, f32[3,6,6]{1,2,0:T(8,128)S(1)} %copy.44), kind=kLoop, calls=%fused_computation.3 | loop fusion | flops 8847360 | bytes 14156208 | tf_op jit(solution)/shard_map/convert_element_type | solution.py:69
  77.7 3.5 %fusion.15 = f32[3,6,64,256]{3,2,1,0:T(8,128)S(1)} fusion(bf16[3,6,6,256,64]{3,4,1,2,0:T(8,128)(2,1)S(1)} %get-tuple-element.11, s32[]{:T(128)S(6)} %select_n.65, bf16[3,6,256,64]{2,3,1,0:T(8,128)(2,1)} %collective-permute-done.3, bf16[3,6,256,64]{2,3,1,0:T(8,128)(2,1)} %get-tuple-element.12, pred[]{:T(512)S(6)} %eq.25), kind=kOutput, calls=%fused_computation.19 | convolution fusion | flops 458293248 | bytes 4128773 | tf_op jit(solution)/shard_map/rsac,rstcb->rtab/dot_general | solution.py:76
  81.2 3.4 %fusion.42 = f32[3,6,256,64]{2,3,1,0:T(8,128)} fusion(f32[3,6,64,256]{3,2,1,0:T(8,128)S(1)} %fusion.15, bf16[3,6,6,256,64]{3,4,1,2,0:T(8,128)(2,1)S(1)} %get-tuple-element.10, s32[]{:T(128)S(6)} %select_n.65, bf16[3,6,256,64]{2,3,1,0:T(8,128)(2,1)} %collective-permute-done.3, bf16[3,6,256,64]{2,3,1,0:T(8,128)(2,1)} %get-tuple-element.12, pred[]{:T(512)S(6)} %eq.25), kind=kOutput, calls=%fused_computation.28 | convolution fusion | flops 458588160 | bytes 5308421 | tf_op jit(solution)/shard_map/rsac,rstcb->rtab/dot_general | solution.py:75
  84.6 7.6 %collective-permute-start.4 = (bf16[3,6,256,64]{2,3,1,0:T(8,128)(2,1)S(1)}, bf16[3,6,256,64]{2,3,1,0:T(8,128)(2,1)}, u32[]{:S(2)}, u32[]{:S(2)}) collective-permute-start(bf16[3,6,256,64]{2,3,1,0:T(8,128)(2,1)S(1)} %collective-permute-done.2), channel_id=1, source_target_pairs={{0,128},{1,129},{2,130},{3,131},{4,132},{5,133},{6,134},{7,135},{8... | collective-permute-start | bytes 1769480 | tf_op jit(solution)/shard_map/ppermute | solution.py:89
  92.2 13.1 %collective-permute-done.4 = bf16[3,6,256,64]{2,3,1,0:T(8,128)(2,1)} collective-permute-done((bf16[3,6,256,64]{2,3,1,0:T(8,128)(2,1)S(1)}, bf16[3,6,256,64]{2,3,1,0:T(8,128)(2,1)}, u32[]{:S(2)}, u32[]{:S(2)}) %collective-permute-start.4) | collective-permute-done | bytes 589856 | tf_op jit(solution)/shard_map/ppermute | solution.py:89
  105.4 4.1 %collective-permute-start.5 = (bf16[3,6,256,64]{2,3,1,0:T(8,128)(2,1)}, bf16[3,6,256,64]{2,3,1,0:T(8,128)(2,1)}, u32[]{:S(2)}, u32[]{:S(2)}) collective-permute-start(bf16[3,6,256,64]{2,3,1,0:T(8,128)(2,1)} %collective-permute-done.4), channel_id=1, source_target_pairs={{0,256},{256,0},{512,768},{768,512},{1,257},{257,1},{513,769},{769... | collective-permute-start | bytes 1769480 | tf_op jit(solution)/shard_map/ppermute | solution.py:90
  109.6 1.9 %collective-permute-done.5 = bf16[3,6,256,64]{2,3,1,0:T(8,128)(2,1)} collective-permute-done((bf16[3,6,256,64]{2,3,1,0:T(8,128)(2,1)}, bf16[3,6,256,64]{2,3,1,0:T(8,128)(2,1)}, u32[]{:S(2)}, u32[]{:S(2)}) %collective-permute-start.5) | collective-permute-done | bytes 589856 | tf_op jit(solution)/shard_map/ppermute | solution.py:90
  111.5 2.8 %fusion.21 = f32[3,6,64,256]{3,2,1,0:T(8,128)S(1)} fusion(bf16[3,6,6,256,64]{3,4,1,2,0:T(8,128)(2,1)} %copy-done.1, s32[]{:T(128)S(6)} %select_n.69, bf16[3,6,256,64]{2,3,1,0:T(8,128)(2,1)} %collective-permute-done.5, bf16[3,6,256,64]{2,3,1,0:T(8,128)(2,1)} %collective-permute-done.4, pred[]{:T(512)S(6)} %eq.25), kind=kOutput, calls=%fused_computation.21 | convolution fusion | flops 458293248 | bytes 4128773 | tf_op jit(solution)/shard_map/rsac,rstcb->rtab/dot_general | solution.py:76
  114.3 3.4 %multiply_subtract_fusion = f32[3,6,256,64]{2,3,1,0:T(8,128)} fusion(f32[3,6,256,64]{2,3,1,0:T(8,128)S(1)} %copy-done.2, f32[3,6,256,64]{2,3,1,0:T(8,128)S(1)} %copy-done.4, f32[3,6,64,256]{3,2,1,0:T(8,128)S(1)} %fusion.21, bf16[3,6,256,64]{2,3,1,0:T(8,128)(2,1)} %collective-permute-done.5, bf16[3,6,256,64]{2,3,1,0:T(8,128)(2,1)} %collective-permute-done.4, ...), kind=kOutput, calls=%fused_computation.33 | convolution fusion | flops 459767808 | bytes 7667717 | tf_op jit(solution)/shard_map/rsac,rstcb->rtab/dot_general | solution.py:75
  (17 shorter events, 0.1 us)
Async XLA Ops:
  3.9 36.9 %copy-start = (f32[3,6,256,64]{2,3,1,0:T(8,128)}, f32[3,6,256,64]{2,3,1,0:T(8,128)S(1)}, u32[]{:S(2)}) copy-start(f32[3,6,256,64]{2,3,1,0:T(8,128)S(1)} %copy.69) | copy-start | bytes 3538948
  3.9 36.9 %collective-permute-start = (f32[3,6,256,64]{2,3,1,0:T(8,128)S(1)}, f32[3,6,256,64]{2,3,1,0:T(8,128)S(1)}, u32[]{:S(2)}, u32[]{:S(2)}) collective-permute-start(f32[3,6,256,64]{2,3,1,0:T(8,128)S(1)} %copy.69), channel_id=1, source_target_pairs={{0,1},{1,2},{2,3},{3,4},{4,5},{5,6},{6,7},{7,8},{8,9},{9,10},{10,1... | collective-permute-start | bytes 3538952 | tf_op jit(solution)/shard_map/ppermute | solution.py:16
  7.8 34.0 %collective-permute-start.1 = (f32[3,6,256,64]{2,3,1,0:T(8,128)S(1)}, f32[3,6,256,64]{2,3,1,0:T(8,128)}, u32[]{:S(2)}, u32[]{:S(2)}) collective-permute-start(f32[3,6,256,64]{2,3,1,0:T(8,128)S(1)} %copy.69), channel_id=1, source_target_pairs={{1,0},{2,1},{3,2},{4,3},{5,4},{6,5},{7,6},{8,7},{9,8},{10,9},{11,1... | collective-permute-start | bytes 3538952 | tf_op jit(solution)/shard_map/ppermute | solution.py:17
  40.8 1.0 copy-start.3
  57.3 20.3 %collective-permute-start.3 = (bf16[3,6,256,64]{2,3,1,0:T(8,128)(2,1)}, bf16[3,6,256,64]{2,3,1,0:T(8,128)(2,1)}, u32[]{:S(2)}, u32[]{:S(2)}) collective-permute-start(bf16[3,6,256,64]{2,3,1,0:T(8,128)(2,1)} %get-tuple-element.12), channel_id=1, source_target_pairs={{0,256},{256,0},{512,768},{768,512},{1,257},{257,1},{513,769},{769... | collective-permute-start | bytes 1769480 | tf_op jit(solution)/shard_map/ppermute | solution.py:80
  66.6 18.0 %collective-permute-start.2 = (bf16[3,6,256,64]{2,3,1,0:T(8,128)(2,1)}, bf16[3,6,256,64]{2,3,1,0:T(8,128)(2,1)S(1)}, u32[]{:S(2)}, u32[]{:S(2)}) collective-permute-start(bf16[3,6,256,64]{2,3,1,0:T(8,128)(2,1)} %get-tuple-element.12), channel_id=1, source_target_pairs={{0,128},{1,129},{2,130},{3,131},{4,132},{5,133},{6,134},{7,135},{8... | collective-permute-start | bytes 1769480 | tf_op jit(solution)/shard_map/ppermute | solution.py:87
  77.6 7.0 %copy-start.1 = (bf16[3,6,6,256,64]{3,4,1,2,0:T(8,128)(2,1)}, bf16[3,6,6,256,64]{3,4,1,2,0:T(8,128)(2,1)S(1)}, u32[]{:S(2)}) copy-start(bf16[3,6,6,256,64]{3,4,1,2,0:T(8,128)(2,1)S(1)} %get-tuple-element.11) | copy-start | bytes 10616836
  84.6 20.8 %collective-permute-start.4 = (bf16[3,6,256,64]{2,3,1,0:T(8,128)(2,1)S(1)}, bf16[3,6,256,64]{2,3,1,0:T(8,128)(2,1)}, u32[]{:S(2)}, u32[]{:S(2)}) collective-permute-start(bf16[3,6,256,64]{2,3,1,0:T(8,128)(2,1)S(1)} %collective-permute-done.2), channel_id=1, source_target_pairs={{0,128},{1,129},{2,130},{3,131},{4,132},{5,133},{6,134},{7,135},{8... | collective-permute-start | bytes 1769480 | tf_op jit(solution)/shard_map/ppermute | solution.py:89
  105.4 6.1 %collective-permute-start.5 = (bf16[3,6,256,64]{2,3,1,0:T(8,128)(2,1)}, bf16[3,6,256,64]{2,3,1,0:T(8,128)(2,1)}, u32[]{:S(2)}, u32[]{:S(2)}) collective-permute-start(bf16[3,6,256,64]{2,3,1,0:T(8,128)(2,1)} %collective-permute-done.4), channel_id=1, source_target_pairs={{0,256},{256,0},{512,768},{768,512},{1,257},{257,1},{513,769},{769... | collective-permute-start | bytes 1769480 | tf_op jit(solution)/shard_map/ppermute | solution.py:90
  109.5 4.7 %copy-start.2 = (f32[3,6,256,64]{2,3,1,0:T(8,128)S(1)}, f32[3,6,256,64]{2,3,1,0:T(8,128)}, u32[]{:S(2)}) copy-start(f32[3,6,256,64]{2,3,1,0:T(8,128)} %get-tuple-element.13) | copy-start | bytes 3538948
  109.5 4.7 %copy-start.4 = (f32[3,6,256,64]{2,3,1,0:T(8,128)S(1)}, f32[3,6,256,64]{2,3,1,0:T(8,128)}, u32[]{:S(2)}) copy-start(f32[3,6,256,64]{2,3,1,0:T(8,128)} %fusion.42) | copy-start | bytes 3538948

commit v4 on v1

--- a/solution.py
+++ b/solution.py
@@ -60,28 +60,47 @@
         row_ids = first + jnp.arange(count_rows, dtype=jnp.int32)
         offset = (own - row_ids[:, None] + BAND) % total_rows - BAND
         place = jnp.arange(count_rows, dtype=jnp.int32)[:, None] + BAND + offset
-        col_part = lax.dynamic_slice_in_dim(density, start_col, width, 3)
-        padded = padded_2(col_part, (("blk", 0),), BAND)
-        highest = lax.Precision.HIGHEST
-        picked = padded[place[:, :, None], slot] * valid[:, :, :, None, None]
-
-        def product(left):
-            return jnp.einsum("rsac,rstcb->rtab", left, picked, precision=highest)
-
-        squared = product(density)
-        rounded = squared.astype(jnp.bfloat16)
+        chunks = 2
+        cw = width // chunks
         across = [(i, i ^ 1) for i in range(n_layer)]
-        mate = lax.ppermute(rounded, "layer", across)
-        if relay is None:
-            far = lax.ppermute(rounded, "layer", [(i, i ^ 2) for i in range(n_layer)])
-        else:
-            halfway = lax.ppermute(rounded, ("layer", "blk"), relay)
-            far = lax.ppermute(halfway, ("layer", "blk"), relay)
-        far_mate = lax.ppermute(far, "layer", across)
-        pieces = jnp.stack([rounded, mate, far, far_mate])
-        quarters = jnp.take(pieces, jnp.bitwise_xor(jnp.arange(4, dtype=jnp.int32), me), axis=0)
-        gathered = jnp.moveaxis(quarters, 0, 3).reshape(count_rows, slots, order, order)
-        cubed = product(gathered.astype(jnp.float32))
+        order_q = jnp.bitwise_xor(jnp.arange(4, dtype=jnp.int32), me)
+        squares, lefts, pickeds = [], [], []
+        arrived = None
+        for h in range(chunks):
+            col_part = lax.dynamic_slice_in_dim(density, start_col + h * cw, cw, 3)
+            if arrived is not None:
+                _, col_part = lax.optimization_barrier((arrived, col_part))
+            padded = padded_2(col_part, (("blk", 0),), BAND)
+            arrived = padded
+            picked = padded[place[:, :, None], slot] * valid[:, :, :, None, None]
+            squared = jnp.einsum("rsac,rstcb->rtab", density, picked, precision=lax.Precision.HIGH)
+            rounded = squared.astype(jnp.bfloat16)
+            mate = lax.ppermute(rounded, "layer", across)
+            if relay is None:
+                far = lax.ppermute(rounded, "layer", [(i, i ^ 2) for i in range(n_layer)])
+            else:
+                far = lax.ppermute(lax.ppermute(rounded, ("layer", "blk"), relay), ("layer", "blk"), relay)
+            far_mate = lax.ppermute(far, "layer", across)
+            pieces = jnp.take(jnp.stack([rounded, mate, far, far_mate]), order_q, axis=0)
+            lefts.append(jnp.moveaxis(pieces, 0, 3).reshape(count_rows, slots, order, 4 * cw))
+            squares.append(squared)
+            pickeds.append(picked)
+        squared = jnp.concatenate(squares, 3)
+        picked = jnp.concatenate(pickeds, 4)
+        top = lax.reduce_precision(picked, exponent_bits=8, mantissa_bits=7)
+        high = top.astype(jnp.bfloat16)
+        low = (picked - top).astype(jnp.bfloat16)
+        grid = (count_rows, slots, slots, n_layer, chunks, cw, width)
+        high = high.reshape(grid)
+        low = low.reshape(grid)
+        cubed = None
+        for h in range(chunks):
+            rows_high = high[:, :, :, :, h].reshape(count_rows, slots, slots, n_layer * cw, width)
+            rows_low = low[:, :, :, :, h].reshape(count_rows, slots, slots, n_layer * cw, width)
+            one = jnp.einsum("rsac,rstcb->rtab", lefts[h], rows_high, preferred_element_type=jnp.float32)
+            two = jnp.einsum("rsac,rstcb->rtab", lefts[h], rows_low, preferred_element_type=jnp.float32)
+            part = one + two
+            cubed = part if cubed is None else cubed + part
         return (squared, 3.0 * squared - 2.0 * cubed)
 
     return body

time: 135 us -> 227 us (1.68)
  local copies, waits for them, and re-layouts: 16.1 us -> 106 us
  waiting for transfers between devices: 50.1 us -> 15.2 us
  other arithmetic: 8.79 us -> 27.6 us
  starting transfers between devices: 38.8 us -> 56.9 us
    gather x1 -> x6, local copies, waits for them, and re-layouts: 4.48 us -> 74.9 us  [body(): picked = padded[place[:, :, None], slot] * valid[:, :, :, None, None]]
    ppermute x2 -> x4, waiting for transfers between devices: 21.8 us -> 0.01 us  [the longest x2 0.01 us: body(): lax.ppermute(rounded, ('layer', 'blk'), relay)]
    slice x0 -> x2, local copies, waits for them, and re-layouts: none -> 13.8 us  [the longest x1 9.1 us: body(): low[:, :, :, :, h].reshape(count_rows, slots, slots, n_layer * cw, width)]
    ppermute x1 -> x2, waiting for transfers between devices: 17.9 us -> 5.24 us  [padded_2(): after = lax.ppermute(initial, axis, down)]
    ppermute x2 -> x4, starting transfers between devices: 12.2 us -> 24.1 us  [the longest x2 14.4 us: body(): lax.ppermute(lax.ppermute(rounded, ('layer', 'blk'), relay), ('layer', 'b...]
    mul x0 -> x1, other arithmetic: none -> 10.6 us  [body(): picked = padded[place[:, :, None], slot] * valid[:, :, :, None, None]]
    convert_element_type x0 -> x1, other arithmetic: none -> 6.98 us  [body(): high = top.astype(jnp.bfloat16)]
    unnamed x12 -> x36, local copies, waits for them, and re-layouts: 4.01 us -> 7.89 us
  transfers between devices with their start and end apart: 6 -> 12, of which waited for: 5 -> 2; matrix products, arithmetic and copies ran while one was open for 4% -> 58% of each run, Pallas kernels for 0% -> 0%
where the time goes in v4:
time: 227 us; the launch traced here: 225 us
  local copies, waits for them, and re-layouts  106 us (47%)
  starting transfers between devices  56.9 us (25%)
  other arithmetic  27.6 us (12%)
  matrix products  18.5 us (8%)
  waiting for transfers between devices  15.2 us (7%)
    gather x6, local copies, waits for them, and re-layouts, body(): picked = padded[place[:, :, None], slot] * valid[:, :, :, None, None]  74.9 us
    ppermute x2, starting transfers between devices, padded_2(): after = lax.ppermute(initial, axis, down)  19.1 us
    ppermute x2, starting transfers between devices, body(): lax.ppermute(lax.ppermute(rounded, ('layer', 'blk'), relay), ('layer', 'b...  14.4 us
    dot_general x2, matrix products, body(): jnp.einsum('rsac,rstcb->rtab', density, picked, precision=lax.Precision.H...  12.8 us
    mul x1, other arithmetic, body(): picked = padded[place[:, :, None], slot] * valid[:, :, :, None, None]  10.6 us
    ppermute x2, waiting for transfers between devices, padded_2(): before = lax.ppermute(last, axis, up)  9.96 us
    ppermute x2, starting transfers between devices, body(): lax.ppermute(rounded, ('layer', 'blk'), relay)  9.61 us
    slice x1, local copies, waits for them, and re-layouts, body(): low[:, :, :, :, h].reshape(count_rows, slots, slots, n_layer * cw, width)  9.1 us
  transfers between devices with their start and end apart: 12, of which 2 were waited for; matrix products, arithmetic and copies ran while one was open for 58% of the time, Pallas kernels for 0%

profile of v4, /device:TPU:1, one launch (start us, length us, event | category | flops | bytes accessed | tf_op | source)
XLA Modules:
  0.0 225.1 jit_solution(6615348659288546575)
XLA Ops:
  0.6 5.1 %constant_dynamic-slice_fusion = (f32[3,6,256,32]{3,2,1,0:T(8,128)S(1)}, f32[3,6,256,32]{3,2,1,0:T(8,128)}) fusion(f32[3,6,256,256]{3,2,1,0:T(8,128)} %param.4, s32[]{:T(128)S(6)} %select_n.45, s32[]{:T(128)S(6)} %select_n.39), kind=kLoop, calls=%fused_computation.58 | loop fusion | bytes 2359304 | tf_op jit(solution)/shard_map/dynamic_slice | solution.py:70
  5.7 2.3 %copy.109 = f32[3,6,256,32]{2,3,1,0:T(8,128)S(1)} copy(f32[3,6,256,32]{3,2,1,0:T(8,128)} %get-tuple-element.16) | data formatting | bytes 1179648
  8.0 17.2 %collective-permute-start.1 = (f32[3,6,256,32]{2,3,1,0:T(8,128)S(1)}, f32[3,6,256,32]{2,3,1,0:T(8,128)}, u32[]{:S(2)}, u32[]{:S(2)}) collective-permute-start(f32[3,6,256,32]{2,3,1,0:T(8,128)S(1)} %copy.109), channel_id=1, source_target_pairs={{1,0},{2,1},{3,2},{4,3},{5,4},{6,5},{7,6},{8,7},{9,8},{10,9},{11,1... | collective-permute-start | bytes 1769480 | tf_op jit(solution)/shard_map/ppermute | solution.py:17
  25.2 1.9 collective-permute-start
  27.7 1.5 copy.110
  32.0 5.2 %collective-permute-done.1 = f32[3,6,256,32]{2,3,1,0:T(8,128)} collective-permute-done((f32[3,6,256,32]{2,3,1,0:T(8,128)S(1)}, f32[3,6,256,32]{2,3,1,0:T(8,128)}, u32[]{:S(2)}, u32[]{:S(2)}) %collective-permute-start.1) | collective-permute-done | bytes 589856 | tf_op jit(solution)/shard_map/ppermute | solution.py:17
  37.2 10.0 %collective-permute-done = f32[3,6,256,32]{2,3,1,0:T(8,128)} collective-permute-done((f32[3,6,256,32]{2,3,1,0:T(8,128)S(1)}, f32[3,6,256,32]{2,3,1,0:T(8,128)}, u32[]{:S(2)}, u32[]{:S(2)}) %collective-permute-start) | collective-permute-done | bytes 589856 | tf_op jit(solution)/shard_map/ppermute | solution.py:16
  48.6 1.9 collective-permute-start.3
  50.5 3.4 %collective-permute-start.2 = (f32[3,6,256,32]{2,3,1,0:T(8,128)}, f32[3,6,256,32]{2,3,1,0:T(8,128)}, u32[]{:S(2)}, u32[]{:S(2)}) collective-permute-start(f32[3,6,256,32]{2,3,1,0:T(8,128)} %copy.110), channel_id=1, source_target_pairs={{0,1},{1,2},{2,3},{3,4},{4,5},{5,6},{6,7},{7,8},{8,9},{9,10},{10,1... | collective-permute-start | bytes 1769480 | tf_op jit(solution)/shard_map/ppermute | solution.py:16
  53.9 3.2 %gather_fusion.1 = f32[108,256,32]{1,2,0:T(8,128)} fusion(f32[9,6,256,32]{2,3,1,0:T(8,128)S(1)} %pad_maximum_fusion.1, s32[108]{0:T(128)S(1)} %reshape.68), kind=kCustom, calls=%fused_computation.3 | custom fusion | bytes 7078752 | tf_op jit(solution)/shard_map/gather | solution.py:75
  57.1 7.0 %fusion.30 = (bf16[3,6,256,32]{2,3,1,0:T(8,128)(2,1)}, f32[3,6,256,32]{2,3,1,0:T(8,128)}) fusion(f32[3,6,256,256]{3,2,1,0:T(8,128)} %param.4, f32[3,6,6,256,32]{3,4,2,1,0:T(8,128)} %bitcast.115, f32[3,6,6]{1,2,0:T(8,128)S(1)} %copy.65), kind=kOutput, calls=%fused_computation.65 | convolution fusion | flops 1359986688 | bytes 9142704 | tf_op jit(solution)/shard_map/rsac,rstcb->rtab/dot_general | solution.py:76
  64.1 5.2 %collective-permute-start.5 = (bf16[3,6,256,32]{2,3,1,0:T(8,128)(2,1)}, bf16[3,6,256,32]{2,3,1,0:T(8,128)(2,1)}, u32[]{:S(2)}, u32[]{:S(2)}) collective-permute-start(bf16[3,6,256,32]{2,3,1,0:T(8,128)(2,1)} %get-tuple-element.21), channel_id=1, source_target_pairs={{0,128},{1,129},{2,130},{3,131},{4,132},{5,133},{6,134},{7,135},{8... | collective-permute-start | bytes 884744 | tf_op jit(solution)/shard_map/ppermute | solution.py:82
  70.4 12.9 %gather.19 = f32[3,6,6,4,2,32,32]{5,4,3,6,2,1,0:T(2,128)} reshape(f32[108,256,32]{1,2,0:T(8,128)S(1)} %copy-done) | data formatting | bytes 7077888 | tf_op jit(solution)/shard_map/gather | solution.py:75
  83.3 1.9 collective-permute-start.4
  85.2 20.0 %copy.69 = f32[3,6,6,4,2,32,32]{6,5,3,2,1,0,4:T(8,128)} copy(f32[3,6,6,4,2,32,32]{5,4,3,6,2,1,0:T(2,128)} %gather.19) | data formatting | bytes 7077888 | tf_op jit(solution)/shard_map/gather | solution.py:75
  105.3 8.7 %collective-permute-start.6 = (bf16[3,6,256,32]{2,3,1,0:T(8,128)(2,1)}, bf16[3,6,256,32]{2,3,1,0:T(8,128)(2,1)}, u32[]{:S(2)}, u32[]{:S(2)}) collective-permute-start(bf16[3,6,256,32]{2,3,1,0:T(8,128)(2,1)} %collective-permute-done.5), channel_id=1, source_target_pairs={{0,128},{1,129},{2,130},{3,131},{4,132},{5,133},{6,134},{7,135},{8... | collective-permute-start | bytes 884744 | tf_op jit(solution)/shard_map/ppermute | solution.py:82
  114.0 1.5 pad_maximum_fusion.2
  115.5 3.3 %gather_fusion.2 = f32[108,256,32]{1,2,0:T(8,128)} fusion(f32[9,6,256,32]{2,3,1,0:T(8,128)S(1)} %pad_maximum_fusion.2, s32[108]{0:T(128)S(1)} %reshape.68), kind=kCustom, calls=%fused_computation.4 | custom fusion | bytes 7078752 | tf_op jit(solution)/shard_map/gather | solution.py:75
  118.8 15.5 %gather.20 = f32[3,6,6,4,2,32,32]{5,4,3,6,2,1,0:T(2,128)} reshape(f32[108,256,32]{1,2,0:T(8,128)} %gather_fusion.2) | data formatting | bytes 7077888 | tf_op jit(solution)/shard_map/gather | solution.py:75
  134.3 5.8 %fusion.31 = (bf16[3,6,256,32]{2,3,1,0:T(8,128)(2,1)}, f32[3,6,256,32]{2,3,1,0:T(8,128)}) fusion(f32[3,6,256,256]{3,2,1,0:T(8,128)} %param.4, f32[3,6,6,256,32]{3,4,2,1,0:T(8,128)S(1)} %bitcast.116, f32[3,6,6]{1,2,0:T(8,128)S(1)} %copy.65), kind=kOutput, calls=%fused_computation.66 | convolution fusion | flops 1359986688 | bytes 9142704 | tf_op jit(solution)/shard_map/rsac,rstcb->rtab/dot_general | solution.py:76
  140.1 4.4 %collective-permute-start.9 = (bf16[3,6,256,32]{2,3,1,0:T(8,128)(2,1)}, bf16[3,6,256,32]{2,3,1,0:T(8,128)(2,1)}, u32[]{:S(2)}, u32[]{:S(2)}) collective-permute-start(bf16[3,6,256,32]{2,3,1,0:T(8,128)(2,1)} %get-tuple-element.23), channel_id=1, source_target_pairs={{0,128},{1,129},{2,130},{3,131},{4,132},{5,133},{6,134},{7,135},{8... | collective-permute-start | bytes 884744 | tf_op jit(solution)/shard_map/ppermute | solution.py:82
  144.5 2.5 %collective-permute-start.8 = (bf16[3,6,256,32]{2,3,1,0:T(8,128)(2,1)}, bf16[3,6,256,32]{2,3,1,0:T(8,128)(2,1)S(1)}, u32[]{:S(2)}, u32[]{:S(2)}) collective-permute-start(bf16[3,6,256,32]{2,3,1,0:T(8,128)(2,1)} %get-tuple-element.23), channel_id=1, source_target_pairs={{0,256},{256,0},{512,768},{768,512},{1,257},{257,1},{513,769},{769... | collective-permute-start | bytes 884744 | tf_op jit(solution)/shard_map/ppermute | solution.py:78
  147.0 20.0 %copy.70 = f32[3,6,6,4,2,32,32]{6,5,3,2,1,0,4:T(8,128)} copy(f32[3,6,6,4,2,32,32]{5,4,3,6,2,1,0:T(2,128)} %gather.20) | data formatting | bytes 7077888 | tf_op jit(solution)/shard_map/gather | solution.py:75
  167.0 10.6 %broadcast_multiply_fusion.1 = (f32[3,6,6,4,2,32,32]{6,5,3,2,1,0,4:T(8,128)S(1)}, f32[3,6,6,4,2,32,32]{6,5,3,2,1,0,4:T(8,128)S(1)}) fusion(f32[3,6,6,4,2,32,32]{6,5,3,2,1,0,4:T(8,128)} %copy.69, f32[3,6,6]{2,1,0:T(8,128)S(1)} %copy-done.12, f32[3,6,6,4,2,32,32]{6,5,3,2,1,0,4:T(8,128)} %copy.70), kind=kLoop, calls=%fused_computation.10 | loop fusion | flops 1769472 | bytes 14156208 | tf_op jit(solution)/shard_map/mul | solution.py:75
  177.5 1.9 collective-permute-start.7
  179.5 7.0 %reduce-precision_convert_fusion = (bf16[3,6,6,4,2,32,64]{6,5,3,2,1,0,4:T(8,128)(2,1)}, bf16[3,6,6,4,2,32,64]{6,5,3,2,1,0,4:T(8,128)(2,1)}) fusion(f32[3,6,6,4,2,32,32]{6,5,3,2,1,0,4:T(8,128)S(1)} %get-tuple-element.18, f32[3,6,6,4,2,32,32]{6,5,3,2,1,0,4:T(8,128)S(1)} %get-tuple-element.17), kind=kLoop, calls=%fused_computation.6 | loop fusion | flops 8847360 | bytes 14155776 | tf_op jit(solution)/shard_map/convert_element_type | solution.py:91
  186.4 5.7 %collective-permute-start.10 = (bf16[3,6,256,32]{2,3,1,0:T(8,128)(2,1)}, bf16[3,6,256,32]{2,3,1,0:T(8,128)(2,1)S(1)}, u32[]{:S(2)}, u32[]{:S(2)}) collective-permute-start(bf16[3,6,256,32]{2,3,1,0:T(8,128)(2,1)} %collective-permute-done.9), channel_id=1, source_target_pairs={{0,128},{1,129},{2,130},{3,131},{4,132},{5,133},{6,134},{7,135},{8... | collective-permute-start | bytes 884744 | tf_op jit(solution)/shard_map/ppermute | solution.py:82
  192.2 9.1 %fusion.29 = (bf16[3,6,6,4,1,32,64]{6,5,3,2,1,0,4:T(8,128)(2,1)}, bf16[3,6,6,4,1,32,64]{6,5,3,2,1,0,4:T(8,128)(2,1)}) fusion(bf16[3,6,6,4,2,32,64]{6,5,3,2,1,0,4:T(8,128)(2,1)} %get-tuple-element.10), kind=kLoop, calls=%fused_computation.64 | loop fusion | bytes 7077888 | tf_op jit(solution)/shard_map/slice | solution.py:99
  201.3 2.1 collective-permute-start.11
  203.5 4.7 %fusion.28 = (bf16[3,6,6,4,1,32,64]{6,5,3,2,1,0,4:T(8,128)(2,1)}, bf16[3,6,6,4,1,32,64]{6,5,3,2,1,0,4:T(8,128)(2,1)}) fusion(bf16[3,6,6,4,2,32,64]{6,5,3,2,1,0,4:T(8,128)(2,1)S(1)} %bitcast.118), kind=kLoop, calls=%fused_computation.63 | loop fusion | bytes 7077888 | tf_op jit(solution)/shard_map/slice | solution.py:98
  214.8 1.8 copy-done.5
  222.9 2.3 %fusion.11 = f32[3,6,256,64]{2,3,1,0:T(8,128)} fusion(f32[3,6,64,256]{3,2,1,0:T(8,128)S(1)} %fusion.12, f32[3,6,64,256]{3,2,1,0:T(8,128)S(1)} %convolution_bitcast_fusion.2, bf16[3,6,6,128,64]{4,3,2,1,0:T(8,128)(2,1)S(1)} %bitcast.119, bf16[3,6,256,128,1]{2,3,4,1,0:T(8,128)(2,1)S(1)} %bitcast.124, f32[3,6,256,64]{2,3,1,0:T(8,128)S(1)} %copy-done.6), kind=kOutput, calls=%fused_computation.29 | convolution fusion | flops 454459392 | bytes 7667712 | tf_op jit(solution)/shard_map/rsac,rstcb->rtab/dot_general | solution.py:100
  (76 shorter events, 18.6 us)
Async XLA Ops:
  5.7 21.4 %copy-start.13 = (s32[768,6]{0,1:T(8,128)S(1)}, s32[768,6]{0,1:T(8,128)}, u32[]{:S(2)}) copy-start(s32[768,6]{0,1:T(8,128)} %param.5) | copy-start | bytes 55300
  8.0 29.2 %collective-permute-start.1 = (f32[3,6,256,32]{2,3,1,0:T(8,128)S(1)}, f32[3,6,256,32]{2,3,1,0:T(8,128)}, u32[]{:S(2)}, u32[]{:S(2)}) collective-permute-start(f32[3,6,256,32]{2,3,1,0:T(8,128)S(1)} %copy.109), channel_id=1, source_target_pairs={{1,0},{2,1},{3,2},{4,3},{5,4},{6,5},{7,6},{8,7},{9,8},{10,9},{11,1... | collective-permute-start | bytes 1769480 | tf_op jit(solution)/shard_map/ppermute | solution.py:17
  25.2 21.9 %collective-permute-start = (f32[3,6,256,32]{2,3,1,0:T(8,128)S(1)}, f32[3,6,256,32]{2,3,1,0:T(8,128)}, u32[]{:S(2)}, u32[]{:S(2)}) collective-permute-start(f32[3,6,256,32]{2,3,1,0:T(8,128)S(1)} %copy.109), channel_id=1, source_target_pairs={{0,1},{1,2},{2,3},{3,4},{4,5},{5,6},{6,7},{7,8},{8,9},{9,10},{10,1... | collective-permute-start | bytes 1769480 | tf_op jit(solution)/shard_map/ppermute | solution.py:16
  31.9 16.7 %copy-start.11 = (f32[3,6,6]{2,1,0:T(8,128)}, f32[3,6,6]{2,1,0:T(8,128)S(1)}, u32[]{:S(2)}) copy-start(f32[3,6,6]{2,1,0:T(8,128)S(1)} %convert_element_type.25) | copy-start | bytes 1300
  48.6 65.4 %collective-permute-start.3 = (f32[3,6,256,32]{2,3,1,0:T(8,128)}, f32[3,6,256,32]{2,3,1,0:T(8,128)}, u32[]{:S(2)}, u32[]{:S(2)}) collective-permute-start(f32[3,6,256,32]{2,3,1,0:T(8,128)} %copy.110), channel_id=1, source_target_pairs={{1,0},{2,1},{3,2},{4,3},{5,4},{6,5},{7,6},{8,7},{9,8},{10,9},{11,1... | collective-permute-start | bytes 1769480 | tf_op jit(solution)/shard_map/ppermute | solution.py:17
  50.5 63.5 %collective-permute-start.2 = (f32[3,6,256,32]{2,3,1,0:T(8,128)}, f32[3,6,256,32]{2,3,1,0:T(8,128)}, u32[]{:S(2)}, u32[]{:S(2)}) collective-permute-start(f32[3,6,256,32]{2,3,1,0:T(8,128)} %copy.110), channel_id=1, source_target_pairs={{0,1},{1,2},{2,3},{3,4},{4,5},{5,6},{6,7},{7,8},{8,9},{9,10},{10,1... | collective-permute-start | bytes 1769480 | tf_op jit(solution)/shard_map/ppermute | solution.py:16
  57.1 13.4 %copy-start = (f32[108,256,32]{1,2,0:T(8,128)S(1)}, f32[108,256,32]{1,2,0:T(8,128)}, u32[]{:S(2)}) copy-start(f32[108,256,32]{1,2,0:T(8,128)} %gather_fusion.1) | copy-start | bytes 10616836
  64.1 41.2 %collective-permute-start.5 = (bf16[3,6,256,32]{2,3,1,0:T(8,128)(2,1)}, bf16[3,6,256,32]{2,3,1,0:T(8,128)(2,1)}, u32[]{:S(2)}, u32[]{:S(2)}) collective-permute-start(bf16[3,6,256,32]{2,3,1,0:T(8,128)(2,1)} %get-tuple-element.21), channel_id=1, source_target_pairs={{0,128},{1,129},{2,130},{3,131},{4,132},{5,133},{6,134},{7,135},{8... | collective-permute-start | bytes 884744 | tf_op jit(solution)/shard_map/ppermute | solution.py:82
  83.3 126.0 %collective-permute-start.4 = (bf16[3,6,256,32]{2,3,1,0:T(8,128)(2,1)}, bf16[3,6,256,32]{2,3,1,0:T(8,128)(2,1)}, u32[]{:S(2)}, u32[]{:S(2)}) collective-permute-start(bf16[3,6,256,32]{2,3,1,0:T(8,128)(2,1)} %get-tuple-element.21), channel_id=1, source_target_pairs={{0,256},{256,0},{512,768},{768,512},{1,257},{257,1},{513,769},{769... | collective-permute-start | bytes 884744 | tf_op jit(solution)/shard_map/ppermute | solution.py:78
  105.3 72.3 %collective-permute-start.6 = (bf16[3,6,256,32]{2,3,1,0:T(8,128)(2,1)}, bf16[3,6,256,32]{2,3,1,0:T(8,128)(2,1)}, u32[]{:S(2)}, u32[]{:S(2)}) collective-permute-start(bf16[3,6,256,32]{2,3,1,0:T(8,128)(2,1)} %collective-permute-done.5), channel_id=1, source_target_pairs={{0,128},{1,129},{2,130},{3,131},{4,132},{5,133},{6,134},{7,135},{8... | collective-permute-start | bytes 884744 | tf_op jit(solution)/shard_map/ppermute | solution.py:82
  118.8 15.5 %copy-start.1 = (f32[108,256,32]{1,2,0:T(8,128)S(1)}, f32[108,256,32]{1,2,0:T(8,128)}, u32[]{:S(2)}) copy-start(f32[108,256,32]{1,2,0:T(8,128)} %gather_fusion.2) | copy-start | bytes 10616836
  140.1 26.9 %copy-start.12 = (f32[3,6,6]{2,1,0:T(8,128)S(1)}, f32[3,6,6]{2,1,0:T(8,128)}, u32[]{:S(2)}) copy-start(f32[3,6,6]{2,1,0:T(8,128)} %copy-done.11) | copy-start | bytes 1300
  140.1 46.4 %collective-permute-start.9 = (bf16[3,6,256,32]{2,3,1,0:T(8,128)(2,1)}, bf16[3,6,256,32]{2,3,1,0:T(8,128)(2,1)}, u32[]{:S(2)}, u32[]{:S(2)}) collective-permute-start(bf16[3,6,256,32]{2,3,1,0:T(8,128)(2,1)} %get-tuple-element.23), channel_id=1, source_target_pairs={{0,128},{1,129},{2,130},{3,131},{4,132},{5,133},{6,134},{7,135},{8... | collective-permute-start | bytes 884744 | tf_op jit(solution)/shard_map/ppermute | solution.py:82
  144.5 66.9 %collective-permute-start.8 = (bf16[3,6,256,32]{2,3,1,0:T(8,128)(2,1)}, bf16[3,6,256,32]{2,3,1,0:T(8,128)(2,1)S(1)}, u32[]{:S(2)}, u32[]{:S(2)}) collective-permute-start(bf16[3,6,256,32]{2,3,1,0:T(8,128)(2,1)} %get-tuple-element.23), channel_id=1, source_target_pairs={{0,256},{256,0},{512,768},{768,512},{1,257},{257,1},{513,769},{769... | collective-permute-start | bytes 884744 | tf_op jit(solution)/shard_map/ppermute | solution.py:78
  177.5 31.8 %collective-permute-start.7 = (bf16[3,6,256,32]{2,3,1,0:T(8,128)(2,1)}, bf16[3,6,256,32]{2,3,1,0:T(8,128)(2,1)S(1)}, u32[]{:S(2)}, u32[]{:S(2)}) collective-permute-start(bf16[3,6,256,32]{2,3,1,0:T(8,128)(2,1)} %collective-permute-done.6), channel_id=1, source_target_pairs={{0,256},{256,0},{512,768},{768,512},{1,257},{257,1},{513,769},{769... | collective-permute-start | bytes 884744 | tf_op jit(solution)/shard_map/ppermute | solution.py:83
  186.4 14.9 %collective-permute-start.10 = (bf16[3,6,256,32]{2,3,1,0:T(8,128)(2,1)}, bf16[3,6,256,32]{2,3,1,0:T(8,128)(2,1)S(1)}, u32[]{:S(2)}, u32[]{:S(2)}) collective-permute-start(bf16[3,6,256,32]{2,3,1,0:T(8,128)(2,1)} %collective-permute-done.9), channel_id=1, source_target_pairs={{0,128},{1,129},{2,130},{3,131},{4,132},{5,133},{6,134},{7,135},{8... | collective-permute-start | bytes 884744 | tf_op jit(solution)/shard_map/ppermute | solution.py:82
  192.2 11.3 %slice-start = ((s8[7077888]{0:T(1024)(128)(4,1)}), s8[4194304]{0:T(1024)(128)(4,1)S(1)}, s32[]{:S(2)}) async-start(s8[7077888]{0:T(1024)(128)(4,1)} %bitcast.117), calls=%async_computation | async-start | bytes 8388608
  192.2 11.3 %slice-start.1 = ((s8[7077888]{0:T(1024)(128)(4,1)}), s8[2883584]{0:T(1024)(128)(4,1)S(1)}, s32[]{:S(2)}) async-start(s8[7077888]{0:T(1024)(128)(4,1)} %bitcast.117), calls=%async_computation.1 | async-start | bytes 5767168
  201.3 6.9 %copy-start.10 = (bf16[3,6,256,32]{2,3,1,0:T(8,128)(2,1)}, bf16[3,6,256,32]{2,3,1,0:T(8,128)(2,1)S(1)}, u32[]{:S(2)}) copy-start(bf16[3,6,256,32]{2,3,1,0:T(8,128)(2,1)S(1)} %collective-permute-done.10) | copy-start | bytes 884740
  201.3 10.1 %collective-permute-start.11 = (bf16[3,6,256,32]{2,3,1,0:T(8,128)(2,1)S(1)}, bf16[3,6,256,32]{2,3,1,0:T(8,128)(2,1)}, u32[]{:S(2)}, u32[]{:S(2)}) collective-permute-start(bf16[3,6,256,32]{2,3,1,0:T(8,128)(2,1)S(1)} %collective-permute-done.10), channel_id=1, source_target_pairs={{0,256},{256,0},{512,768},{768,512},{1,257},{257,1},{513,769},{769... | collective-permute-start | bytes 884744 | tf_op jit(solution)/shard_map/ppermute | solution.py:83
  203.5 4.7 %copy-start.7 = (f32[3,6,256,32]{2,3,1,0:T(8,128)S(1)}, f32[3,6,256,32]{2,3,1,0:T(8,128)}, u32[]{:S(2)}) copy-start(f32[3,6,256,32]{2,3,1,0:T(8,128)} %get-tuple-element.22) | copy-start | bytes 1769476
  203.5 4.7 %copy-start.8 = (f32[3,6,256,32]{2,3,1,0:T(8,128)S(1)}, f32[3,6,256,32]{2,3,1,0:T(8,128)}, u32[]{:S(2)}) copy-start(f32[3,6,256,32]{2,3,1,0:T(8,128)} %get-tuple-element.24) | copy-start | bytes 1769476
  211.4 0.7 copy-start.9
  213.5 0.8 copy-start.14
  214.5 2.0 copy-start.5
  216.5 2.0 copy-start.3
  218.5 2.0 copy-start.4
  220.5 2.0 copy-start.2
  220.5 2.3 %copy-start.6 = (f32[3,6,256,64]{2,3,1,0:T(8,128)S(1)}, f32[3,6,256,64]{2,3,1,0:T(8,128)}, u32[]{:S(2)}) copy-start(f32[3,6,256,64]{2,3,1,0:T(8,128)} %pad_maximum_fusion.3) | copy-start | bytes 3538948

commit v5 on v3

--- a/solution.py
+++ b/solution.py
@@ -1,4 +1,5 @@
 import jax
+import numpy as np
 import jax.numpy as jnp
 from jax import lax
 from jax.sharding import PartitionSpec as P
@@ -61,9 +62,34 @@
         offset = (own - row_ids[:, None] + BAND) % total_rows - BAND
         place = jnp.arange(count_rows, dtype=jnp.int32)[:, None] + BAND + offset
         col_part = lax.dynamic_slice_in_dim(density, start_col, width, 3)
+        m_ids = jnp.arange(count_rows, dtype=jnp.int32)
+        groups = []
+        for near in (True, False):
+            lists = [[d for d in range(-BAND, BAND + 1) if (0 <= m + d < count_rows) == near] for m in range(count_rows)]
+            size = max(len(ds) for ds in lists)
+            offs = np.array([ds + [0] * (size - len(ds)) for ds in lists], np.int32)
+            real = np.array([[1] * len(ds) + [0] * (size - len(ds)) for ds in lists], bool)
+            groups.append((near, jnp.asarray(offs), jnp.asarray(real)))
+
+        def offset_terms(near, offs, real, source):
+            target = (row_ids[:, None] + offs) % total_rows
+            hit = own[:, None, :] == target[:, :, None]
+            present = jnp.logical_and(jnp.any(hit, axis=2), real)
+            where_s = jnp.argmax(hit.astype(jnp.int32), axis=2)
+            left = density[m_ids[:, None], where_s] * present[:, :, None, None].astype(jnp.float32)
+            rows_of = pattern[target]
+            match = rows_of[:, :, None, :] == own[:, None, :, None]
+            use = jnp.logical_and(jnp.any(match, axis=3), present[:, :, None])
+            where_u = jnp.argmax(match.astype(jnp.int32), axis=3)
+            local = m_ids[:, None] + offs
+            at = jnp.clip(local, 0, count_rows - 1) if near else local + BAND
+            block = source[at[:, :, None], where_u] * use[:, :, :, None, None].astype(jnp.float32)
+            return jnp.einsum("rsac,rstcb->rtab", left, block, precision=lax.Precision.HIGH)
+
+        near_terms = offset_terms(groups[0][0], groups[0][1], groups[0][2], col_part)
         padded = padded_2(col_part, (("blk", 0),), BAND)
+        squared = near_terms + offset_terms(groups[1][0], groups[1][1], groups[1][2], padded)
         picked = padded[place[:, :, None], slot] * valid[:, :, :, None, None]
-        squared = jnp.einsum("rsac,rstcb->rtab", density, picked, precision=lax.Precision.HIGH)
         rounded = squared.astype(jnp.bfloat16)
         top = lax.reduce_precision(picked, exponent_bits=8, mantissa_bits=7)
         high = top.astype(jnp.bfloat16)

time: 118 us -> 141 us (1.19)
  local copies, waits for them, and re-layouts: 10.8 us -> 35 us
  other arithmetic: 8.59 us -> 24.2 us
  waiting for transfers between devices: 28.1 us -> 14.2 us
  starting transfers between devices: 47.5 us -> 39.9 us
  matrix products: 21.9 us -> 25.1 us
    gather x0 -> x8, local copies, waits for them, and re-layouts: none -> 15.5 us  [the longest x2 7.86 us: offset_terms(): density[m_ids[:, None], where_s]]
    ppermute x1, waiting for transfers between devices: 13 us -> 0.01 us  [padded_2(): before = lax.ppermute(last, axis, up)]
    ppermute x1, starting transfers between devices: 9.23 us -> 2.85 us  [body(): mate = lax.ppermute(rounded, 'layer', across)]
    another operation x0 -> x4, other arithmetic: none -> 4.06 us  [the longest x2 2.44 us: offset_terms(): where_u = jnp.argmax(match.astype(jnp.int32), axis=3)]
    convert_element_type x0 -> x4, other arithmetic: none -> 3.65 us  [the longest x2 1.88 us: offset_terms(): use[:, :, :, None, None].astype(jnp.float32)]
    dot_general x1 -> x2, matrix products: 8.78 us -> 12 us  [offset_terms(): jnp.einsum('rsac,rstcb->rtab', left, block, precision=lax.Precision.HIGH)]
    gather x2, local copies, waits for them, and re-layouts: 0.57 us -> 3.57 us  [body(): neighbor = pattern[own]]
    concatenate x0 -> x5, other arithmetic: none -> 2.63 us  [the longest x3 2.02 us: offset_terms(): source[at[:, :, None], where_u]]
  transfers between devices with their start and end apart: 6 -> 6, of which waited for: 3 -> 2; matrix products, arithmetic and copies ran while one was open for 13% -> 45% of each run, Pallas kernels for 0% -> 0%
where the time goes in v5:
time: 141 us; the launch traced here: 139 us
  starting transfers between devices  39.9 us (28%)
  local copies, waits for them, and re-layouts  35 us (25%)
  matrix products  25.1 us (18%)
  other arithmetic  24.2 us (17%)
  waiting for transfers between devices  14.2 us (10%)
    ppermute x1, starting transfers between devices, padded_2(): after = lax.ppermute(initial, axis, down)  17.2 us
    ppermute x1, waiting for transfers between devices, body(): far = lax.ppermute(halfway, ('layer', 'blk'), relay)  12.3 us
    dot_general x2, matrix products, offset_terms(): jnp.einsum('rsac,rstcb->rtab', left, block, precision=lax.Precision.HIGH)  12 us
    gather x2, local copies, waits for them, and re-layouts, offset_terms(): density[m_ids[:, None], where_s]  7.86 us
    ppermute x1, starting transfers between devices, body(): halfway = lax.ppermute(rounded, ('layer', 'blk'), relay)  7.21 us
    ppermute x1, starting transfers between devices, body(): far = lax.ppermute(halfway, ('layer', 'blk'), relay)  6.78 us
    dot_general x2, matrix products, cubed_part(): jnp.einsum('rsac,rstcb->rtab', left, rows, preferred_element_type=jnp.flo...  6.77 us
    gather x2, local copies, waits for them, and re-layouts, offset_terms(): source[at[:, :, None], where_u]  6.49 us
  transfers between devices with their start and end apart: 6, of which 2 were waited for; matrix products, arithmetic and copies ran while one was open for 45% of the time, Pallas kernels for 0%

profile of v5, /device:TPU:1, one launch (start us, length us, event | category | flops | bytes accessed | tf_op | source)
XLA Modules:
  0.0 139.5 jit_solution(9012819765507367256)
XLA Ops:
  0.6 2.3 %constant_dynamic-slice_fusion.1 = f32[3,6,256,64]{3,2,1,0:T(8,128)S(1)} fusion(f32[3,6,256,256]{3,2,1,0:T(8,128)} %param.6, s32[]{:T(128)S(6)} %select_n.114), kind=kLoop, calls=%fused_computation.121 | loop fusion | bytes 2359300 | tf_op jit(solution)/shard_map/dynamic_slice | solution.py:64
  3.9 17.2 %collective-permute-start.1 = (f32[3,6,256,64]{2,3,1,0:T(8,128)S(1)}, f32[3,6,256,64]{2,3,1,0:T(8,128)}, u32[]{:S(2)}, u32[]{:S(2)}) collective-permute-start(f32[3,6,256,64]{2,3,1,0:T(8,128)S(1)} %copy.109), channel_id=1, source_target_pairs={{1,0},{2,1},{3,2},{4,3},{5,4},{6,5},{7,6},{8,7},{9,8},{10,9},{11,1... | collective-permute-start | bytes 3538952 | tf_op jit(solution)/shard_map/ppermute | solution.py:18
  21.1 1.9 %collective-permute-start = (f32[3,6,256,64]{2,3,1,0:T(8,128)S(1)}, f32[3,6,256,64]{2,3,1,0:T(8,128)}, u32[]{:S(2)}, u32[]{:S(2)}) collective-permute-start(f32[3,6,256,64]{2,3,1,0:T(8,128)S(1)} %copy.109), channel_id=1, source_target_pairs={{0,1},{1,2},{2,3},{3,4},{4,5},{5,6},{6,7},{7,8},{8,9},{9,10},{10,1... | collective-permute-start | bytes 3538952 | tf_op jit(solution)/shard_map/ppermute | solution.py:17
  24.1 1.4 %fusion.89 = (s32[3,6]{0,1:T(8,128)}, s32[3,6]{0,1:T(8,128)S(1)}) fusion(s32[3]{0:T(128)S(1)} %get-tuple-element.27, s32[3]{0:T(128)S(1)} %get-tuple-element.26, s32[768,6]{0,1:T(8,128)} %param.7, s32[]{:T(128)S(6)} %select_n.118), kind=kLoop, calls=%fused_computation.93 | loop fusion | flops 270 | bytes 244 | tf_op jit(solution)/shard_map/concatenate | solution.py:92
  31.6 1.4 fusion.72
  33.3 1.3 fusion.85
  37.2 3.0 %gather_fusion.2 = f32[9,256,256]{2,1,0:T(8,128)S(1)} fusion(f32[3,6,256,256]{3,2,1,0:T(8,128)} %param.6, s32[9]{0:T(128)S(1)} %reshape.70), kind=kCustom, calls=%fused_computation.2 | custom fusion | bytes 4718664 | tf_op jit(solution)/shard_map/gather | solution.py:79
  41.0 2.8 %gather_fusion.1 = f32[54,256,64]{1,2,0:T(8,128)} fusion(f32[3,6,256,64]{2,3,1,0:T(8,128)S(1)} %copy.109, s32[54]{0:T(128)S(1)} %reshape.64), kind=kCustom, calls=%fused_computation.1 | custom fusion | bytes 7078320 | tf_op jit(solution)/shard_map/gather | solution.py:86
  43.8 1.4 copy.69
  45.9 4.8 %gather_fusion.5 = f32[12,256,256]{2,1,0:T(8,128)} fusion(f32[3,6,256,256]{3,2,1,0:T(8,128)} %param.6, s32[12]{0:T(128)S(1)} %reshape.90), kind=kCustom, calls=%fused_computation.5 | custom fusion | bytes 6291552 | tf_op jit(solution)/shard_map/gather | solution.py:79
  52.7 2.3 %gather_fusion.6 = s32[18,6]{1,0:T(8,128)} fusion(s32[768,6]{1,0:T(8,128)} %copy-done.4, s32[1024]{0:T(1024)} %pad_clamp_fusion), kind=kCustom, calls=%fused_computation.6 | custom fusion | bytes 936 | tf_op jit(solution)/shard_map/gather | solution.py:57
  55.0 1.3 reshape.153
  56.3 1.3 copy.76
  58.1 1.2 and_convert_fusion
  59.3 2.0 %fusion.71 = (s32[3,6,6]{2,1,0:T(8,128)}, s32[3,6,6]{2,1,0:T(8,128)S(1)}) fusion(s32[3,6]{1,0:T(4,128)S(1)} %copy.67, s32[3,6,6]{2,1,0:T(8,128)} %reshape.153), kind=kLoop, calls=%fused_computation.54 | loop fusion | flops 5076 | bytes 1368 | tf_op jit(solution)/shard_map/make_body.<locals>.body/reduce | solution.py:59
  61.3 1.3 fusion.79
  62.7 4.9 %fusion.33 = f32[3,6,64,256]{3,2,1,0:T(8,128)} fusion(f32[3,3,256,256]{3,2,1,0:T(8,128)S(1)} %bitcast.121, f32[3,3,6,256,64]{3,4,2,1,0:T(8,128)} %bitcast.119, f32[3,3,6]{1,2,0:T(8,128)} %copy.69, f32[3,3]{1,0:T(4,128)} %convert_element_type.58), kind=kOutput, calls=%fused_computation.37 | convolution fusion | flops 1360429056 | bytes 7078140 | tf_op jit(solution)/shard_map/rsac,rstcb->rtab/dot_general | solution.py:87
  67.6 1.9 %pad_maximum_fusion = f32[9,6,256,64]{2,3,1,0:T(8,128)S(1)} fusion(f32[3,6,256,64]{2,3,1,0:T(8,128)} %collective-permute-done.1, f32[3,6,256,64]{2,3,1,0:T(8,128)S(1)} %copy-done.1, f32[3,6,256,64]{2,3,1,0:T(8,128)} %collective-permute-done), kind=kLoop, calls=%fused_computation.14 | loop fusion | flops 1769472 | bytes 7077888 | tf_op jit(solution)/shard_map/concatenate | solution.py:19
  69.5 3.7 %gather_fusion.4 = f32[72,256,64]{1,2,0:T(8,128)} fusion(f32[9,6,256,64]{2,3,1,0:T(8,128)S(1)} %pad_maximum_fusion, s32[72]{0:T(128)S(1)} %reshape.84), kind=kCustom, calls=%fused_computation.4 | custom fusion | bytes 9437760 | tf_op jit(solution)/shard_map/gather | solution.py:86
  73.2 7.1 %fusion.112 = (bf16[3,6,256,64]{2,3,1,0:T(8,128)(2,1)}, f32[3,6,256,64]{2,3,1,0:T(8,128)}) fusion(f32[3,6,64,256]{3,2,1,0:T(8,128)} %fusion.33, f32[3,4,256,256]{3,2,1,0:T(8,128)} %bitcast.120, f32[3,4]{1,0:T(4,128)S(1)} %copy-done.6, f32[3,4,6,256,64]{3,4,2,1,0:T(8,128)} %bitcast.118, f32[3,4,6]{1,2,0:T(8,128)} %and_convert_fusion), kind=kOutput, calls=%fused_computation.128 | convolution fusion | flops 1814495232 | bytes 10813776 | tf_op jit(solution)/shard_map/rsac,rstcb->rtab/dot_general | solution.py:87
  80.3 2.9 %collective-permute-start.3 = (bf16[3,6,256,64]{2,3,1,0:T(8,128)(2,1)}, bf16[3,6,256,64]{2,3,1,0:T(8,128)(2,1)}, u32[]{:S(2)}, u32[]{:S(2)}) collective-permute-start(bf16[3,6,256,64]{2,3,1,0:T(8,128)(2,1)} %get-tuple-element.24), channel_id=1, source_target_pairs={{0,256},{256,0},{512,768},{768,512},{1,257},{257,1},{513,769},{769... | collective-permute-start | bytes 1769480 | tf_op jit(solution)/shard_map/ppermute | solution.py:106
  85.8 7.2 %collective-permute-start.2 = (bf16[3,6,256,64]{2,3,1,0:T(8,128)(2,1)}, bf16[3,6,256,64]{2,3,1,0:T(8,128)(2,1)}, u32[]{:S(2)}, u32[]{:S(2)}) collective-permute-start(bf16[3,6,256,64]{2,3,1,0:T(8,128)(2,1)} %get-tuple-element.24), channel_id=1, source_target_pairs={{0,128},{1,129},{2,130},{3,131},{4,132},{5,133},{6,134},{7,135},{8... | collective-permute-start | bytes 1769480 | tf_op jit(solution)/shard_map/ppermute | solution.py:113
  93.1 4.5 %gather_fusion.7 = f32[108,256,64]{1,2,0:T(8,128)} fusion(f32[9,6,256,64]{2,3,1,0:T(8,128)S(1)} %pad_maximum_fusion, s32[108]{0:T(128)S(1)} %reshape.104), kind=kCustom, calls=%fused_computation.7 | custom fusion | bytes 14156640 | tf_op jit(solution)/shard_map/gather | solution.py:92
  97.5 3.7 %reduce-precision_convert_fusion = (bf16[3,6,6,256,64]{3,4,1,2,0:T(8,128)(2,1)S(1)}, bf16[3,6,6,256,64]{3,4,1,2,0:T(8,128)(2,1)S(1)}) fusion(f32[3,6,6,256,64]{3,4,2,1,0:T(8,128)} %bitcast.117, f32[3,6,6]{1,2,0:T(8,128)S(1)} %copy.82), kind=kLoop, calls=%fused_computation.9 | loop fusion | flops 8847360 | bytes 14156208 | tf_op jit(solution)/shard_map/convert_element_type | solution.py:95
  101.3 3.5 %fusion.24 = f32[3,6,64,256]{3,2,1,0:T(8,128)S(1)} fusion(bf16[3,6,6,256,64]{3,4,1,2,0:T(8,128)(2,1)S(1)} %get-tuple-element.23, s32[]{:T(128)S(6)} %select_n.131, bf16[3,6,256,64]{2,3,1,0:T(8,128)(2,1)} %collective-permute-done.3, bf16[3,6,256,64]{2,3,1,0:T(8,128)(2,1)} %get-tuple-element.24, pred[]{:T(512)S(6)} %eq.101), kind=kOutput, calls=%fused_computation.34 | convolution fusion | flops 458293248 | bytes 4128773 | tf_op jit(solution)/shard_map/rsac,rstcb->rtab/dot_general | solution.py:102
  104.8 3.3 %fusion.57 = f32[3,6,256,64]{2,3,1,0:T(8,128)} fusion(f32[3,6,64,256]{3,2,1,0:T(8,128)S(1)} %fusion.24, bf16[3,6,6,256,64]{3,4,1,2,0:T(8,128)(2,1)S(1)} %get-tuple-element.22, s32[]{:T(128)S(6)} %select_n.131, bf16[3,6,256,64]{2,3,1,0:T(8,128)(2,1)} %collective-permute-done.3, bf16[3,6,256,64]{2,3,1,0:T(8,128)(2,1)} %get-tuple-element.24, pred[]{:T(512)S(6)} %eq.101), kind=kOutput, calls=%fused_computation.45 | convolution fusion | flops 458588160 | bytes 5308421 | tf_op jit(solution)/shard_map/rsac,rstcb->rtab/dot_general | solution.py:101
  108.1 6.8 %collective-permute-start.4 = (bf16[3,6,256,64]{2,3,1,0:T(8,128)(2,1)}, bf16[3,6,256,64]{2,3,1,0:T(8,128)(2,1)}, u32[]{:S(2)}, u32[]{:S(2)}) collective-permute-start(bf16[3,6,256,64]{2,3,1,0:T(8,128)(2,1)} %collective-permute-done.2), channel_id=1, source_target_pairs={{0,128},{1,129},{2,130},{3,131},{4,132},{5,133},{6,134},{7,135},{8... | collective-permute-start | bytes 1769480 | tf_op jit(solution)/shard_map/ppermute | solution.py:115
  114.9 12.3 %collective-permute-done.4 = bf16[3,6,256,64]{2,3,1,0:T(8,128)(2,1)} collective-permute-done((bf16[3,6,256,64]{2,3,1,0:T(8,128)(2,1)}, bf16[3,6,256,64]{2,3,1,0:T(8,128)(2,1)}, u32[]{:S(2)}, u32[]{:S(2)}) %collective-permute-start.4) | collective-permute-done | bytes 589856 | tf_op jit(solution)/shard_map/ppermute | solution.py:115
  127.2 4.0 %collective-permute-start.5 = (bf16[3,6,256,64]{2,3,1,0:T(8,128)(2,1)}, bf16[3,6,256,64]{2,3,1,0:T(8,128)(2,1)}, u32[]{:S(2)}, u32[]{:S(2)}) collective-permute-start(bf16[3,6,256,64]{2,3,1,0:T(8,128)(2,1)} %collective-permute-done.4), channel_id=1, source_target_pairs={{0,256},{256,0},{512,768},{768,512},{1,257},{257,1},{513,769},{769... | collective-permute-start | bytes 1769480 | tf_op jit(solution)/shard_map/ppermute | solution.py:116
  131.3 1.9 %collective-permute-done.5 = bf16[3,6,256,64]{2,3,1,0:T(8,128)(2,1)} collective-permute-done((bf16[3,6,256,64]{2,3,1,0:T(8,128)(2,1)}, bf16[3,6,256,64]{2,3,1,0:T(8,128)(2,1)}, u32[]{:S(2)}, u32[]{:S(2)}) %collective-permute-start.5) | collective-permute-done | bytes 589856 | tf_op jit(solution)/shard_map/ppermute | solution.py:116
  133.2 2.8 %fusion.30 = f32[3,6,64,256]{3,2,1,0:T(8,128)S(1)} fusion(bf16[3,6,6,256,64]{3,4,1,2,0:T(8,128)(2,1)} %copy-done.2, s32[]{:T(128)S(6)} %select_n.135, bf16[3,6,256,64]{2,3,1,0:T(8,128)(2,1)} %collective-permute-done.5, bf16[3,6,256,64]{2,3,1,0:T(8,128)(2,1)} %collective-permute-done.4, pred[]{:T(512)S(6)} %eq.101), kind=kOutput, calls=%fused_computation.36 | convolution fusion | flops 458293248 | bytes 4128773 | tf_op jit(solution)/shard_map/rsac,rstcb->rtab/dot_general | solution.py:102
  136.0 3.4 %multiply_subtract_fusion = f32[3,6,256,64]{2,3,1,0:T(8,128)} fusion(f32[3,6,256,64]{2,3,1,0:T(8,128)S(1)} %copy-done.3, f32[3,6,256,64]{2,3,1,0:T(8,128)S(1)} %copy-done.10, f32[3,6,64,256]{3,2,1,0:T(8,128)S(1)} %fusion.30, bf16[3,6,256,64]{2,3,1,0:T(8,128)(2,1)} %collective-permute-done.5, bf16[3,6,256,64]{2,3,1,0:T(8,128)(2,1)} %collective-permute-done.4, ...), kind=kOutput, calls=%fused_computation.50 | convolution fusion | flops 459767808 | bytes 7667717 | tf_op jit(solution)/shard_map/rsac,rstcb->rtab/dot_general | solution.py:101
  (67 shorter events, 17.5 us)
Async XLA Ops:
  3.0 21.0 %copy-start.9 = (s32[3,3]{1,0:T(4,128)S(1)}, s32[3,3]{1,0:T(4,128)}, u32[]{:S(2)}) copy-start(s32[3,3]{1,0:T(4,128)} %constant.135.clone) | copy-start | bytes 112
  3.0 25.7 %copy-start.8 = (s32[3,4]{1,0:T(4,128)S(1)}, s32[3,4]{1,0:T(4,128)}, u32[]{:S(2)}) copy-start(s32[3,4]{1,0:T(4,128)} %constant.137.clone) | copy-start | bytes 148
  3.0 32.3 %copy-start.7 = (s32[3,4]{1,0:T(4,128)S(1)}, s32[3,4]{1,0:T(4,128)}, u32[]{:S(2)}) copy-start(s32[3,4]{1,0:T(4,128)} %constant.217) | copy-start | bytes 148
  3.9 37.1 %copy-start = (f32[3,6,256,64]{2,3,1,0:T(8,128)}, f32[3,6,256,64]{2,3,1,0:T(8,128)S(1)}, u32[]{:S(2)}) copy-start(f32[3,6,256,64]{2,3,1,0:T(8,128)S(1)} %copy.109) | copy-start | bytes 3538948
  3.9 63.6 %collective-permute-start.1 = (f32[3,6,256,64]{2,3,1,0:T(8,128)S(1)}, f32[3,6,256,64]{2,3,1,0:T(8,128)}, u32[]{:S(2)}, u32[]{:S(2)}) collective-permute-start(f32[3,6,256,64]{2,3,1,0:T(8,128)S(1)} %copy.109), channel_id=1, source_target_pairs={{1,0},{2,1},{3,2},{4,3},{5,4},{6,5},{7,6},{8,7},{9,8},{10,9},{11,1... | collective-permute-start | bytes 3538952 | tf_op jit(solution)/shard_map/ppermute | solution.py:18
  21.1 46.4 %collective-permute-start = (f32[3,6,256,64]{2,3,1,0:T(8,128)S(1)}, f32[3,6,256,64]{2,3,1,0:T(8,128)}, u32[]{:S(2)}, u32[]{:S(2)}) collective-permute-start(f32[3,6,256,64]{2,3,1,0:T(8,128)S(1)} %copy.109), channel_id=1, source_target_pairs={{0,1},{1,2},{2,3},{3,4},{4,5},{5,6},{6,7},{7,8},{8,9},{9,10},{10,1... | collective-permute-start | bytes 3538952 | tf_op jit(solution)/shard_map/ppermute | solution.py:17
  24.0 13.1 %copy-start.4 = (s32[768,6]{1,0:T(8,128)}, s32[768,6]{1,0:T(8,128)S(1)}, u32[]{:S(2)}) copy-start(s32[768,6]{1,0:T(8,128)S(1)} %copy.66) | copy-start | bytes 55300
  62.7 4.9 %copy-start.1 = (f32[3,6,256,64]{2,3,1,0:T(8,128)S(1)}, f32[3,6,256,64]{2,3,1,0:T(8,128)}, u32[]{:S(2)}) copy-start(f32[3,6,256,64]{2,3,1,0:T(8,128)} %copy-done) | copy-start | bytes 3538948
  69.5 3.7 %copy-start.6 = (f32[3,4]{1,0:T(4,128)S(1)}, f32[3,4]{1,0:T(4,128)}, u32[]{:S(2)}) copy-start(f32[3,4]{1,0:T(4,128)} %convert_element_type.62) | copy-start | bytes 148
  73.2 10.0 %copy-start.5 = (s32[3,6,6]{2,1,0:T(8,128)S(1)}, s32[3,6,6]{2,1,0:T(8,128)}, u32[]{:S(2)}) copy-start(s32[3,6,6]{2,1,0:T(8,128)} %reshape.153) | copy-start | bytes 1300
  80.3 21.0 %collective-permute-start.3 = (bf16[3,6,256,64]{2,3,1,0:T(8,128)(2,1)}, bf16[3,6,256,64]{2,3,1,0:T(8,128)(2,1)}, u32[]{:S(2)}, u32[]{:S(2)}) collective-permute-start(bf16[3,6,256,64]{2,3,1,0:T(8,128)(2,1)} %get-tuple-element.24), channel_id=1, source_target_pairs={{0,256},{256,0},{512,768},{768,512},{1,257},{257,1},{513,769},{769... | collective-permute-start | bytes 1769480 | tf_op jit(solution)/shard_map/ppermute | solution.py:106
  85.8 22.3 %collective-permute-start.2 = (bf16[3,6,256,64]{2,3,1,0:T(8,128)(2,1)}, bf16[3,6,256,64]{2,3,1,0:T(8,128)(2,1)}, u32[]{:S(2)}, u32[]{:S(2)}) collective-permute-start(bf16[3,6,256,64]{2,3,1,0:T(8,128)(2,1)} %get-tuple-element.24), channel_id=1, source_target_pairs={{0,128},{1,129},{2,130},{3,131},{4,132},{5,133},{6,134},{7,135},{8... | collective-permute-start | bytes 1769480 | tf_op jit(solution)/shard_map/ppermute | solution.py:113
  101.2 3.6 %copy-start.2 = (bf16[3,6,6,256,64]{3,4,1,2,0:T(8,128)(2,1)}, bf16[3,6,6,256,64]{3,4,1,2,0:T(8,128)(2,1)S(1)}, u32[]{:S(2)}) copy-start(bf16[3,6,6,256,64]{3,4,1,2,0:T(8,128)(2,1)S(1)} %get-tuple-element.23) | copy-start | bytes 10616836
  108.1 19.1 %collective-permute-start.4 = (bf16[3,6,256,64]{2,3,1,0:T(8,128)(2,1)}, bf16[3,6,256,64]{2,3,1,0:T(8,128)(2,1)}, u32[]{:S(2)}, u32[]{:S(2)}) collective-permute-start(bf16[3,6,256,64]{2,3,1,0:T(8,128)(2,1)} %collective-permute-done.2), channel_id=1, source_target_pairs={{0,128},{1,129},{2,130},{3,131},{4,132},{5,133},{6,134},{7,135},{8... | collective-permute-start | bytes 1769480 | tf_op jit(solution)/shard_map/ppermute | solution.py:115
  127.2 6.0 %collective-permute-start.5 = (bf16[3,6,256,64]{2,3,1,0:T(8,128)(2,1)}, bf16[3,6,256,64]{2,3,1,0:T(8,128)(2,1)}, u32[]{:S(2)}, u32[]{:S(2)}) collective-permute-start(bf16[3,6,256,64]{2,3,1,0:T(8,128)(2,1)} %collective-permute-done.4), channel_id=1, source_target_pairs={{0,256},{256,0},{512,768},{768,512},{1,257},{257,1},{513,769},{769... | collective-permute-start | bytes 1769480 | tf_op jit(solution)/shard_map/ppermute | solution.py:116
  131.3 4.8 %copy-start.3 = (f32[3,6,256,64]{2,3,1,0:T(8,128)S(1)}, f32[3,6,256,64]{2,3,1,0:T(8,128)}, u32[]{:S(2)}) copy-start(f32[3,6,256,64]{2,3,1,0:T(8,128)} %get-tuple-element.25) | copy-start | bytes 3538948
  131.3 4.7 %copy-start.10 = (f32[3,6,256,64]{2,3,1,0:T(8,128)S(1)}, f32[3,6,256,64]{2,3,1,0:T(8,128)}, u32[]{:S(2)}) copy-start(f32[3,6,256,64]{2,3,1,0:T(8,128)} %fusion.57) | copy-start | bytes 3538948

commit v6 on v3

--- a/solution.py
+++ b/solution.py
@@ -69,9 +69,9 @@
         high = top.astype(jnp.bfloat16)
         low = (picked - top).astype(jnp.bfloat16)
 
-        def cubed_part(left, half):
-            rows = lax.dynamic_slice_in_dim(high, half * 2 * width, 2 * width, 3)
-            rest = lax.dynamic_slice_in_dim(low, half * 2 * width, 2 * width, 3)
+        def cubed_part(left, first, size):
+            rows = lax.dynamic_slice_in_dim(high, first, size, 3)
+            rest = lax.dynamic_slice_in_dim(low, first, size, 3)
             one = jnp.einsum("rsac,rstcb->rtab", left, rows, preferred_element_type=jnp.float32)
             two = jnp.einsum("rsac,rstcb->rtab", left, rest, preferred_element_type=jnp.float32)
             return one + two
@@ -80,7 +80,7 @@
         mate = lax.ppermute(rounded, "layer", across)
         even = (me % 2) == 0
         near_pair = jnp.where(even, jnp.concatenate([rounded, mate], 3), jnp.concatenate([mate, rounded], 3))
-        near_part = cubed_part(near_pair, me // 2)
+        near_part = cubed_part(near_pair, (me // 2) * 2 * width, 2 * width)
         if relay is None:
             far = lax.ppermute(rounded, "layer", [(i, i ^ 2) for i in range(n_layer)])
         else:
@@ -88,8 +88,8 @@
             halfway, near_part = lax.optimization_barrier((halfway, near_part))
             far = lax.ppermute(halfway, ("layer", "blk"), relay)
         far_mate = lax.ppermute(far, "layer", across)
-        far_pair = jnp.where(even, jnp.concatenate([far, far_mate], 3), jnp.concatenate([far_mate, far], 3))
-        cubed = near_part + cubed_part(far_pair, 1 - me // 2)
+        far_part = cubed_part(far, (me ^ 2) * width, width)
+        cubed = near_part + far_part + cubed_part(far_mate, (me ^ 3) * width, width)
         return (squared, 3.0 * squared - 2.0 * cubed)
 
     return body

time: 118 us -> 120 us (1.017)
  matrix products: 21.9 us -> 25.6 us
    dot_general x2 -> x3, matrix products: 6.83 us -> 8.83 us  [cubed_part(): jnp.einsum('rsac,rstcb->rtab', left, rows, preferred_element_type=jnp.flo...]
    ppermute x1, waiting for transfers between devices: 1.92 us -> 0.01 us  [body(): far_mate = lax.ppermute(far, 'layer', across)]
    dot_general x2 -> x3, matrix products: 6.32 us -> 8.01 us  [cubed_part(): jnp.einsum('rsac,rstcb->rtab', left, rest, preferred_element_type=jnp.flo...]
  transfers between devices with their start and end apart: 6 -> 6, of which waited for: 3 -> 3; matrix products, arithmetic and copies ran while one was open for 13% -> 16% of each run, Pallas kernels for 0% -> 0%
where the time goes in v6:
time: 120 us
  starting transfers between devices  47.8 us (40%)
  waiting for transfers between devices  27.1 us (23%)
  matrix products  25.6 us (21%)
  local copies, waits for them, and re-layouts  9.8 us (8%)
  other arithmetic  8.59 us (7%)
    ppermute x1, starting transfers between devices, padded_2(): after = lax.ppermute(initial, axis, down)  15.2 us
    ppermute x1, waiting for transfers between devices, padded_2(): before = lax.ppermute(last, axis, up)  13.1 us
    ppermute x1, waiting for transfers between devices, body(): far = lax.ppermute(halfway, ('layer', 'blk'), relay)  13.1 us
    ppermute x1, starting transfers between devices, body(): mate = lax.ppermute(rounded, 'layer', across)  9.35 us
    dot_general x3, matrix products, cubed_part(): jnp.einsum('rsac,rstcb->rtab', left, rows, preferred_element_type=jnp.flo...  8.83 us
    dot_general x1, matrix products, body(): jnp.einsum('rsac,rstcb->rtab', density, picked, precision=lax.Precision.H...  8.78 us
    dot_general x3, matrix products, cubed_part(): jnp.einsum('rsac,rstcb->rtab', left, rest, preferred_element_type=jnp.flo...  8.01 us
    ppermute x1, starting transfers between devices, body(): far = lax.ppermute(halfway, ('layer', 'blk'), relay)  7.62 us
  transfers between devices with their start and end apart: 6, of which 3 were waited for; matrix products, arithmetic and copies ran while one was open for 16% of the time, Pallas kernels for 0%

profile of v6, /device:TPU:1, one launch (start us, length us, event | category | flops | bytes accessed | tf_op | source)
XLA Modules:
  0.0 119.8 jit_solution(9995503215301075581)
XLA Ops:
  0.6 2.3 %constant_dynamic-slice_fusion.1 = f32[3,6,256,64]{3,2,1,0:T(8,128)S(1)} fusion(f32[3,6,256,256]{3,2,1,0:T(8,128)} %param.2, s32[]{:T(128)S(6)} %select_n.57), kind=kLoop, calls=%fused_computation.68 | loop fusion | bytes 2359300 | tf_op jit(solution)/shard_map/dynamic_slice | solution.py:63
  3.0 0.9 copy.59
  3.9 3.9 %collective-permute-start = (f32[3,6,256,64]{2,3,1,0:T(8,128)S(1)}, f32[3,6,256,64]{2,3,1,0:T(8,128)}, u32[]{:S(2)}, u32[]{:S(2)}) collective-permute-start(f32[3,6,256,64]{2,3,1,0:T(8,128)S(1)} %copy.59), channel_id=1, source_target_pairs={{0,1},{1,2},{2,3},{3,4},{4,5},{5,6},{6,7},{7,8},{8,9},{9,10},{10,1... | collective-permute-start | bytes 3538952 | tf_op jit(solution)/shard_map/ppermute | solution.py:16
  7.8 15.2 %collective-permute-start.1 = (f32[3,6,256,64]{2,3,1,0:T(8,128)S(1)}, f32[3,6,256,64]{2,3,1,0:T(8,128)}, u32[]{:S(2)}, u32[]{:S(2)}) collective-permute-start(f32[3,6,256,64]{2,3,1,0:T(8,128)S(1)} %copy.59), channel_id=1, source_target_pairs={{1,0},{2,1},{3,2},{4,3},{5,4},{6,5},{7,6},{8,7},{9,8},{10,9},{11,1... | collective-permute-start | bytes 3538952 | tf_op jit(solution)/shard_map/ppermute | solution.py:17
  23.0 0.9 copy.34
  24.0 0.8 fusion.79
  24.8 0.1 copy.37
  24.8 0.1 copy.33
  24.9 0.1 reshape.25
  25.0 0.6 gather_fusion
  25.6 0.1 copy.32
  25.7 1.3 %fusion.71 = (s32[3,6,6]{2,1,0:T(8,128)}, s32[3,6,6]{2,1,0:T(8,128)S(1)}) fusion(s32[3,6]{1,0:T(4,128)S(1)} %copy.37, s32[3,6,6]{2,1,0:T(8,128)S(1)} %reshape.56), kind=kLoop, calls=%fused_computation.46 | loop fusion | flops 5076 | bytes 1368 | tf_op jit(solution)/shard_map/make_body.<locals>.body/reduce | solution.py:58
  27.1 0.1 reshape.31
  27.2 0.5 compare_reduce_fusion
  27.7 0.1 copy.38
  27.8 13.1 %collective-permute-done = f32[3,6,256,64]{2,3,1,0:T(8,128)} collective-permute-done((f32[3,6,256,64]{2,3,1,0:T(8,128)S(1)}, f32[3,6,256,64]{2,3,1,0:T(8,128)}, u32[]{:S(2)}, u32[]{:S(2)}) %collective-permute-start) | collective-permute-done | bytes 1179680 | tf_op jit(solution)/shard_map/ppermute | solution.py:16
  40.9 0.8 collective-permute-done.1
  41.7 2.2 %pad_maximum_fusion = f32[9,6,256,64]{2,3,1,0:T(8,128)S(1)} fusion(f32[3,6,256,64]{2,3,1,0:T(8,128)} %collective-permute-done.1, f32[3,6,256,64]{2,3,1,0:T(8,128)} %copy-done.3, f32[3,6,256,64]{2,3,1,0:T(8,128)} %collective-permute-done), kind=kLoop, calls=%fused_computation.8 | loop fusion | flops 1769472 | bytes 7077888 | tf_op jit(solution)/shard_map/concatenate | solution.py:18
  43.9 4.5 %gather_fusion.1 = f32[108,256,64]{1,2,0:T(8,128)} fusion(f32[9,6,256,64]{2,3,1,0:T(8,128)S(1)} %pad_maximum_fusion, s32[108]{0:T(128)S(1)} %reshape.31), kind=kCustom, calls=%fused_computation.1 | custom fusion | bytes 14156640 | tf_op jit(solution)/shard_map/gather | solution.py:65
  48.4 8.8 %fusion.88 = (bf16[3,6,256,64]{2,3,1,0:T(8,128)(2,1)}, f32[3,6,256,64]{2,3,1,0:T(8,128)}) fusion(f32[3,6,256,256]{3,2,1,0:T(8,128)} %param.2, f32[3,6,6,256,64]{3,4,2,1,0:T(8,128)} %bitcast.90, f32[3,6,6]{1,2,0:T(8,128)S(1)} %copy.38), kind=kOutput, calls=%fused_computation.73 | convolution fusion | flops 2719973376 | bytes 13566384 | tf_op jit(solution)/shard_map/rsac,rstcb->rtab/dot_general | solution.py:66
  57.2 9.4 %collective-permute-start.3 = (bf16[3,6,256,64]{2,3,1,0:T(8,128)(2,1)}, bf16[3,6,256,64]{2,3,1,0:T(8,128)(2,1)}, u32[]{:S(2)}, u32[]{:S(2)}) collective-permute-start(bf16[3,6,256,64]{2,3,1,0:T(8,128)(2,1)} %get-tuple-element.12), channel_id=1, source_target_pairs={{0,256},{256,0},{512,768},{768,512},{1,257},{257,1},{513,769},{769... | collective-permute-start | bytes 1769480 | tf_op jit(solution)/shard_map/ppermute | solution.py:80
  66.6 7.3 %collective-permute-start.2 = (bf16[3,6,256,64]{2,3,1,0:T(8,128)(2,1)}, bf16[3,6,256,64]{2,3,1,0:T(8,128)(2,1)S(1)}, u32[]{:S(2)}, u32[]{:S(2)}) collective-permute-start(bf16[3,6,256,64]{2,3,1,0:T(8,128)(2,1)} %get-tuple-element.12), channel_id=1, source_target_pairs={{0,128},{1,129},{2,130},{3,131},{4,132},{5,133},{6,134},{7,135},{8... | collective-permute-start | bytes 1769480 | tf_op jit(solution)/shard_map/ppermute | solution.py:87
  73.9 3.7 %reduce-precision_convert_fusion = (bf16[3,6,6,256,64]{3,4,1,2,0:T(8,128)(2,1)S(1)}, bf16[3,6,6,256,64]{3,4,1,2,0:T(8,128)(2,1)S(1)}) fusion(f32[3,6,6,256,64]{3,4,2,1,0:T(8,128)} %bitcast.91, f32[3,6,6]{1,2,0:T(8,128)S(1)} %copy.38), kind=kLoop, calls=%fused_computation.3 | loop fusion | flops 8847360 | bytes 14156208 | tf_op jit(solution)/shard_map/convert_element_type | solution.py:69
  77.7 3.5 %fusion.19 = f32[3,6,64,256]{3,2,1,0:T(8,128)S(1)} fusion(bf16[3,6,6,256,64]{3,4,1,2,0:T(8,128)(2,1)S(1)} %get-tuple-element.11, s32[]{:T(128)S(6)} %select_n.64, bf16[3,6,256,64]{2,3,1,0:T(8,128)(2,1)} %collective-permute-done.3, bf16[3,6,256,64]{2,3,1,0:T(8,128)(2,1)} %get-tuple-element.12, pred[]{:T(512)S(6)} %eq.25), kind=kOutput, calls=%fused_computation.23 | convolution fusion | flops 458293248 | bytes 4128773 | tf_op jit(solution)/shard_map/rsac,rstcb->rtab/dot_general | solution.py:76
  81.2 3.4 %fusion.40 = f32[3,6,256,64]{2,3,1,0:T(8,128)} fusion(f32[3,6,64,256]{3,2,1,0:T(8,128)S(1)} %fusion.19, bf16[3,6,6,256,64]{3,4,1,2,0:T(8,128)(2,1)S(1)} %get-tuple-element.10, s32[]{:T(128)S(6)} %select_n.64, bf16[3,6,256,64]{2,3,1,0:T(8,128)(2,1)} %collective-permute-done.3, bf16[3,6,256,64]{2,3,1,0:T(8,128)(2,1)} %get-tuple-element.12, pred[]{:T(512)S(6)} %eq.25), kind=kOutput, calls=%fused_computation.30 | convolution fusion | flops 458588160 | bytes 5308421 | tf_op jit(solution)/shard_map/rsac,rstcb->rtab/dot_general | solution.py:75
  84.6 7.6 %collective-permute-start.4 = (bf16[3,6,256,64]{2,3,1,0:T(8,128)(2,1)S(1)}, bf16[3,6,256,64]{2,3,1,0:T(8,128)(2,1)}, u32[]{:S(2)}, u32[]{:S(2)}) collective-permute-start(bf16[3,6,256,64]{2,3,1,0:T(8,128)(2,1)S(1)} %collective-permute-done.2), channel_id=1, source_target_pairs={{0,128},{1,129},{2,130},{3,131},{4,132},{5,133},{6,134},{7,135},{8... | collective-permute-start | bytes 1769480 | tf_op jit(solution)/shard_map/ppermute | solution.py:89
  92.2 13.1 %collective-permute-done.4 = bf16[3,6,256,64]{2,3,1,0:T(8,128)(2,1)} collective-permute-done((bf16[3,6,256,64]{2,3,1,0:T(8,128)(2,1)S(1)}, bf16[3,6,256,64]{2,3,1,0:T(8,128)(2,1)}, u32[]{:S(2)}, u32[]{:S(2)}) %collective-permute-start.4) | collective-permute-done | bytes 589856 | tf_op jit(solution)/shard_map/ppermute | solution.py:89
  105.4 4.4 %collective-permute-start.5 = (bf16[3,6,256,64]{2,3,1,0:T(8,128)(2,1)}, bf16[3,6,256,64]{2,3,1,0:T(8,128)(2,1)}, u32[]{:S(2)}, u32[]{:S(2)}) collective-permute-start(bf16[3,6,256,64]{2,3,1,0:T(8,128)(2,1)} %collective-permute-done.4), channel_id=1, source_target_pairs={{0,256},{256,0},{512,768},{768,512},{1,257},{257,1},{513,769},{769... | collective-permute-start | bytes 1769480 | tf_op jit(solution)/shard_map/ppermute | solution.py:90
  109.8 2.2 %fusion.25 = f32[3,6,64,256]{3,2,1,0:T(8,128)S(1)} fusion(bf16[3,6,6,256,64]{3,4,1,2,0:T(8,128)(2,1)S(1)} %get-tuple-element.11, s32[]{:T(128)S(6)} %select_n.68, bf16[3,6,256,64]{2,3,1,0:T(8,128)(2,1)} %collective-permute-done.4), kind=kOutput, calls=%fused_computation.25 | convolution fusion | flops 226492416 | bytes 3538948 | tf_op jit(solution)/shard_map/rsac,rstcb->rtab/dot_general | solution.py:76
  112.0 2.1 %fusion.61 = f32[3,6,256,64]{2,3,1,0:T(8,128)S(1)} fusion(f32[3,6,64,256]{3,2,1,0:T(8,128)S(1)} %fusion.25, bf16[3,6,6,256,64]{3,4,1,2,0:T(8,128)(2,1)S(1)} %copy-done.1, s32[]{:T(128)S(6)} %select_n.68, bf16[3,6,256,64]{2,3,1,0:T(8,128)(2,1)} %collective-permute-done.4), kind=kOutput, calls=%fused_computation.37 | convolution fusion | flops 226787328 | bytes 4718596 | tf_op jit(solution)/shard_map/rsac,rstcb->rtab/dot_general | solution.py:75
  114.2 2.2 %fusion.31 = f32[3,6,64,256]{3,2,1,0:T(8,128)S(1)} fusion(bf16[3,6,6,256,64]{3,4,1,2,0:T(8,128)(2,1)S(1)} %get-tuple-element.11, s32[]{:T(128)S(6)} %select_n.69, bf16[3,6,256,64]{2,3,1,0:T(8,128)(2,1)} %collective-permute-done.5), kind=kOutput, calls=%fused_computation.27 | convolution fusion | flops 226492416 | bytes 3538948 | tf_op jit(solution)/shard_map/rsac,rstcb->rtab/dot_general | solution.py:76
  116.4 3.3 %fusion.55 = f32[3,6,256,64]{2,3,1,0:T(8,128)} fusion(f32[3,6,64,256]{3,2,1,0:T(8,128)S(1)} %fusion.31, bf16[3,6,6,256,64]{3,4,1,2,0:T(8,128)(2,1)S(1)} %copy-done.1, s32[]{:T(128)S(6)} %select_n.69, f32[3,6,256,64]{2,3,1,0:T(8,128)S(1)} %copy-done.4, f32[3,6,256,64]{2,3,1,0:T(8,128)S(1)} %fusion.61, f32[3,6,256,64]{2,3,1,0:T(8,128)S(1)} %copy-done.2, ...), kind=kOutput, calls=%fused_computation.35 | convolution fusion | flops 228261888 | bytes 8257540 | tf_op jit(solution)/shard_map/rsac,rstcb->rtab/dot_general | solution.py:75
  (19 shorter events, 0.1 us)
Async XLA Ops:
  3.9 37.0 %copy-start.3 = (f32[3,6,256,64]{2,3,1,0:T(8,128)}, f32[3,6,256,64]{2,3,1,0:T(8,128)S(1)}, u32[]{:S(2)}) copy-start(f32[3,6,256,64]{2,3,1,0:T(8,128)S(1)} %copy.59) | copy-start | bytes 3538948
  3.9 37.0 %collective-permute-start = (f32[3,6,256,64]{2,3,1,0:T(8,128)S(1)}, f32[3,6,256,64]{2,3,1,0:T(8,128)}, u32[]{:S(2)}, u32[]{:S(2)}) collective-permute-start(f32[3,6,256,64]{2,3,1,0:T(8,128)S(1)} %copy.59), channel_id=1, source_target_pairs={{0,1},{1,2},{2,3},{3,4},{4,5},{5,6},{6,7},{7,8},{8,9},{9,10},{10,1... | collective-permute-start | bytes 3538952 | tf_op jit(solution)/shard_map/ppermute | solution.py:16
  7.8 33.9 %collective-permute-start.1 = (f32[3,6,256,64]{2,3,1,0:T(8,128)S(1)}, f32[3,6,256,64]{2,3,1,0:T(8,128)}, u32[]{:S(2)}, u32[]{:S(2)}) collective-permute-start(f32[3,6,256,64]{2,3,1,0:T(8,128)S(1)} %copy.59), channel_id=1, source_target_pairs={{1,0},{2,1},{3,2},{4,3},{5,4},{6,5},{7,6},{8,7},{9,8},{10,9},{11,1... | collective-permute-start | bytes 3538952 | tf_op jit(solution)/shard_map/ppermute | solution.py:17
  57.2 20.5 %collective-permute-start.3 = (bf16[3,6,256,64]{2,3,1,0:T(8,128)(2,1)}, bf16[3,6,256,64]{2,3,1,0:T(8,128)(2,1)}, u32[]{:S(2)}, u32[]{:S(2)}) collective-permute-start(bf16[3,6,256,64]{2,3,1,0:T(8,128)(2,1)} %get-tuple-element.12), channel_id=1, source_target_pairs={{0,256},{256,0},{512,768},{768,512},{1,257},{257,1},{513,769},{769... | collective-permute-start | bytes 1769480 | tf_op jit(solution)/shard_map/ppermute | solution.py:80
  66.6 18.0 %collective-permute-start.2 = (bf16[3,6,256,64]{2,3,1,0:T(8,128)(2,1)}, bf16[3,6,256,64]{2,3,1,0:T(8,128)(2,1)S(1)}, u32[]{:S(2)}, u32[]{:S(2)}) collective-permute-start(bf16[3,6,256,64]{2,3,1,0:T(8,128)(2,1)} %get-tuple-element.12), channel_id=1, source_target_pairs={{0,128},{1,129},{2,130},{3,131},{4,132},{5,133},{6,134},{7,135},{8... | collective-permute-start | bytes 1769480 | tf_op jit(solution)/shard_map/ppermute | solution.py:87
  77.6 3.6 %copy-start = (bf16[3,6,6,256,64]{3,4,1,2,0:T(8,128)(2,1)}, bf16[3,6,6,256,64]{3,4,1,2,0:T(8,128)(2,1)S(1)}, u32[]{:S(2)}) copy-start(bf16[3,6,6,256,64]{3,4,1,2,0:T(8,128)(2,1)S(1)} %get-tuple-element.10) | copy-start | bytes 10616836
  84.6 20.8 %collective-permute-start.4 = (bf16[3,6,256,64]{2,3,1,0:T(8,128)(2,1)S(1)}, bf16[3,6,256,64]{2,3,1,0:T(8,128)(2,1)}, u32[]{:S(2)}, u32[]{:S(2)}) collective-permute-start(bf16[3,6,256,64]{2,3,1,0:T(8,128)(2,1)S(1)} %collective-permute-done.2), channel_id=1, source_target_pairs={{0,128},{1,129},{2,130},{3,131},{4,132},{5,133},{6,134},{7,135},{8... | collective-permute-start | bytes 1769480 | tf_op jit(solution)/shard_map/ppermute | solution.py:89
  105.4 8.8 %collective-permute-start.5 = (bf16[3,6,256,64]{2,3,1,0:T(8,128)(2,1)}, bf16[3,6,256,64]{2,3,1,0:T(8,128)(2,1)}, u32[]{:S(2)}, u32[]{:S(2)}) collective-permute-start(bf16[3,6,256,64]{2,3,1,0:T(8,128)(2,1)} %collective-permute-done.4), channel_id=1, source_target_pairs={{0,256},{256,0},{512,768},{768,512},{1,257},{257,1},{513,769},{769... | collective-permute-start | bytes 1769480 | tf_op jit(solution)/shard_map/ppermute | solution.py:90
  109.8 2.3 %copy-start.1 = (bf16[3,6,6,256,64]{3,4,1,2,0:T(8,128)(2,1)S(1)}, bf16[3,6,6,256,64]{3,4,1,2,0:T(8,128)(2,1)}, u32[]{:S(2)}) copy-start(bf16[3,6,6,256,64]{3,4,1,2,0:T(8,128)(2,1)} %copy-done) | copy-start | bytes 10616836
  114.1 2.3 %copy-start.2 = (f32[3,6,256,64]{2,3,1,0:T(8,128)S(1)}, f32[3,6,256,64]{2,3,1,0:T(8,128)}, u32[]{:S(2)}) copy-start(f32[3,6,256,64]{2,3,1,0:T(8,128)} %get-tuple-element.13) | copy-start | bytes 3538948
  114.2 2.3 %copy-start.4 = (f32[3,6,256,64]{2,3,1,0:T(8,128)S(1)}, f32[3,6,256,64]{2,3,1,0:T(8,128)}, u32[]{:S(2)}) copy-start(f32[3,6,256,64]{2,3,1,0:T(8,128)} %fusion.40) | copy-start | bytes 3538948

commit v7 on v1

--- a/solution.py
+++ b/solution.py
@@ -62,26 +62,40 @@
         place = jnp.arange(count_rows, dtype=jnp.int32)[:, None] + BAND + offset
         col_part = lax.dynamic_slice_in_dim(density, start_col, width, 3)
         padded = padded_2(col_part, (("blk", 0),), BAND)
-        highest = lax.Precision.HIGHEST
-        picked = padded[place[:, :, None], slot] * valid[:, :, :, None, None]
+        across = [(i, i ^ 1) for i in range(n_layer)]
+        even = (me % 2) == 0
+        groups = [(0, 1), (1, count_rows)] if count_rows > 1 else [(0, count_rows)]
+        squares, cubes = [], []
+        for lo, hi in groups:
+            picked = padded[place[lo:hi, :, None], slot[lo:hi]] * valid[lo:hi, :, :, None, None]
+            squared = jnp.einsum("rsac,rstcb->rtab", density[lo:hi], picked, precision=lax.Precision.HIGH)
+            rounded = squared.astype(jnp.bfloat16)
+            top = lax.reduce_precision(picked, exponent_bits=8, mantissa_bits=7)
+            high = top.astype(jnp.bfloat16)
+            low = (picked - top).astype(jnp.bfloat16)
 
-        def product(left):
-            return jnp.einsum("rsac,rstcb->rtab", left, picked, precision=highest)
+            def cubed_part(left, half):
+                rows = lax.dynamic_slice_in_dim(high, half * 2 * width, 2 * width, 3)
+                rest = lax.dynamic_slice_in_dim(low, half * 2 * width, 2 * width, 3)
+                one = jnp.einsum("rsac,rstcb->rtab", left, rows, preferred_element_type=jnp.float32)
+                two = jnp.einsum("rsac,rstcb->rtab", left, rest, preferred_element_type=jnp.float32)
+                return one + two
 
-        squared = product(density)
-        rounded = squared.astype(jnp.bfloat16)
-        across = [(i, i ^ 1) for i in range(n_layer)]
-        mate = lax.ppermute(rounded, "layer", across)
-        if relay is None:
-            far = lax.ppermute(rounded, "layer", [(i, i ^ 2) for i in range(n_layer)])
-        else:
-            halfway = lax.ppermute(rounded, ("layer", "blk"), relay)
-            far = lax.ppermute(halfway, ("layer", "blk"), relay)
-        far_mate = lax.ppermute(far, "layer", across)
-        pieces = jnp.stack([rounded, mate, far, far_mate])
-        quarters = jnp.take(pieces, jnp.bitwise_xor(jnp.arange(4, dtype=jnp.int32), me), axis=0)
-        gathered = jnp.moveaxis(quarters, 0, 3).reshape(count_rows, slots, order, order)
-        cubed = product(gathered.astype(jnp.float32))
+            mate = lax.ppermute(rounded, "layer", across)
+            near_pair = jnp.where(even, jnp.concatenate([rounded, mate], 3), jnp.concatenate([mate, rounded], 3))
+            near_part = cubed_part(near_pair, me // 2)
+            if relay is None:
+                far = lax.ppermute(rounded, "layer", [(i, i ^ 2) for i in range(n_layer)])
+            else:
+                halfway = lax.ppermute(rounded, ("layer", "blk"), relay)
+                halfway, near_part = lax.optimization_barrier((halfway, near_part))
+                far = lax.ppermute(halfway, ("layer", "blk"), relay)
+            far_mate = lax.ppermute(far, "layer", across)
+            far_pair = jnp.where(even, jnp.concatenate([far, far_mate], 3), jnp.concatenate([far_mate, far], 3))
+            squares.append(squared)
+            cubes.append(near_part + cubed_part(far_pair, 1 - me // 2))
+        squared = jnp.concatenate(squares, 0)
+        cubed = jnp.concatenate(cubes, 0)
         return (squared, 3.0 * squared - 2.0 * cubed)
 
     return body

time: 135 us -> 134 us (level)
  waiting for transfers between devices: 50.1 us -> 33.6 us
  starting transfers between devices: 38.8 us -> 52.9 us
  matrix products: 19.8 us -> 23.2 us
  local copies, waits for them, and re-layouts: 16.1 us -> 13.6 us
    ppermute x1 -> x2, waiting for transfers between devices: 13.1 us -> 2.21 us  [body(): halfway = lax.ppermute(rounded, ('layer', 'blk'), relay)]
    ppermute x1 -> x2, starting transfers between devices: 5.23 us -> 13.8 us  [body(): halfway = lax.ppermute(rounded, ('layer', 'blk'), relay)]
    ppermute x1 -> x2, starting transfers between devices: 1.92 us -> 5.63 us  [body(): mate = lax.ppermute(rounded, 'layer', across)]
    dot_general x2 -> x10, matrix products: 19.8 us -> 23.2 us  [the longest x2 9.72 us: body(): jnp.einsum('rsac,rstcb->rtab', density[lo:hi], picked, precision=lax.Prec...]
    ppermute x1 -> x2, waiting for transfers between devices: 8.71 us -> 5.62 us  [body(): far = lax.ppermute(halfway, ('layer', 'blk'), relay)]
    gather x2, local copies, waits for them, and re-layouts: 8.39 us -> 6.18 us  [body(): padded[place[lo:hi, :, None], slot[lo:hi]] * valid[lo:hi, :, :, None, None]]
    ppermute x1 -> x2, starting transfers between devices: 5.59 us -> 7.77 us  [body(): far_mate = lax.ppermute(far, 'layer', across)]
    select_n x2, other arithmetic: 2.11 us -> 0.01 us  [body(): padded[place[lo:hi, :, None], slot[lo:hi]] * valid[lo:hi, :, :, None, None]]
  transfers between devices with their start and end apart: 6 -> 10, of which waited for: 5 -> 4; matrix products, arithmetic and copies ran while one was open for 4% -> 20% of each run, Pallas kernels for 0% -> 0%
where the time goes in v7:
time: 134 us; the launch traced here: 132 us
  starting transfers between devices  52.9 us (39%)
  waiting for transfers between devices  33.6 us (25%)
  matrix products  23.2 us (17%)
  local copies, waits for them, and re-layouts  13.6 us (10%)
  other arithmetic  7.89 us (6%)
    ppermute x1, starting transfers between devices, padded_2(): after = lax.ppermute(initial, axis, down)  17.2 us
    ppermute x1, waiting for transfers between devices, padded_2(): after = lax.ppermute(initial, axis, down)  16.9 us
    ppermute x2, starting transfers between devices, body(): halfway = lax.ppermute(rounded, ('layer', 'blk'), relay)  13.8 us
    dot_general x2, matrix products, body(): jnp.einsum('rsac,rstcb->rtab', density[lo:hi], picked, precision=lax.Prec...  9.72 us
    ppermute x1, waiting for transfers between devices, padded_2(): before = lax.ppermute(last, axis, up)  8.94 us
    ppermute x2, starting transfers between devices, body(): far_mate = lax.ppermute(far, 'layer', across)  7.77 us
    dot_general x4, matrix products, cubed_part(): jnp.einsum('rsac,rstcb->rtab', left, rows, preferred_element_type=jnp.flo...  7.22 us
    ppermute x2, starting transfers between devices, body(): far = lax.ppermute(halfway, ('layer', 'blk'), relay)  6.61 us
  transfers between devices with their start and end apart: 10, of which 4 were waited for; matrix products, arithmetic and copies ran while one was open for 20% of the time, Pallas kernels for 0%

profile of v7, /device:TPU:1, one launch (start us, length us, event | category | flops | bytes accessed | tf_op | source)
XLA Modules:
  0.0 132.4 jit_solution(4956420054847555926)
XLA Ops:
  0.6 2.3 %constant_dynamic-slice_fusion.1 = f32[3,6,256,64]{3,2,1,0:T(8,128)S(1)} fusion(f32[3,6,256,256]{3,2,1,0:T(8,128)} %param.2, s32[]{:T(128)S(6)} %select_n.95), kind=kLoop, calls=%fused_computation.101 | loop fusion | bytes 2359300 | tf_op jit(solution)/shard_map/dynamic_slice | solution.py:63
  3.0 0.9 copy.151
  3.9 17.2 %collective-permute-start.1 = (f32[3,6,256,64]{2,3,1,0:T(8,128)S(1)}, f32[3,6,256,64]{2,3,1,0:T(8,128)S(1)}, u32[]{:S(2)}, u32[]{:S(2)}) collective-permute-start(f32[3,6,256,64]{2,3,1,0:T(8,128)S(1)} %copy.151), channel_id=1, source_target_pairs={{1,0},{2,1},{3,2},{4,3},{5,4},{6,5},{7,6},{8,7},{9,8},{10,9},{11,1... | collective-permute-start | bytes 3538952 | tf_op jit(solution)/shard_map/ppermute | solution.py:17
  21.1 1.9 %collective-permute-start = (f32[3,6,256,64]{2,3,1,0:T(8,128)S(1)}, f32[3,6,256,64]{2,3,1,0:T(8,128)}, u32[]{:S(2)}, u32[]{:S(2)}) collective-permute-start(f32[3,6,256,64]{2,3,1,0:T(8,128)S(1)} %copy.151), channel_id=1, source_target_pairs={{0,1},{1,2},{2,3},{3,4},{4,5},{5,6},{6,7},{7,8},{8,9},{9,10},{10,1... | collective-permute-start | bytes 3538952 | tf_op jit(solution)/shard_map/ppermute | solution.py:16
  23.9 0.9 copy.98
  26.1 1.4 %fusion.55 = (s32[3,6,6]{2,1,0:T(8,128)}, s32[3,6,6]{2,1,0:T(8,128)S(1)}) fusion(s32[3,6]{1,0:T(4,128)S(1)} %copy.101, s32[3,6,6]{2,1,0:T(8,128)S(1)} %reshape.206), kind=kLoop, calls=%fused_computation.66 | loop fusion | flops 5076 | bytes 1368 | tf_op jit(solution)/shard_map/make_body.<locals>.body/reduce | solution.py:58
  28.9 16.9 %collective-permute-done.1 = f32[3,6,256,64]{2,3,1,0:T(8,128)S(1)} collective-permute-done((f32[3,6,256,64]{2,3,1,0:T(8,128)S(1)}, f32[3,6,256,64]{2,3,1,0:T(8,128)S(1)}, u32[]{:S(2)}, u32[]{:S(2)}) %collective-permute-start.1) | collective-permute-done | bytes 1179680 | tf_op jit(solution)/shard_map/ppermute | solution.py:17
  45.7 1.0 copy-done.6
  46.7 8.9 %collective-permute-done = f32[3,6,256,64]{2,3,1,0:T(8,128)} collective-permute-done((f32[3,6,256,64]{2,3,1,0:T(8,128)S(1)}, f32[3,6,256,64]{2,3,1,0:T(8,128)}, u32[]{:S(2)}, u32[]{:S(2)}) %collective-permute-start) | collective-permute-done | bytes 1179680 | tf_op jit(solution)/shard_map/ppermute | solution.py:16
  55.7 2.2 %pad_maximum_fusion = f32[9,6,256,64]{2,3,1,0:T(8,128)S(1)} fusion(f32[3,6,256,64]{2,3,1,0:T(8,128)} %copy-done.6, f32[3,6,256,64]{2,3,1,0:T(8,128)} %copy-done.2, f32[3,6,256,64]{2,3,1,0:T(8,128)} %collective-permute-done), kind=kLoop, calls=%fused_computation.8 | loop fusion | flops 1769472 | bytes 7077888 | tf_op jit(solution)/shard_map/concatenate | solution.py:18
  57.9 2.5 %gather_fusion.1 = f32[36,256,64]{1,2,0:T(8,128)} fusion(f32[9,6,256,64]{2,3,1,0:T(8,128)S(1)} %pad_maximum_fusion, s32[36]{0:T(128)S(1)} %reshape.165), kind=kCustom, calls=%fused_computation.1 | custom fusion | bytes 4718880 | tf_op jit(solution)/shard_map/gather | solution.py:70
  60.4 4.1 %fusion.83 = (bf16[1,6,256,64]{2,3,1,0:T(8,128)(2,1)}, f32[1,6,256,64]{2,3,1,0:T(8,128)}) fusion(f32[3,6,256,256]{3,2,1,0:T(8,128)} %param.2, f32[6,6,256,64]{2,3,1,0:T(8,128)} %bitcast.146, f32[6,6]{0,1:T(8,128)} %copy.103), kind=kOutput, calls=%fused_computation.113 | convolution fusion | flops 906657792 | bytes 4526080 | tf_op jit(solution)/shard_map/rsac,rstcb->rtab/dot_general | solution.py:71
  64.4 3.7 %collective-permute-start.3 = (bf16[1,6,256,64]{2,3,1,0:T(8,128)(2,1)}, bf16[1,6,256,64]{2,3,1,0:T(8,128)(2,1)}, u32[]{:S(2)}, u32[]{:S(2)}) collective-permute-start(bf16[1,6,256,64]{2,3,1,0:T(8,128)(2,1)} %get-tuple-element.22), channel_id=1, source_target_pairs={{0,256},{256,0},{512,768},{768,512},{1,257},{257,1},{513,769},{769... | collective-permute-start | bytes 589832 | tf_op jit(solution)/shard_map/ppermute | solution.py:84
  68.2 5.2 %collective-permute-start.2 = (bf16[1,6,256,64]{2,3,1,0:T(8,128)(2,1)}, bf16[1,6,256,64]{2,3,1,0:T(8,128)(2,1)}, u32[]{:S(2)}, u32[]{:S(2)}) collective-permute-start(bf16[1,6,256,64]{2,3,1,0:T(8,128)(2,1)} %get-tuple-element.22), channel_id=1, source_target_pairs={{0,128},{1,129},{2,130},{3,131},{4,132},{5,133},{6,134},{7,135},{8... | collective-permute-start | bytes 589832 | tf_op jit(solution)/shard_map/ppermute | solution.py:90
  73.4 3.7 %gather_fusion.2 = f32[72,256,64]{1,2,0:T(8,128)} fusion(f32[9,6,256,64]{2,3,1,0:T(8,128)S(1)} %pad_maximum_fusion, s32[72]{0:T(128)S(1)} %reshape.171), kind=kCustom, calls=%fused_computation.2 | custom fusion | bytes 9437760 | tf_op jit(solution)/shard_map/gather | solution.py:70
  77.1 5.6 %fusion.82 = (bf16[2,6,256,64]{2,3,1,0:T(8,128)(2,1)S(1)}, f32[2,6,256,64]{2,3,1,0:T(8,128)S(1)}) fusion(f32[3,6,256,256]{3,2,1,0:T(8,128)} %param.2, f32[2,6,6,256,64]{3,4,2,1,0:T(8,128)} %bitcast.144, f32[2,6,6]{1,2,0:T(8,128)S(1)} %copy.107), kind=kOutput, calls=%fused_computation.112 | convolution fusion | flops 1813315584 | bytes 9044256 | tf_op jit(solution)/shard_map/rsac,rstcb->rtab/dot_general | solution.py:71
  83.5 1.9 %collective-permute-start.7 = (bf16[2,6,256,64]{2,3,1,0:T(8,128)(2,1)S(1)}, bf16[2,6,256,64]{2,3,1,0:T(8,128)(2,1)S(1)}, u32[]{:S(2)}, u32[]{:S(2)}) collective-permute-start(bf16[2,6,256,64]{2,3,1,0:T(8,128)(2,1)S(1)} %get-tuple-element.20), channel_id=1, source_target_pairs={{0,256},{256,0},{512,768},{768,512},{1,257},{257,1},{513,769},{769... | collective-permute-start | bytes 1179656 | tf_op jit(solution)/shard_map/ppermute | solution.py:84
  85.5 8.5 %collective-permute-start.6 = (bf16[2,6,256,64]{2,3,1,0:T(8,128)(2,1)S(1)}, bf16[2,6,256,64]{2,3,1,0:T(8,128)(2,1)S(1)}, u32[]{:S(2)}, u32[]{:S(2)}) collective-permute-start(bf16[2,6,256,64]{2,3,1,0:T(8,128)(2,1)S(1)} %get-tuple-element.20), channel_id=1, source_target_pairs={{0,128},{1,129},{2,130},{3,131},{4,132},{5,133},{6,134},{7,135},{8... | collective-permute-start | bytes 1179656 | tf_op jit(solution)/shard_map/ppermute | solution.py:90
  94.5 2.4 %convolution_bitcast_fusion.6 = f32[6,64,256]{2,1,0:T(8,128)S(1)} fusion(bf16[1,6,6,256,64]{3,4,1,2,0:T(8,128)(2,1)S(1)} %get-tuple-element.19, s32[]{:T(128)S(6)} %select_n.104, bf16[6,256,64]{1,2,0:T(8,128)(2,1)} %bitcast.20, bf16[6,256,64]{1,2,0:T(8,128)(2,1)} %bitcast.19, pred[]{:T(512)S(6)} %eq.25), kind=kOutput, calls=%fused_computation.33 | convolution fusion | flops 152764416 | bytes 1376261 | tf_op jit(solution)/shard_map/rsac,rstcb->rtab/dot_general | solution.py:81
  97.4 1.4 %fusion.13 = f32[2,6,256,64]{2,3,1,0:T(8,128)} fusion(f32[2,6,64,256]{3,2,1,0:T(8,128)S(1)} %convolution_bitcast_fusion.2, bf16[2,6,6,256,64]{3,4,1,2,0:T(8,128)(2,1)S(1)} %get-tuple-element.16, s32[]{:T(128)S(6)} %select_n.104, bf16[2,6,256,64]{2,3,1,0:T(8,128)(2,1)S(1)} %collective-permute-done.7, bf16[2,6,256,64]{2,3,1,0:T(8,128)(2,1)S(1)} %get-tuple-element.20, ...), kind=kOutput, calls=%fused_computation.26 | convolution fusion | flops 305725440 | bytes 3538949 | tf_op jit(solution)/shard_map/rsac,rstcb->rtab/dot_general | solution.py:80
  98.8 2.2 %collective-permute-done.6 = bf16[2,6,256,64]{2,3,1,0:T(8,128)(2,1)S(1)} collective-permute-done((bf16[2,6,256,64]{2,3,1,0:T(8,128)(2,1)S(1)}, bf16[2,6,256,64]{2,3,1,0:T(8,128)(2,1)S(1)}, u32[]{:S(2)}, u32[]{:S(2)}) %collective-permute-start.6) | collective-permute-done | bytes 393248 | tf_op jit(solution)/shard_map/ppermute | solution.py:90
  101.1 3.6 %collective-permute-start.8 = (bf16[2,6,256,64]{2,3,1,0:T(8,128)(2,1)S(1)}, bf16[2,6,256,64]{2,3,1,0:T(8,128)(2,1)S(1)}, u32[]{:S(2)}, u32[]{:S(2)}) collective-permute-start(bf16[2,6,256,64]{2,3,1,0:T(8,128)(2,1)S(1)} %collective-permute-done.6), channel_id=1, source_target_pairs={{0,128},{1,129},{2,130},{3,131},{4,132},{5,133},{6,134},{7,135},{8... | collective-permute-start | bytes 1179656 | tf_op jit(solution)/shard_map/ppermute | solution.py:92
  104.6 2.3 %fusion.21 = f32[1,6,256,64]{2,3,1,0:T(8,128)} fusion(f32[6,64,256]{2,1,0:T(8,128)S(1)} %convolution_bitcast_fusion.6, bf16[1,6,6,256,64]{3,4,1,2,0:T(8,128)(2,1)S(1)} %get-tuple-element.18, s32[]{:T(128)S(6)} %select_n.104, bf16[6,256,64]{1,2,0:T(8,128)(2,1)} %bitcast.20, bf16[6,256,64]{1,2,0:T(8,128)(2,1)} %bitcast.19, pred[]{:T(512)S(6)} %eq.25), kind=kOutput, calls=%fused_computation.36 | convolution fusion | flops 152862720 | bytes 1769477 | tf_op jit(solution)/shard_map/rsac,rstcb->rtab/dot_general | solution.py:80
  107.0 3.0 %collective-permute-start.4 = (bf16[1,6,256,64]{2,3,1,0:T(8,128)(2,1)}, bf16[1,6,256,64]{2,3,1,0:T(8,128)(2,1)}, u32[]{:S(2)}, u32[]{:S(2)}) collective-permute-start(bf16[1,6,256,64]{2,3,1,0:T(8,128)(2,1)} %collective-permute-done.2), channel_id=1, source_target_pairs={{0,128},{1,129},{2,130},{3,131},{4,132},{5,133},{6,134},{7,135},{8... | collective-permute-start | bytes 589832 | tf_op jit(solution)/shard_map/ppermute | solution.py:92
  110.0 5.6 %collective-permute-done.4 = bf16[1,6,256,64]{2,3,1,0:T(8,128)(2,1)} collective-permute-done((bf16[1,6,256,64]{2,3,1,0:T(8,128)(2,1)}, bf16[1,6,256,64]{2,3,1,0:T(8,128)(2,1)}, u32[]{:S(2)}, u32[]{:S(2)}) %collective-permute-start.4) | collective-permute-done | bytes 196640 | tf_op jit(solution)/shard_map/ppermute | solution.py:92
  115.7 5.8 %collective-permute-start.5 = (bf16[1,6,256,64]{2,3,1,0:T(8,128)(2,1)}, bf16[1,6,256,64]{2,3,1,0:T(8,128)(2,1)}, u32[]{:S(2)}, u32[]{:S(2)}) collective-permute-start(bf16[1,6,256,64]{2,3,1,0:T(8,128)(2,1)} %collective-permute-done.4), channel_id=1, source_target_pairs={{0,256},{256,0},{512,768},{768,512},{1,257},{257,1},{513,769},{769... | collective-permute-start | bytes 589832 | tf_op jit(solution)/shard_map/ppermute | solution.py:93
  121.5 1.9 %collective-permute-start.9 = (bf16[2,6,256,64]{2,3,1,0:T(8,128)(2,1)S(1)}, bf16[2,6,256,64]{2,3,1,0:T(8,128)(2,1)}, u32[]{:S(2)}, u32[]{:S(2)}) collective-permute-start(bf16[2,6,256,64]{2,3,1,0:T(8,128)(2,1)S(1)} %collective-permute-done.8), channel_id=1, source_target_pairs={{0,256},{256,0},{512,768},{768,512},{1,257},{257,1},{513,769},{769... | collective-permute-start | bytes 1179656 | tf_op jit(solution)/shard_map/ppermute | solution.py:93
  123.5 1.8 %convolution_bitcast_fusion.4 = f32[6,64,256]{2,1,0:T(8,128)S(1)} fusion(bf16[1,6,6,256,64]{3,4,1,2,0:T(8,128)(2,1)} %copy-done.9, s32[]{:T(128)S(6)} %select_n.108, bf16[6,256,64]{1,2,0:T(8,128)(2,1)} %bitcast.32, bf16[6,256,64]{1,2,0:T(8,128)(2,1)} %bitcast.31, pred[]{:T(512)S(6)} %eq.25), kind=kOutput, calls=%fused_computation.31 | convolution fusion | flops 152764416 | bytes 1376261 | tf_op jit(solution)/shard_map/rsac,rstcb->rtab/dot_general | solution.py:81
  125.3 1.7 %fusion.48 = f32[1,6,256,64]{2,3,1,0:T(8,128)S(1)} fusion(f32[1,6,256,64]{2,3,1,0:T(8,128)S(1)} %copy-done.11, f32[6,64,256]{2,1,0:T(8,128)S(1)} %convolution_bitcast_fusion.4, bf16[6,256,64]{1,2,0:T(8,128)(2,1)} %bitcast.32, bf16[6,256,64]{1,2,0:T(8,128)(2,1)} %bitcast.31, pred[]{:T(512)S(6)} %eq.25, bf16[1,6,6,256,64]{3,4,1,2,0:T(8,128)(2,1)S(1)} %copy-done.8, ...), kind=kOutput, calls=%fused_computation.63 | convolution fusion | flops 152961024 | bytes 2162693 | tf_op jit(solution)/shard_map/rsac,rstcb->rtab/dot_general | solution.py:80
  127.3 1.6 %convolution_bitcast_fusion = f32[2,6,64,256]{3,2,1,0:T(8,128)S(1)} fusion(bf16[2,6,6,256,64]{3,4,1,2,0:T(8,128)(2,1)S(1)} %copy-done.4, s32[]{:T(128)S(6)} %select_n.108, bf16[2,6,256,64]{2,3,1,0:T(8,128)(2,1)} %collective-permute-done.9, bf16[2,6,256,64]{2,3,1,0:T(8,128)(2,1)S(1)} %collective-permute-done.8, pred[]{:T(512)S(6)} %eq.25), kind=kOutput, calls=%fused_computation.21 | convolution fusion | flops 305528832 | bytes 2752517 | tf_op jit(solution)/shard_map/rsac,rstcb->rtab/dot_general | solution.py:81
  128.9 1.7 %fusion.16 = f32[2,6,256,64]{2,3,1,0:T(8,128)S(1)} fusion(f32[2,6,256,64]{2,3,1,0:T(8,128)S(1)} %copy-done.12, f32[2,6,64,256]{3,2,1,0:T(8,128)S(1)} %convolution_bitcast_fusion, bf16[2,6,6,256,64]{3,4,1,2,0:T(8,128)(2,1)S(1)} %get-tuple-element.16, s32[]{:T(128)S(6)} %select_n.108, bf16[2,6,256,64]{2,3,1,0:T(8,128)(2,1)} %collective-permute-done.9, ...), kind=kOutput, calls=%fused_computation.29 | convolution fusion | flops 305922048 | bytes 4325381 | tf_op jit(solution)/shard_map/rsac,rstcb->rtab/dot_general | solution.py:80
  130.7 1.7 %fusion.24 = (f32[3,6,256,64]{2,3,1,0:T(8,128)}, f32[3,6,256,64]{2,3,1,0:T(8,128)}) fusion(f32[2,6,256,64]{2,3,1,0:T(8,128)S(1)} %fusion.16, f32[1,6,256,64]{2,3,1,0:T(8,128)S(1)} %fusion.48, f32[2,6,256,64]{2,3,1,0:T(8,128)S(1)} %get-tuple-element.21, f32[1,6,256,64]{2,3,1,0:T(8,128)S(1)} %copy-done.5), kind=kLoop, calls=%fused_computation.41 | loop fusion | flops 1474560 | bytes 4718592 | tf_op jit(solution)/shard_map/sub | solution.py:99
  (63 shorter events, 5.4 us)
Async XLA Ops:
  3.9 41.8 %copy-start.2 = (f32[3,6,256,64]{2,3,1,0:T(8,128)}, f32[3,6,256,64]{2,3,1,0:T(8,128)S(1)}, u32[]{:S(2)}) copy-start(f32[3,6,256,64]{2,3,1,0:T(8,128)S(1)} %copy.151) | copy-start | bytes 3538948
  3.9 41.8 %collective-permute-start.1 = (f32[3,6,256,64]{2,3,1,0:T(8,128)S(1)}, f32[3,6,256,64]{2,3,1,0:T(8,128)S(1)}, u32[]{:S(2)}, u32[]{:S(2)}) collective-permute-start(f32[3,6,256,64]{2,3,1,0:T(8,128)S(1)} %copy.151), channel_id=1, source_target_pairs={{1,0},{2,1},{3,2},{4,3},{5,4},{6,5},{7,6},{8,7},{9,8},{10,9},{11,1... | collective-permute-start | bytes 3538952 | tf_op jit(solution)/shard_map/ppermute | solution.py:17
  21.1 34.6 %collective-permute-start = (f32[3,6,256,64]{2,3,1,0:T(8,128)S(1)}, f32[3,6,256,64]{2,3,1,0:T(8,128)}, u32[]{:S(2)}, u32[]{:S(2)}) collective-permute-start(f32[3,6,256,64]{2,3,1,0:T(8,128)S(1)} %copy.151), channel_id=1, source_target_pairs={{0,1},{1,2},{2,3},{3,4},{4,5},{5,6},{6,7},{7,8},{8,9},{9,10},{10,1... | collective-permute-start | bytes 3538952 | tf_op jit(solution)/shard_map/ppermute | solution.py:16
  45.7 1.0 copy-start.6
  64.4 30.0 %collective-permute-start.3 = (bf16[1,6,256,64]{2,3,1,0:T(8,128)(2,1)}, bf16[1,6,256,64]{2,3,1,0:T(8,128)(2,1)}, u32[]{:S(2)}, u32[]{:S(2)}) collective-permute-start(bf16[1,6,256,64]{2,3,1,0:T(8,128)(2,1)} %get-tuple-element.22), channel_id=1, source_target_pairs={{0,256},{256,0},{512,768},{768,512},{1,257},{257,1},{513,769},{769... | collective-permute-start | bytes 589832 | tf_op jit(solution)/shard_map/ppermute | solution.py:84
  68.2 38.8 %collective-permute-start.2 = (bf16[1,6,256,64]{2,3,1,0:T(8,128)(2,1)}, bf16[1,6,256,64]{2,3,1,0:T(8,128)(2,1)}, u32[]{:S(2)}, u32[]{:S(2)}) collective-permute-start(bf16[1,6,256,64]{2,3,1,0:T(8,128)(2,1)} %get-tuple-element.22), channel_id=1, source_target_pairs={{0,128},{1,129},{2,130},{3,131},{4,132},{5,133},{6,134},{7,135},{8... | collective-permute-start | bytes 589832 | tf_op jit(solution)/shard_map/ppermute | solution.py:90
  77.1 5.6 %copy-start = (f32[72,256,64]{1,2,0:T(8,128)S(1)}, f32[72,256,64]{1,2,0:T(8,128)}, u32[]{:S(2)}) copy-start(f32[72,256,64]{1,2,0:T(8,128)} %gather_fusion.2) | copy-start | bytes 14155780
  82.8 11.3 %copy-start.1 = (f32[36,256,64]{1,2,0:T(8,128)S(1)}, f32[36,256,64]{1,2,0:T(8,128)}, u32[]{:S(2)}) copy-start(f32[36,256,64]{1,2,0:T(8,128)} %gather_fusion.1) | copy-start | bytes 7077892
  82.8 11.3 %copy-start.10 = (f32[6,6]{0,1:T(8,128)S(1)}, f32[6,6]{0,1:T(8,128)}, u32[]{:S(2)}) copy-start(f32[6,6]{0,1:T(8,128)} %copy.103) | copy-start | bytes 436
  83.5 13.4 %copy-start.3 = (bf16[2,6,6,256,64]{3,4,1,2,0:T(8,128)(2,1)}, bf16[2,6,6,256,64]{3,4,1,2,0:T(8,128)(2,1)S(1)}, u32[]{:S(2)}) copy-start(bf16[2,6,6,256,64]{3,4,1,2,0:T(8,128)(2,1)S(1)} %get-tuple-element.17) | copy-start | bytes 7077892
  83.5 13.3 %collective-permute-start.7 = (bf16[2,6,256,64]{2,3,1,0:T(8,128)(2,1)S(1)}, bf16[2,6,256,64]{2,3,1,0:T(8,128)(2,1)S(1)}, u32[]{:S(2)}, u32[]{:S(2)}) collective-permute-start(bf16[2,6,256,64]{2,3,1,0:T(8,128)(2,1)S(1)} %get-tuple-element.20), channel_id=1, source_target_pairs={{0,256},{256,0},{512,768},{768,512},{1,257},{257,1},{513,769},{769... | collective-permute-start | bytes 1179656 | tf_op jit(solution)/shard_map/ppermute | solution.py:84
  85.5 15.6 %collective-permute-start.6 = (bf16[2,6,256,64]{2,3,1,0:T(8,128)(2,1)S(1)}, bf16[2,6,256,64]{2,3,1,0:T(8,128)(2,1)S(1)}, u32[]{:S(2)}, u32[]{:S(2)}) collective-permute-start(bf16[2,6,256,64]{2,3,1,0:T(8,128)(2,1)S(1)} %get-tuple-element.20), channel_id=1, source_target_pairs={{0,128},{1,129},{2,130},{3,131},{4,132},{5,133},{6,134},{7,135},{8... | collective-permute-start | bytes 1179656 | tf_op jit(solution)/shard_map/ppermute | solution.py:90
  94.5 3.0 %copy-start.9 = (bf16[1,6,6,256,64]{3,4,1,2,0:T(8,128)(2,1)}, bf16[1,6,6,256,64]{3,4,1,2,0:T(8,128)(2,1)S(1)}, u32[]{:S(2)}) copy-start(bf16[1,6,6,256,64]{3,4,1,2,0:T(8,128)(2,1)S(1)} %get-tuple-element.19) | copy-start | bytes 3538948
  94.5 10.2 %copy-start.7 = (bf16[1,6,6,256,64]{3,4,1,2,0:T(8,128)(2,1)}, bf16[1,6,6,256,64]{3,4,1,2,0:T(8,128)(2,1)S(1)}, u32[]{:S(2)}) copy-start(bf16[1,6,6,256,64]{3,4,1,2,0:T(8,128)(2,1)S(1)} %get-tuple-element.18) | copy-start | bytes 3538948
  101.1 20.5 %collective-permute-start.8 = (bf16[2,6,256,64]{2,3,1,0:T(8,128)(2,1)S(1)}, bf16[2,6,256,64]{2,3,1,0:T(8,128)(2,1)S(1)}, u32[]{:S(2)}, u32[]{:S(2)}) collective-permute-start(bf16[2,6,256,64]{2,3,1,0:T(8,128)(2,1)S(1)} %collective-permute-done.6), channel_id=1, source_target_pairs={{0,128},{1,129},{2,130},{3,131},{4,132},{5,133},{6,134},{7,135},{8... | collective-permute-start | bytes 1179656 | tf_op jit(solution)/shard_map/ppermute | solution.py:92
  107.0 8.7 %collective-permute-start.4 = (bf16[1,6,256,64]{2,3,1,0:T(8,128)(2,1)}, bf16[1,6,256,64]{2,3,1,0:T(8,128)(2,1)}, u32[]{:S(2)}, u32[]{:S(2)}) collective-permute-start(bf16[1,6,256,64]{2,3,1,0:T(8,128)(2,1)} %collective-permute-done.2), channel_id=1, source_target_pairs={{0,128},{1,129},{2,130},{3,131},{4,132},{5,133},{6,134},{7,135},{8... | collective-permute-start | bytes 589832 | tf_op jit(solution)/shard_map/ppermute | solution.py:92
  115.7 7.8 %collective-permute-start.5 = (bf16[1,6,256,64]{2,3,1,0:T(8,128)(2,1)}, bf16[1,6,256,64]{2,3,1,0:T(8,128)(2,1)}, u32[]{:S(2)}, u32[]{:S(2)}) collective-permute-start(bf16[1,6,256,64]{2,3,1,0:T(8,128)(2,1)} %collective-permute-done.4), channel_id=1, source_target_pairs={{0,256},{256,0},{512,768},{768,512},{1,257},{257,1},{513,769},{769... | collective-permute-start | bytes 589832 | tf_op jit(solution)/shard_map/ppermute | solution.py:93
  121.5 5.5 %collective-permute-start.9 = (bf16[2,6,256,64]{2,3,1,0:T(8,128)(2,1)S(1)}, bf16[2,6,256,64]{2,3,1,0:T(8,128)(2,1)}, u32[]{:S(2)}, u32[]{:S(2)}) collective-permute-start(bf16[2,6,256,64]{2,3,1,0:T(8,128)(2,1)S(1)} %collective-permute-done.8), channel_id=1, source_target_pairs={{0,256},{256,0},{512,768},{768,512},{1,257},{257,1},{513,769},{769... | collective-permute-start | bytes 1179656 | tf_op jit(solution)/shard_map/ppermute | solution.py:93
  123.5 1.8 %copy-start.8 = (bf16[1,6,6,256,64]{3,4,1,2,0:T(8,128)(2,1)S(1)}, bf16[1,6,6,256,64]{3,4,1,2,0:T(8,128)(2,1)}, u32[]{:S(2)}) copy-start(bf16[1,6,6,256,64]{3,4,1,2,0:T(8,128)(2,1)} %copy-done.7) | copy-start | bytes 3538948
  123.5 1.8 %copy-start.11 = (f32[1,6,256,64]{2,3,1,0:T(8,128)S(1)}, f32[1,6,256,64]{2,3,1,0:T(8,128)}, u32[]{:S(2)}) copy-start(f32[1,6,256,64]{2,3,1,0:T(8,128)} %fusion.21) | copy-start | bytes 1179652
  125.3 2.0 %copy-start.4 = (bf16[2,6,6,256,64]{3,4,1,2,0:T(8,128)(2,1)S(1)}, bf16[2,6,6,256,64]{3,4,1,2,0:T(8,128)(2,1)}, u32[]{:S(2)}) copy-start(bf16[2,6,6,256,64]{3,4,1,2,0:T(8,128)(2,1)} %copy-done.3) | copy-start | bytes 7077892
  127.0 1.9 %copy-start.12 = (f32[2,6,256,64]{2,3,1,0:T(8,128)S(1)}, f32[2,6,256,64]{2,3,1,0:T(8,128)}, u32[]{:S(2)}) copy-start(f32[2,6,256,64]{2,3,1,0:T(8,128)} %fusion.13) | copy-start | bytes 2359300
  128.9 1.8 %copy-start.5 = (f32[1,6,256,64]{2,3,1,0:T(8,128)S(1)}, f32[1,6,256,64]{2,3,1,0:T(8,128)}, u32[]{:S(2)}) copy-start(f32[1,6,256,64]{2,3,1,0:T(8,128)} %get-tuple-element.23) | copy-start | bytes 1179652

commit v8 on v3

--- a/solution.py
+++ b/solution.py
@@ -96,7 +96,7 @@
 
 
 def solution(mesh):
-    relay = relay_pairs(mesh) if mesh.shape["layer"] == 4 else None
+    relay = None
     return jax.shard_map(
         make_body(relay),
         mesh=mesh,

time: 118 us -> 111 us (0.941)
  matrix products: 21.9 us -> 12 us
  waiting for transfers between devices: 28.1 us -> 36 us
  starting transfers between devices: 47.5 us -> 43.3 us
    ppermute x2 -> x1, waiting for transfers between devices: 13.1 us -> 22 us  [body(): far = lax.ppermute(rounded, 'layer', [(i, i ^ 2) for i in range(n_layer)])]
    ppermute x1, starting transfers between devices: 9.23 us -> 3.71 us  [body(): mate = lax.ppermute(rounded, 'layer', across)]
    dot_general x2, matrix products: 6.32 us -> 1.39 us  [cubed_part(): jnp.einsum('rsac,rstcb->rtab', left, rest, preferred_element_type=jnp.flo...]
    dot_general x2, matrix products: 6.83 us -> 2.53 us  [cubed_part(): jnp.einsum('rsac,rstcb->rtab', left, rows, preferred_element_type=jnp.flo...]
    ppermute x2 -> x1, starting transfers between devices: 15 us -> 17.5 us  [body(): far = lax.ppermute(rounded, 'layer', [(i, i ^ 2) for i in range(n_layer)])]
    ppermute x1, waiting for transfers between devices: 1.92 us -> 0.01 us  [body(): far_mate = lax.ppermute(far, 'layer', across)]
    ppermute x1, starting transfers between devices: 4.15 us -> 2.95 us  [body(): far_mate = lax.ppermute(far, 'layer', across)]
    unnamed x12 -> x6, local copies, waits for them, and re-layouts: 2.86 us -> 1.83 us
  transfers between devices with their start and end apart: 6 -> 5, of which waited for: 3 -> 3; matrix products, arithmetic and copies ran while one was open for 13% -> 9% of each run, Pallas kernels for 0% -> 0%
where the time goes in v8:
time: 111 us; the launch traced here: 110 us
  starting transfers between devices  43.3 us (39%)
  waiting for transfers between devices  36 us (32%)
  matrix products  12 us (11%)
  local copies, waits for them, and re-layouts  9.78 us (9%)
  other arithmetic  8.59 us (8%)
    ppermute x1, waiting for transfers between devices, body(): far = lax.ppermute(rounded, 'layer', [(i, i ^ 2) for i in range(n_layer)])  22 us
    ppermute x1, starting transfers between devices, body(): far = lax.ppermute(rounded, 'layer', [(i, i ^ 2) for i in range(n_layer)])  17.5 us
    ppermute x1, starting transfers between devices, padded_2(): after = lax.ppermute(initial, axis, down)  15.2 us
    ppermute x1, waiting for transfers between devices, padded_2(): before = lax.ppermute(last, axis, up)  13.1 us
    dot_general x1, matrix products, body(): jnp.einsum('rsac,rstcb->rtab', density, picked, precision=lax.Precision.H...  8.1 us
    gather x1, local copies, waits for them, and re-layouts, body(): picked = padded[place[:, :, None], slot] * valid[:, :, :, None, None]  4.48 us
    ppermute x1, starting transfers between devices, padded_2(): before = lax.ppermute(last, axis, up)  3.94 us
    ppermute x1, starting transfers between devices, body(): mate = lax.ppermute(rounded, 'layer', across)  3.71 us
  transfers between devices with their start and end apart: 5, of which 3 were waited for; matrix products, arithmetic and copies ran while one was open for 9% of the time, Pallas kernels for 0%

profile of v8, /device:TPU:1, one launch (start us, length us, event | category | flops | bytes accessed | tf_op | source)
XLA Modules:
  0.0 110.5 jit_solution(16327911223850836487)
XLA Ops:
  0.6 2.3 %constant_dynamic-slice_fusion.1 = f32[3,6,256,64]{3,2,1,0:T(8,128)S(1)} fusion(f32[3,6,256,256]{3,2,1,0:T(8,128)} %param.2, s32[]{:T(128)S(6)} %select_n.58), kind=kLoop, calls=%fused_computation.55 | loop fusion | bytes 2359300 | tf_op jit(solution)/shard_map/dynamic_slice | solution.py:63
  3.0 0.9 copy.69
  3.9 0.0 copy-start
  3.9 3.9 %collective-permute-start = (f32[3,6,256,64]{2,3,1,0:T(8,128)S(1)}, f32[3,6,256,64]{2,3,1,0:T(8,128)}, u32[]{:S(2)}, u32[]{:S(2)}) collective-permute-start(f32[3,6,256,64]{2,3,1,0:T(8,128)S(1)} %copy.69), channel_id=1, source_target_pairs={{0,1},{1,2},{2,3},{3,4},{4,5},{5,6},{6,7},{7,8},{8,9},{9,10},{10,1... | collective-permute-start | bytes 3538952 | tf_op jit(solution)/shard_map/ppermute | solution.py:16
  7.8 15.2 %collective-permute-start.1 = (f32[3,6,256,64]{2,3,1,0:T(8,128)S(1)}, f32[3,6,256,64]{2,3,1,0:T(8,128)}, u32[]{:S(2)}, u32[]{:S(2)}) collective-permute-start(f32[3,6,256,64]{2,3,1,0:T(8,128)S(1)} %copy.69), channel_id=1, source_target_pairs={{1,0},{2,1},{3,2},{4,3},{5,4},{6,5},{7,6},{8,7},{9,8},{10,9},{11,1... | collective-permute-start | bytes 3538952 | tf_op jit(solution)/shard_map/ppermute | solution.py:17
  23.0 0.9 copy.40
  24.0 0.8 fusion.59
  24.8 0.1 copy.43
  24.8 0.1 copy.39
  24.9 0.1 reshape.25
  25.0 0.6 gather_fusion
  25.6 0.1 copy.38
  25.7 1.3 %fusion.51 = (s32[3,6,6]{2,1,0:T(8,128)}, s32[3,6,6]{2,1,0:T(8,128)S(1)}) fusion(s32[3,6]{1,0:T(4,128)S(1)} %copy.43, s32[3,6,6]{2,1,0:T(8,128)S(1)} %reshape.54), kind=kLoop, calls=%fused_computation.35 | loop fusion | flops 5076 | bytes 1368 | tf_op jit(solution)/shard_map/make_body.<locals>.body/reduce | solution.py:58
  27.0 0.1 fusion.55
  27.1 0.1 reshape.31
  27.2 0.5 compare_reduce_fusion
  27.7 0.1 copy.44
  27.8 13.1 %collective-permute-done = f32[3,6,256,64]{2,3,1,0:T(8,128)} collective-permute-done((f32[3,6,256,64]{2,3,1,0:T(8,128)S(1)}, f32[3,6,256,64]{2,3,1,0:T(8,128)}, u32[]{:S(2)}, u32[]{:S(2)}) %collective-permute-start) | collective-permute-done | bytes 1179680 | tf_op jit(solution)/shard_map/ppermute | solution.py:16
  40.9 0.8 collective-permute-done.1
  41.7 2.2 %pad_maximum_fusion = f32[9,6,256,64]{2,3,1,0:T(8,128)S(1)} fusion(f32[3,6,256,64]{2,3,1,0:T(8,128)} %collective-permute-done.1, f32[3,6,256,64]{2,3,1,0:T(8,128)} %copy-done, f32[3,6,256,64]{2,3,1,0:T(8,128)} %collective-permute-done), kind=kLoop, calls=%fused_computation.8 | loop fusion | flops 1769472 | bytes 7077888 | tf_op jit(solution)/shard_map/concatenate | solution.py:18
  43.9 4.5 %gather_fusion.1 = f32[108,256,64]{1,2,0:T(8,128)} fusion(f32[9,6,256,64]{2,3,1,0:T(8,128)S(1)} %pad_maximum_fusion, s32[108]{0:T(128)S(1)} %reshape.31), kind=kCustom, calls=%fused_computation.1 | custom fusion | bytes 14156640 | tf_op jit(solution)/shard_map/gather | solution.py:65
  48.4 8.1 %fusion.68 = (bf16[3,6,256,64]{2,3,1,0:T(8,128)(2,1)S(1)}, f32[3,6,256,64]{2,3,1,0:T(8,128)S(1)}) fusion(f32[3,6,256,256]{3,2,1,0:T(8,128)} %param.2, f32[3,6,6,256,64]{3,4,2,1,0:T(8,128)} %bitcast.63, f32[3,6,6]{1,2,0:T(8,128)S(1)} %copy.44), kind=kOutput, calls=%fused_computation.62 | convolution fusion | flops 2719973376 | bytes 13566384 | tf_op jit(solution)/shard_map/rsac,rstcb->rtab/dot_general | solution.py:66
  56.5 0.0 copy-start.1
  56.5 17.5 %collective-permute-start.3 = (bf16[3,6,256,64]{2,3,1,0:T(8,128)(2,1)S(1)}, bf16[3,6,256,64]{2,3,1,0:T(8,128)(2,1)S(1)}, u32[]{:S(2)}, u32[]{:S(2)}) collective-permute-start(bf16[3,6,256,64]{2,3,1,0:T(8,128)(2,1)S(1)} %get-tuple-element.8), channel_id=1, source_target_pairs={{0,512},{256,768},{512,0},{768,256},{1,513},{257,769},{513,1},{769... | collective-permute-start | bytes 1769480 | tf_op jit(solution)/shard_map/ppermute | solution.py:85
  74.0 3.7 %collective-permute-start.2 = (bf16[3,6,256,64]{2,3,1,0:T(8,128)(2,1)S(1)}, bf16[3,6,256,64]{2,3,1,0:T(8,128)(2,1)S(1)}, u32[]{:S(2)}, u32[]{:S(2)}) collective-permute-start(bf16[3,6,256,64]{2,3,1,0:T(8,128)(2,1)S(1)} %get-tuple-element.8), channel_id=1, source_target_pairs={{0,256},{256,0},{512,768},{768,512},{1,257},{257,1},{513,769},{769... | collective-permute-start | bytes 1769480 | tf_op jit(solution)/shard_map/ppermute | solution.py:80
  77.8 22.0 %collective-permute-done.3 = bf16[3,6,256,64]{2,3,1,0:T(8,128)(2,1)S(1)} collective-permute-done((bf16[3,6,256,64]{2,3,1,0:T(8,128)(2,1)S(1)}, bf16[3,6,256,64]{2,3,1,0:T(8,128)(2,1)S(1)}, u32[]{:S(2)}, u32[]{:S(2)}) %collective-permute-start.3) | collective-permute-done | bytes 589856 | tf_op jit(solution)/shard_map/ppermute | solution.py:85
  99.8 3.0 %collective-permute-start.4 = (bf16[3,6,256,64]{2,3,1,0:T(8,128)(2,1)S(1)}, bf16[3,6,256,64]{2,3,1,0:T(8,128)(2,1)S(1)}, u32[]{:S(2)}, u32[]{:S(2)}) collective-permute-start(bf16[3,6,256,64]{2,3,1,0:T(8,128)(2,1)S(1)} %collective-permute-done.3), channel_id=1, source_target_pairs={{0,256},{256,0},{512,768},{768,512},{1,257},{257,1},{513,769},{769... | collective-permute-start | bytes 1769480 | tf_op jit(solution)/shard_map/ppermute | solution.py:90
  102.8 3.7 %reduce-precision_convert_fusion = (bf16[3,6,6,256,64]{3,4,1,2,0:T(8,128)(2,1)S(1)}, bf16[3,6,6,256,64]{3,4,1,2,0:T(8,128)(2,1)S(1)}) fusion(f32[3,6,6,256,64]{3,4,2,1,0:T(8,128)} %bitcast.64, f32[3,6,6]{1,2,0:T(8,128)S(1)} %copy.44), kind=kLoop, calls=%fused_computation.3 | loop fusion | flops 8847360 | bytes 14156208 | tf_op jit(solution)/shard_map/convert_element_type | solution.py:69
  106.5 0.7 fusion.15
  107.2 0.7 fusion.42
  107.9 0.7 fusion.21
  108.6 1.8 %fusion.39 = f32[3,6,256,64]{2,3,1,0:T(8,128)} fusion(f32[3,6,64,256]{3,2,1,0:T(8,128)S(1)} %fusion.42, f32[3,6,64,256]{3,2,1,0:T(8,128)S(1)} %fusion.21, bf16[3,6,6,256,64]{3,4,1,2,0:T(8,128)(2,1)S(1)} %get-tuple-element.6, s32[]{:T(128)S(6)} %select_n.69, f32[3,6,256,64]{2,3,1,0:T(8,128)S(1)} %get-tuple-element.9, ...), kind=kOutput, calls=%fused_computation.27 | convolution fusion | flops 459767808 | bytes 7667717 | tf_op jit(solution)/shard_map/rsac,rstcb->rtab/dot_general | solution.py:75
  (9 shorter events, 0.0 us)
Async XLA Ops:
  3.9 37.0 %copy-start = (f32[3,6,256,64]{2,3,1,0:T(8,128)}, f32[3,6,256,64]{2,3,1,0:T(8,128)S(1)}, u32[]{:S(2)}) copy-start(f32[3,6,256,64]{2,3,1,0:T(8,128)S(1)} %copy.69) | copy-start | bytes 3538948
  3.9 37.0 %collective-permute-start = (f32[3,6,256,64]{2,3,1,0:T(8,128)S(1)}, f32[3,6,256,64]{2,3,1,0:T(8,128)}, u32[]{:S(2)}, u32[]{:S(2)}) collective-permute-start(f32[3,6,256,64]{2,3,1,0:T(8,128)S(1)} %copy.69), channel_id=1, source_target_pairs={{0,1},{1,2},{2,3},{3,4},{4,5},{5,6},{6,7},{7,8},{8,9},{9,10},{10,1... | collective-permute-start | bytes 3538952 | tf_op jit(solution)/shard_map/ppermute | solution.py:16
  7.8 33.9 %collective-permute-start.1 = (f32[3,6,256,64]{2,3,1,0:T(8,128)S(1)}, f32[3,6,256,64]{2,3,1,0:T(8,128)}, u32[]{:S(2)}, u32[]{:S(2)}) collective-permute-start(f32[3,6,256,64]{2,3,1,0:T(8,128)S(1)} %copy.69), channel_id=1, source_target_pairs={{1,0},{2,1},{3,2},{4,3},{5,4},{6,5},{7,6},{8,7},{9,8},{10,9},{11,1... | collective-permute-start | bytes 3538952 | tf_op jit(solution)/shard_map/ppermute | solution.py:17
  56.5 52.1 %copy-start.1 = (f32[3,6,256,64]{2,3,1,0:T(8,128)}, f32[3,6,256,64]{2,3,1,0:T(8,128)S(1)}, u32[]{:S(2)}) copy-start(f32[3,6,256,64]{2,3,1,0:T(8,128)S(1)} %get-tuple-element.9) | copy-start | bytes 3538948
  56.5 43.3 %collective-permute-start.3 = (bf16[3,6,256,64]{2,3,1,0:T(8,128)(2,1)S(1)}, bf16[3,6,256,64]{2,3,1,0:T(8,128)(2,1)S(1)}, u32[]{:S(2)}, u32[]{:S(2)}) collective-permute-start(bf16[3,6,256,64]{2,3,1,0:T(8,128)(2,1)S(1)} %get-tuple-element.8), channel_id=1, source_target_pairs={{0,512},{256,768},{512,0},{768,256},{1,513},{257,769},{513,1},{769... | collective-permute-start | bytes 1769480 | tf_op jit(solution)/shard_map/ppermute | solution.py:85
  74.0 32.5 %collective-permute-start.2 = (bf16[3,6,256,64]{2,3,1,0:T(8,128)(2,1)S(1)}, bf16[3,6,256,64]{2,3,1,0:T(8,128)(2,1)S(1)}, u32[]{:S(2)}, u32[]{:S(2)}) collective-permute-start(bf16[3,6,256,64]{2,3,1,0:T(8,128)(2,1)S(1)} %get-tuple-element.8), channel_id=1, source_target_pairs={{0,256},{256,0},{512,768},{768,512},{1,257},{257,1},{513,769},{769... | collective-permute-start | bytes 1769480 | tf_op jit(solution)/shard_map/ppermute | solution.py:80
  99.8 8.1 %collective-permute-start.4 = (bf16[3,6,256,64]{2,3,1,0:T(8,128)(2,1)S(1)}, bf16[3,6,256,64]{2,3,1,0:T(8,128)(2,1)S(1)}, u32[]{:S(2)}, u32[]{:S(2)}) collective-permute-start(bf16[3,6,256,64]{2,3,1,0:T(8,128)(2,1)S(1)} %collective-permute-done.3), channel_id=1, source_target_pairs={{0,256},{256,0},{512,768},{768,512},{1,257},{257,1},{513,769},{769... | collective-permute-start | bytes 1769480 | tf_op jit(solution)/shard_map/ppermute | solution.py:90

commit v9 on v8

--- a/solution.py
+++ b/solution.py
@@ -83,6 +83,7 @@
         near_part = cubed_part(near_pair, me // 2)
         if relay is None:
             far = lax.ppermute(rounded, "layer", [(i, i ^ 2) for i in range(n_layer)])
+            far, near_part = lax.optimization_barrier((far, near_part))
         else:
             halfway = lax.ppermute(rounded, ("layer", "blk"), relay)
             halfway, near_part = lax.optimization_barrier((halfway, near_part))

time: 111 us -> 114 us (1.027)
  local copies, waits for them, and re-layouts: 9.78 us -> 12.3 us
  matrix products: 12 us -> 13.9 us
  waiting for transfers between devices: 36 us -> 34.6 us
  other arithmetic: 8.59 us -> 9.97 us
    ppermute x1, starting transfers between devices: 17.5 us -> 11.6 us  [body(): far = lax.ppermute(rounded, 'layer', [(i, i ^ 2) for i in range(n_layer)])]
    ppermute x1, starting transfers between devices: 3.71 us -> 9.24 us  [body(): mate = lax.ppermute(rounded, 'layer', across)]
    unnamed x6 -> x14, local copies, waits for them, and re-layouts: 1.83 us -> 4.35 us
    ppermute x1, waiting for transfers between devices: 22 us -> 19.7 us  [body(): far = lax.ppermute(rounded, 'layer', [(i, i ^ 2) for i in range(n_layer)])]
    ppermute x1, waiting for transfers between devices: 0.01 us -> 1.8 us  [body(): far_mate = lax.ppermute(far, 'layer', across)]
    dot_general x2, matrix products: 1.39 us -> 3.13 us  [cubed_part(): jnp.einsum('rsac,rstcb->rtab', left, rest, preferred_element_type=jnp.flo...]
    sub x0 -> x1, other arithmetic: none -> 1.38 us  [body(): return (squared, 3.0 * squared - 2.0 * cubed)]
where the time goes in v9:
time: 114 us
  starting transfers between devices  42.4 us (37%)
  waiting for transfers between devices  34.6 us (30%)
  matrix products  13.9 us (12%)
  local copies, waits for them, and re-layouts  12.3 us (11%)
  other arithmetic  9.97 us (9%)
    ppermute x1, waiting for transfers between devices, body(): far = lax.ppermute(rounded, 'layer', [(i, i ^ 2) for i in range(n_layer)])  19.7 us
    ppermute x1, starting transfers between devices, padded_2(): after = lax.ppermute(initial, axis, down)  15.2 us
    ppermute x1, waiting for transfers between devices, padded_2(): before = lax.ppermute(last, axis, up)  13 us
    ppermute x1, starting transfers between devices, body(): far = lax.ppermute(rounded, 'layer', [(i, i ^ 2) for i in range(n_layer)])  11.6 us
    ppermute x1, starting transfers between devices, body(): mate = lax.ppermute(rounded, 'layer', across)  9.24 us
    dot_general x1, matrix products, body(): jnp.einsum('rsac,rstcb->rtab', density, picked, precision=lax.Precision.H...  8.1 us
    gather x1, local copies, waits for them, and re-layouts, body(): picked = padded[place[:, :, None], slot] * valid[:, :, :, None, None]  4.49 us
    unnamed x14, local copies, waits for them, and re-layouts  4.35 us
  transfers between devices with their start and end apart: 5, of which 3 were waited for; matrix products, arithmetic and copies ran while one was open for 9% of the time, Pallas kernels for 0%

profile of v9, /device:TPU:1, one launch (start us, length us, event | category | flops | bytes accessed | tf_op | source)
XLA Modules:
  0.0 114.0 jit_solution(13692715610482293268)
XLA Ops:
  0.6 2.3 %constant_dynamic-slice_fusion.1 = f32[3,6,256,64]{3,2,1,0:T(8,128)S(1)} fusion(f32[3,6,256,256]{3,2,1,0:T(8,128)} %param.2, s32[]{:T(128)S(6)} %select_n.58), kind=kLoop, calls=%fused_computation.54 | loop fusion | bytes 2359300 | tf_op jit(solution)/shard_map/dynamic_slice | solution.py:63
  3.0 0.9 copy.69
  3.9 3.9 %collective-permute-start = (f32[3,6,256,64]{2,3,1,0:T(8,128)S(1)}, f32[3,6,256,64]{2,3,1,0:T(8,128)S(1)}, u32[]{:S(2)}, u32[]{:S(2)}) collective-permute-start(f32[3,6,256,64]{2,3,1,0:T(8,128)S(1)} %copy.69), channel_id=1, source_target_pairs={{0,1},{1,2},{2,3},{3,4},{4,5},{5,6},{6,7},{7,8},{8,9},{9,10},{10,1... | collective-permute-start | bytes 3538952 | tf_op jit(solution)/shard_map/ppermute | solution.py:16
  7.8 15.2 %collective-permute-start.1 = (f32[3,6,256,64]{2,3,1,0:T(8,128)S(1)}, f32[3,6,256,64]{2,3,1,0:T(8,128)}, u32[]{:S(2)}, u32[]{:S(2)}) collective-permute-start(f32[3,6,256,64]{2,3,1,0:T(8,128)S(1)} %copy.69), channel_id=1, source_target_pairs={{1,0},{2,1},{3,2},{4,3},{5,4},{6,5},{7,6},{8,7},{9,8},{10,9},{11,1... | collective-permute-start | bytes 3538952 | tf_op jit(solution)/shard_map/ppermute | solution.py:17
  23.0 0.9 copy.40
  24.0 0.8 fusion.53
  24.8 0.1 copy.43
  24.8 0.1 copy.39
  25.0 0.6 gather_fusion
  25.6 0.1 copy.38
  25.7 1.3 %fusion.45 = (s32[3,6,6]{2,1,0:T(8,128)}, s32[3,6,6]{2,1,0:T(8,128)S(1)}) fusion(s32[3,6]{1,0:T(4,128)S(1)} %copy.43, s32[3,6,6]{2,1,0:T(8,128)S(1)} %reshape.54), kind=kLoop, calls=%fused_computation.34 | loop fusion | flops 5076 | bytes 1368 | tf_op jit(solution)/shard_map/make_body.<locals>.body/reduce | solution.py:58
  27.1 0.1 reshape.31
  27.2 0.5 compare_reduce_fusion
  27.7 0.1 copy.44
  27.8 13.0 %collective-permute-done = f32[3,6,256,64]{2,3,1,0:T(8,128)S(1)} collective-permute-done((f32[3,6,256,64]{2,3,1,0:T(8,128)S(1)}, f32[3,6,256,64]{2,3,1,0:T(8,128)S(1)}, u32[]{:S(2)}, u32[]{:S(2)}) %collective-permute-start) | collective-permute-done | bytes 1179680 | tf_op jit(solution)/shard_map/ppermute | solution.py:16
  40.8 1.0 copy-done.5
  41.8 2.2 %pad_maximum_fusion = f32[9,6,256,64]{2,3,1,0:T(8,128)S(1)} fusion(f32[3,6,256,64]{2,3,1,0:T(8,128)} %collective-permute-done.1, f32[3,6,256,64]{2,3,1,0:T(8,128)} %copy-done.1, f32[3,6,256,64]{2,3,1,0:T(8,128)} %copy-done.5), kind=kLoop, calls=%fused_computation.8 | loop fusion | flops 1769472 | bytes 7077888 | tf_op jit(solution)/shard_map/concatenate | solution.py:18
  44.0 4.5 %gather_fusion.1 = f32[108,256,64]{1,2,0:T(8,128)} fusion(f32[9,6,256,64]{2,3,1,0:T(8,128)S(1)} %pad_maximum_fusion, s32[108]{0:T(128)S(1)} %reshape.31), kind=kCustom, calls=%fused_computation.1 | custom fusion | bytes 14156640 | tf_op jit(solution)/shard_map/gather | solution.py:65
  48.5 8.1 %fusion.62 = (bf16[3,6,256,64]{2,3,1,0:T(8,128)(2,1)S(1)}, f32[3,6,256,64]{2,3,1,0:T(8,128)S(1)}) fusion(f32[3,6,256,256]{3,2,1,0:T(8,128)} %param.2, f32[3,6,6,256,64]{3,4,2,1,0:T(8,128)} %bitcast.59, f32[3,6,6]{1,2,0:T(8,128)S(1)} %copy.44), kind=kOutput, calls=%fused_computation.61 | convolution fusion | flops 2719973376 | bytes 13566384 | tf_op jit(solution)/shard_map/rsac,rstcb->rtab/dot_general | solution.py:66
  56.7 9.2 %collective-permute-start.3 = (bf16[3,6,256,64]{2,3,1,0:T(8,128)(2,1)S(1)}, bf16[3,6,256,64]{2,3,1,0:T(8,128)(2,1)S(1)}, u32[]{:S(2)}, u32[]{:S(2)}) collective-permute-start(bf16[3,6,256,64]{2,3,1,0:T(8,128)(2,1)S(1)} %get-tuple-element.12), channel_id=1, source_target_pairs={{0,256},{256,0},{512,768},{768,512},{1,257},{257,1},{513,769},{769... | collective-permute-start | bytes 1769480 | tf_op jit(solution)/shard_map/ppermute | solution.py:80
  65.9 11.6 %collective-permute-start.2 = (bf16[3,6,256,64]{2,3,1,0:T(8,128)(2,1)S(1)}, bf16[3,6,256,64]{2,3,1,0:T(8,128)(2,1)}, u32[]{:S(2)}, u32[]{:S(2)}) collective-permute-start(bf16[3,6,256,64]{2,3,1,0:T(8,128)(2,1)S(1)} %get-tuple-element.12), channel_id=1, source_target_pairs={{0,512},{256,768},{512,0},{768,256},{1,513},{257,769},{513,1},{769... | collective-permute-start | bytes 1769480 | tf_op jit(solution)/shard_map/ppermute | solution.py:85
  77.5 3.7 %reduce-precision_convert_fusion = (bf16[3,6,6,256,64]{3,4,1,2,0:T(8,128)(2,1)S(1)}, bf16[3,6,6,256,64]{3,4,1,2,0:T(8,128)(2,1)S(1)}) fusion(f32[3,6,6,256,64]{3,4,2,1,0:T(8,128)} %bitcast.60, f32[3,6,6]{1,2,0:T(8,128)S(1)} %copy.44), kind=kLoop, calls=%fused_computation.3 | loop fusion | flops 8847360 | bytes 14156208 | tf_op jit(solution)/shard_map/convert_element_type | solution.py:69
  81.3 0.7 fusion.15
  81.9 1.0 copy-done.2
  83.0 0.7 fusion.36
  83.7 0.5 copy-done.4
  84.2 19.7 %collective-permute-done.2 = bf16[3,6,256,64]{2,3,1,0:T(8,128)(2,1)} collective-permute-done((bf16[3,6,256,64]{2,3,1,0:T(8,128)(2,1)S(1)}, bf16[3,6,256,64]{2,3,1,0:T(8,128)(2,1)}, u32[]{:S(2)}, u32[]{:S(2)}) %collective-permute-start.2) | collective-permute-done | bytes 589856 | tf_op jit(solution)/shard_map/ppermute | solution.py:85
  103.9 2.5 %collective-permute-start.4 = (bf16[3,6,256,64]{2,3,1,0:T(8,128)(2,1)}, bf16[3,6,256,64]{2,3,1,0:T(8,128)(2,1)S(1)}, u32[]{:S(2)}, u32[]{:S(2)}) collective-permute-start(bf16[3,6,256,64]{2,3,1,0:T(8,128)(2,1)} %collective-permute-done.2), channel_id=1, source_target_pairs={{0,256},{256,0},{512,768},{768,512},{1,257},{257,1},{513,769},{769... | collective-permute-start | bytes 1769480 | tf_op jit(solution)/shard_map/ppermute | solution.py:91
  106.4 1.8 %collective-permute-done.4 = bf16[3,6,256,64]{2,3,1,0:T(8,128)(2,1)S(1)} collective-permute-done((bf16[3,6,256,64]{2,3,1,0:T(8,128)(2,1)}, bf16[3,6,256,64]{2,3,1,0:T(8,128)(2,1)S(1)}, u32[]{:S(2)}, u32[]{:S(2)}) %collective-permute-start.4) | collective-permute-done | bytes 589856 | tf_op jit(solution)/shard_map/ppermute | solution.py:91
  108.2 2.4 %fusion.21 = f32[3,6,64,256]{3,2,1,0:T(8,128)S(1)} fusion(bf16[3,6,6,256,64]{3,4,1,2,0:T(8,128)(2,1)} %copy-done.4, s32[]{:T(128)S(6)} %select_n.69, bf16[3,6,256,64]{2,3,1,0:T(8,128)(2,1)S(1)} %collective-permute-done.4, bf16[3,6,256,64]{2,3,1,0:T(8,128)(2,1)} %collective-permute-done.2, pred[]{:T(512)S(6)} %eq.25), kind=kOutput, calls=%fused_computation.21 | convolution fusion | flops 458293248 | bytes 4128773 | tf_op jit(solution)/shard_map/rsac,rstcb->rtab/dot_general | solution.py:76
  110.6 2.0 %fusion.30 = f32[3,6,256,64]{2,3,1,0:T(8,128)S(1)} fusion(f32[3,6,64,256]{3,2,1,0:T(8,128)S(1)} %fusion.21, bf16[3,6,6,256,64]{3,4,1,2,0:T(8,128)(2,1)S(1)} %copy-done.3, s32[]{:T(128)S(6)} %select_n.69, bf16[3,6,256,64]{2,3,1,0:T(8,128)(2,1)S(1)} %collective-permute-done.4, bf16[3,6,256,64]{2,3,1,0:T(8,128)(2,1)} %collective-permute-done.2, pred[]{:T(512)S(6)} %eq.25), kind=kOutput, calls=%fused_computation.24 | convolution fusion | flops 458588160 | bytes 5308421 | tf_op jit(solution)/shard_map/rsac,rstcb->rtab/dot_general | solution.py:75
  112.7 1.4 %multiply_subtract_fusion = f32[3,6,256,64]{2,3,1,0:T(8,128)} fusion(f32[3,6,256,64]{2,3,1,0:T(8,128)S(1)} %fusion.36, f32[3,6,256,64]{2,3,1,0:T(8,128)S(1)} %fusion.30, f32[3,6,256,64]{2,3,1,0:T(8,128)S(1)} %get-tuple-element.13), kind=kLoop, calls=%fused_computation.31 | loop fusion | flops 1179648 | bytes 4718592 | tf_op jit(solution)/shard_map/sub | solution.py:94
  (18 shorter events, 0.2 us)
Async XLA Ops:
  3.9 36.9 %copy-start.1 = (f32[3,6,256,64]{2,3,1,0:T(8,128)}, f32[3,6,256,64]{2,3,1,0:T(8,128)S(1)}, u32[]{:S(2)}) copy-start(f32[3,6,256,64]{2,3,1,0:T(8,128)S(1)} %copy.69) | copy-start | bytes 3538948
  3.9 36.9 %collective-permute-start = (f32[3,6,256,64]{2,3,1,0:T(8,128)S(1)}, f32[3,6,256,64]{2,3,1,0:T(8,128)S(1)}, u32[]{:S(2)}, u32[]{:S(2)}) collective-permute-start(f32[3,6,256,64]{2,3,1,0:T(8,128)S(1)} %copy.69), channel_id=1, source_target_pairs={{0,1},{1,2},{2,3},{3,4},{4,5},{5,6},{6,7},{7,8},{8,9},{9,10},{10,1... | collective-permute-start | bytes 3538952 | tf_op jit(solution)/shard_map/ppermute | solution.py:16
  7.8 34.0 %collective-permute-start.1 = (f32[3,6,256,64]{2,3,1,0:T(8,128)S(1)}, f32[3,6,256,64]{2,3,1,0:T(8,128)}, u32[]{:S(2)}, u32[]{:S(2)}) collective-permute-start(f32[3,6,256,64]{2,3,1,0:T(8,128)S(1)} %copy.69), channel_id=1, source_target_pairs={{1,0},{2,1},{3,2},{4,3},{5,4},{6,5},{7,6},{8,7},{9,8},{10,9},{11,1... | collective-permute-start | bytes 3538952 | tf_op jit(solution)/shard_map/ppermute | solution.py:17
  40.8 1.0 copy-start.5
  56.6 56.0 %copy-start = (f32[3,6,256,64]{2,3,1,0:T(8,128)}, f32[3,6,256,64]{2,3,1,0:T(8,128)S(1)}, u32[]{:S(2)}) copy-start(f32[3,6,256,64]{2,3,1,0:T(8,128)S(1)} %get-tuple-element.13) | copy-start | bytes 3538948
  56.7 24.6 %collective-permute-start.3 = (bf16[3,6,256,64]{2,3,1,0:T(8,128)(2,1)S(1)}, bf16[3,6,256,64]{2,3,1,0:T(8,128)(2,1)S(1)}, u32[]{:S(2)}, u32[]{:S(2)}) collective-permute-start(bf16[3,6,256,64]{2,3,1,0:T(8,128)(2,1)S(1)} %get-tuple-element.12), channel_id=1, source_target_pairs={{0,256},{256,0},{512,768},{768,512},{1,257},{257,1},{513,769},{769... | collective-permute-start | bytes 1769480 | tf_op jit(solution)/shard_map/ppermute | solution.py:80
  65.9 37.9 %collective-permute-start.2 = (bf16[3,6,256,64]{2,3,1,0:T(8,128)(2,1)S(1)}, bf16[3,6,256,64]{2,3,1,0:T(8,128)(2,1)}, u32[]{:S(2)}, u32[]{:S(2)}) collective-permute-start(bf16[3,6,256,64]{2,3,1,0:T(8,128)(2,1)S(1)} %get-tuple-element.12), channel_id=1, source_target_pairs={{0,512},{256,768},{512,0},{768,256},{1,513},{257,769},{513,1},{769... | collective-permute-start | bytes 1769480 | tf_op jit(solution)/shard_map/ppermute | solution.py:85
  81.2 1.7 %copy-start.2 = (bf16[3,6,6,256,64]{3,4,1,2,0:T(8,128)(2,1)}, bf16[3,6,6,256,64]{3,4,1,2,0:T(8,128)(2,1)S(1)}, u32[]{:S(2)}) copy-start(bf16[3,6,6,256,64]{3,4,1,2,0:T(8,128)(2,1)S(1)} %get-tuple-element.10) | copy-start | bytes 10616836
  81.2 2.9 %copy-start.4 = (bf16[3,6,6,256,64]{3,4,1,2,0:T(8,128)(2,1)}, bf16[3,6,6,256,64]{3,4,1,2,0:T(8,128)(2,1)S(1)}, u32[]{:S(2)}) copy-start(bf16[3,6,6,256,64]{3,4,1,2,0:T(8,128)(2,1)S(1)} %get-tuple-element.11) | copy-start | bytes 10616836
  103.9 4.3 %collective-permute-start.4 = (bf16[3,6,256,64]{2,3,1,0:T(8,128)(2,1)}, bf16[3,6,256,64]{2,3,1,0:T(8,128)(2,1)S(1)}, u32[]{:S(2)}, u32[]{:S(2)}) collective-permute-start(bf16[3,6,256,64]{2,3,1,0:T(8,128)(2,1)} %collective-permute-done.2), channel_id=1, source_target_pairs={{0,256},{256,0},{512,768},{768,512},{1,257},{257,1},{513,769},{769... | collective-permute-start | bytes 1769480 | tf_op jit(solution)/shard_map/ppermute | solution.py:91
  106.4 4.3 %copy-start.3 = (bf16[3,6,6,256,64]{3,4,1,2,0:T(8,128)(2,1)S(1)}, bf16[3,6,6,256,64]{3,4,1,2,0:T(8,128)(2,1)}, u32[]{:S(2)}) copy-start(bf16[3,6,6,256,64]{3,4,1,2,0:T(8,128)(2,1)} %copy-done.2) | copy-start | bytes 10616836
